TPU v7x, 32 devices: a whole 2x2x4 slice. The times are simulated.
32 devices in a mesh: brick: 8 (over y, x, core), plane: 4 (over z).
Axes of the slice: x: 2, y: 2, z: 4, core: 2. Of those that a mesh axis runs over, the one named last changes fastest.
Arguments:
- positions: float32 [8, 4, 3, 4096], P('brick', 'plane'), may hold values from 0 to 64
- aux: float32 [8, 4, 4096], P('brick', 'plane'), may hold values from -1 to 1.8
- aux_prev: float32 [8, 4, 4096], P('brick', 'plane'), may hold values from -3 to 3
- resid: float32 [8, 4, 4096], P('brick', 'plane'), may hold values from -2 to 2
- types: int32 [8, 4, 4096], P('brick', 'plane'), may hold values from 0 to 7
- pair_tiles: int32 [8, 4, 1496], P('brick', 'plane'), may hold values from 0 to 63, as said below
- pair_cands: int32 [8, 4, 1496], P('brick', 'plane'), may hold values from 0 to 319, as said below
- pair_count: int32 [8, 4], P('brick', 'plane'), may hold values from 0 to 1496, as said below
- owner_tile: int32 [8, 4, 64], P('brick', 'plane'), may hold values from 0 to 255, as said below
- electroneg: float32 [8], replicated, may hold values from -3 to 3
- hardness: float32 [8], replicated, may hold values from 6 to 14
- widths: float32 [8], replicated, may hold values from 0.6 to 2
Outputs:
- charges: float32 [8, 4, 4096], P('brick', 'plane')
- next_aux: float32 [8, 4, 4096], P('brick', 'plane')
- resid_field: float32 [8, 4, 4096], P('brick', 'plane')
Inputs may be any that keep to these rules, and one draw needn't show every extreme that they name: `pair_tiles`: entries after the first pair_count[b, p] of a brick's list are not used. `pair_cands`: A used pair never names a neighbour brick beyond the ends of the brick axis. `pair_count`: at most 1496 pairs a brick, reached by some brick. `owner_tile`: for each b the values over all p and t form a permutation of 0 to 255, and each brick (b, p) has exactly 16 tiles of each value // 64.
All inputs are finite; a program needn't handle non-finite values.
Results may differ from a plain program's by a relative error of at most 0.0003.
Values sent between devices are 32-bit elements; how exact they have to be, the bound alone decides.
No kernel may reach another device: no remote copies, remote signals or barrier semaphores. Data moves between devices by JAX's collectives and lax.ppermute only.
A program may use at most 64 MiB of HBM per device.

v0:
```python
import jax
import jax.numpy as jnp
from jax import lax
from jax.sharding import PartitionSpec as P

TX = 2
TY = 4
TILE = 64


cell_edge = 8.0
cutoff = 10.0
soften = 0.5
kappa = 1.86
pair_group = 256


def extended(block, sides, width):
    for axis, dim in sides:
        count = lax.axis_size(axis)
        forward = [(i, i + 1) for i in range(count - 1)]
        forward.append((count - 1, 0))
        backward = [(target, source) for source, target in forward]
        low = lax.ppermute(
            lax.slice_in_dim(block, block.shape[dim] - width, None, axis=dim), axis, forward
        )
        high = lax.ppermute(lax.slice_in_dim(block, 0, width, axis=dim), axis, backward)
        block = jnp.concatenate([low, block, high], axis=dim)
    return block


def lookup(type_table, type_row):
    chosen = (
        type_row[None, :] == jnp.arange(type_table.shape[0], dtype=jnp.int32)[:, None]
    ).astype(type_table.dtype)
    return jnp.sum(type_table[:, None] * chosen, axis=0)


def candidates(blocks, tile_count):
    joined = jnp.stack(blocks, axis=1)
    offsets = jnp.zeros((6, 5), jnp.float32)
    offsets = offsets.at[0, 1].set(-TX * cell_edge).at[0, 2].set(TX * cell_edge)
    offsets = offsets.at[1, 3].set(-TY * cell_edge).at[1, 4].set(TY * cell_edge)
    joined = joined + offsets[:, :, None]
    return joined.reshape(6, 5 * tile_count, TILE)


def pair_terms(home_tiles, candidate, near_ids, far_ids, in_range):
    tile_count = home_tiles.shape[1]
    near_atoms = jnp.take(home_tiles, near_ids, axis=1)
    far_atoms = jnp.take(candidate, far_ids, axis=1)
    delta_x = near_atoms[0][:, :, None] - far_atoms[0][:, None, :]
    delta_y = near_atoms[1][:, :, None] - far_atoms[1][:, None, :]
    delta_z = near_atoms[2][:, :, None] - far_atoms[2][:, None, :]
    dist_sq = delta_x * delta_x + delta_y * delta_y + delta_z * delta_z
    spacing = jnp.sqrt(dist_sq + soften * soften)
    inv_width = lax.rsqrt(near_atoms[5][:, :, None] ** 2 + far_atoms[5][:, None, :] ** 2)
    taper = jnp.square(jnp.maximum(1.0 - dist_sq / (cutoff * cutoff), 0.0))
    kernel = jax.scipy.special.erf(inv_width * spacing) / spacing * taper
    diagonal = (
        jnp.arange(TILE, dtype=jnp.int32)[:, None] == jnp.arange(TILE, dtype=jnp.int32)[None, :]
    )
    self_pairs = (far_ids == near_ids)[:, None, None] & diagonal[None]
    kept_pairs = in_range[:, None, None] & jnp.logical_not(self_pairs)
    kernel = jnp.where(kept_pairs, kernel, 0.0)
    pair_fields = jnp.einsum(
        "pij,cpj->cpi", kernel, far_atoms[3:5], precision=lax.Precision.HIGHEST
    )
    chosen = (near_ids[:, None] == jnp.arange(tile_count, dtype=jnp.int32)[None, :]).astype(
        pair_fields.dtype
    )
    return jnp.einsum("pt,cpi->cti", chosen, pair_fields, precision=lax.Precision.HIGHEST)


def sweep(home_tiles, candidate, near_list, far_list, begin_pair, end_pair, running):
    near_pad = jnp.concatenate([near_list, jnp.zeros((pair_group,), jnp.int32)])
    far_pad = jnp.concatenate([far_list, jnp.zeros((pair_group,), jnp.int32)])
    turns = (end_pair - begin_pair + pair_group - 1) // pair_group

    def advance(block_index, running):
        offset_start = begin_pair + block_index * pair_group
        near_ids = lax.dynamic_slice_in_dim(near_pad, offset_start, pair_group)
        far_ids = lax.dynamic_slice_in_dim(far_pad, offset_start, pair_group)
        in_range = offset_start + jnp.arange(pair_group, dtype=jnp.int32) < end_pair
        return running + pair_terms(home_tiles, candidate, near_ids, far_ids, in_range)

    return lax.fori_loop(0, turns, advance, running)


def on_device(
    positions,
    aux,
    aux_prev,
    resid,
    types,
    pair_tiles,
    pair_cands,
    pair_count,
    owner_tile,
    electroneg,
    hardness,
    widths,
):
    atom_count = aux.shape[-1]
    tile_count = atom_count // TILE
    type_row = types.reshape(atom_count)
    negativity = lookup(electroneg, type_row)
    hardness_row = lookup(hardness, type_row)
    radius = lookup(widths, type_row)
    charge_row = aux.reshape(atom_count)
    resid_row = resid.reshape(atom_count)
    packed = jnp.concatenate(
        [positions.reshape(3, atom_count), charge_row[None], resid_row[None], radius[None]], axis=0
    )
    rimmed = extended(packed[None, None], (("brick", 0), ("plane", 1)), 1)
    candidate = candidates(
        [rimmed[1, 1], rimmed[0, 1], rimmed[2, 1], rimmed[1, 0], rimmed[1, 2]], tile_count
    )
    home_tiles = packed.reshape(6, tile_count, TILE)
    near_list = pair_tiles.reshape(-1)
    far_list = pair_cands.reshape(-1)
    pair_total = pair_count.reshape(())
    start_total = jnp.zeros((2, tile_count, TILE), jnp.float32)
    totals = sweep(home_tiles, candidate, near_list, far_list, 0, pair_total, start_total)
    aux_field = totals[0].reshape(atom_count)
    resid_field = totals[1].reshape(atom_count)
    field = negativity + aux_field + resid_field
    global_sums = lax.psum(
        (jnp.sum(charge_row), jnp.sum(field / hardness_row), jnp.sum(1.0 / hardness_row)),
        ("brick", "plane"),
    )
    potential_level = (global_sums[0] + global_sums[1]) / global_sums[2]
    charges = (potential_level - field) / hardness_row
    stacked = jnp.stack([charge_row, charges]).reshape(2, tile_count, TILE)
    target = owner_tile.reshape(tile_count)
    planes = lax.axis_size("plane")
    quarter = tile_count // planes
    ranking = jnp.argsort(
        target // tile_count * tile_count + jnp.arange(tile_count, dtype=jnp.int32)
    )
    outgoing = jnp.take(stacked, ranking, axis=1).reshape(2, planes, quarter, TILE)
    slot_rows = (
        jnp.take(target % tile_count, ranking).astype(jnp.float32).reshape(1, planes, quarter)
    )
    arrived, arrived_slots = (
        lax.all_to_all(outgoing, "plane", split_axis=1, concat_axis=1, tiled=True),
        lax.all_to_all(slot_rows, "plane", split_axis=1, concat_axis=1, tiled=True),
    )
    arrived = arrived.reshape(2, tile_count, TILE)
    slot_ids = arrived_slots.reshape(tile_count).astype(jnp.int32)
    placer = (slot_ids[None, :] == jnp.arange(tile_count, dtype=jnp.int32)[:, None]).astype(
        jnp.float32
    )
    placed = jnp.einsum("sk,ckj->csj", placer, arrived, precision=lax.Precision.HIGHEST)
    previous = aux_prev.reshape(tile_count, TILE)
    next_aux = 2.0 * placed[0] - previous + kappa * (placed[1] - placed[0])
    return (charges.reshape(aux.shape), next_aux.reshape(aux.shape), resid_field.reshape(aux.shape))


def solution(mesh):
    in_specs = (
        P("brick", "plane", None, None),
        P("brick", "plane", None),
        P("brick", "plane", None),
        P("brick", "plane", None),
        P("brick", "plane", None),
        P("brick", "plane", None),
        P("brick", "plane", None),
        P("brick", "plane"),
        P("brick", "plane", None),
        P(),
        P(),
        P(),
    )
    out_specs = (P("brick", "plane", None), P("brick", "plane", None), P("brick", "plane", None))
    return jax.shard_map(
        on_device, mesh=mesh, in_specs=in_specs, out_specs=out_specs, check_vma=False
    )
```

profile of v0, /device:TPU:0, one launch (start us, length us, event | category | flops | bytes accessed | tf_op | source)
XLA Modules:
  0.0 278.8 jit_solution(11771305782175229596)
XLA Ops:
  0.7 0.9 copy.100
  1.6 0.9 select_reduce_fusion.2
  2.5 0.8 fusion.37
  3.8 2.9 %collective-permute-start.1 = (f32[1,1,6,4096]{3,2,1,0:T(8,128)S(1)}, f32[1,1,6,4096]{3,2,1,0:T(8,128)S(1)}, u32[]{:S(2)}, u32[]{:S(2)}) collective-permute-start(f32[1,1,6,4096]{3,2,1,0:T(8,128)S(1)} %fusion.37), channel_id=1, source_target_pairs={{4,0},{8,4},{12,8},{16,12},{20,16},{24,20},{28,24},{0,28},{5,1},{9... | collective-permute-start | bytes 294920 | tf_op jit(solution)/shard_map/ppermute | solution.py:27
  6.8 0.7 and_select_fusion
  7.4 2.0 sort.17
  9.5 0.8 gather_fusion.3
  10.3 0.7 convert_element_type.29
  10.9 5.6 %all-to-all-start.1 = ((f32[1,4,16]{2,0,1:T(1,128)}), f32[1,4,16]{2,0,1:T(1,128)S(1)}, u32[]{:S(2)}, u32[]{:S(2)}) async-start(f32[1,4,16]{2,0,1:T(1,128)} %bitcast.35), calls=%async_computation.1 | async-start | bytes 4096 | tf_op jit(solution)/shard_map/all_to_all | solution.py:147
  16.5 0.8 bitcast_dynamic-update-slice_fusion.2
  18.6 1.3 fusion.42
  19.8 0.7 reduce.29
  21.3 0.7 fusion.43
  22.0 0.7 and_reduce_fusion
  22.6 1.4 scatter.14
  24.0 1.9 dynamic-slice.29
  27.1 1.4 scatter.15
  30.3 2.1 collective-permute-start.2
  32.4 1.9 collective-permute-start.3
  34.3 9.9 %collective-permute-done.2 = f32[3,1,6,4096]{3,2,1,0:T(8,128)S(1)} collective-permute-done((f32[3,1,6,4096]{3,2,1,0:T(8,128)S(1)}, f32[3,1,6,4096]{3,2,1,0:T(8,128)S(1)}, u32[]{:S(2)}, u32[]{:S(2)}) %collective-permute-start.2) | collective-permute-done | bytes 294944 | tf_op jit(solution)/shard_map/ppermute | solution.py:24
  44.2 5.8 %collective-permute-done.3 = f32[3,1,6,4096]{3,2,1,0:T(8,128)S(1)} collective-permute-done((f32[3,1,6,4096]{3,2,1,0:T(8,128)S(1)}, f32[3,1,6,4096]{3,2,1,0:T(8,128)S(1)}, u32[]{:S(2)}, u32[]{:S(2)}) %collective-permute-start.3) | collective-permute-done | bytes 294944 | tf_op jit(solution)/shard_map/ppermute | solution.py:27
  51.6 28.7 %while.14 = (s32[]{:T(128)}, f32[2,64,64]{1,2,0:T(8,128)S(1)}, s32[]{:T(128)}, s32[1752]{0:T(1024)S(1)}, f32[6,320,64]{2,0,1:T(8,128)S(1)}, /*index=5*/s32[]{:T(...) while((s32[]{:T(128)}, f32[2,64,64]{1,2,0:T(8,128)S(1)}, ...), condition=%wide.region_6.0_spmd, body=%wide.region_5.0_spmd.sunk | while | flops 72616448 | bytes 5868207 | solution.py:87
  51.6 0.7 dynamic-slice_compare_fusion.2
  52.4 1.0 gather_fusion.1
  54.2 1.0 gather_fusion
  55.9 23.9 %fusion.62 = f32[2,256,64]{2,0,1:T(2,128)S(1)} fusion(f32[256,64]{1,0:T(8,128)S(1)} %bitcast.116, f32[256,64]{1,0:T(8,128)S(1)} %bitcast.112, f32[256,64]{1,0:T(8,128)S(1)} %bitcast.117, f32[256,64]{1,0:T(8,128)S(1)} %bitcast.113, f32[256,64]{1,0:T(8,128)S(1)} %bitcast.118, f32[256,64]{1,0:T(8,128)S(1)} %bitcast.114, f32[256,64]{1,0:T(8,128)S(1)} %bitcast.115, ...), kind=kOutput, calls=%fused_computation.26.clone.3 | convolution fusion | flops 47185920 | bytes 1451008 | tf_op jit(solution)/shard_map/while/body/pij,cpj->cpi/dot_general | solution.py:66
  82.4 182.0 %all-reduce.2 = (f32[]{:T(128)}, f32[]{:T(128)}) all-reduce(f32[]{:T(128)S(6)} %add.157, f32[]{:T(128)} %divide_reduce_fusion.1), channel_id=1, replica_groups=mesh['brick'=8,'plane'=4] {'brick','plane'}, use_global_device_ids=true, to_apply=%region_1.0 | all-reduce | flops 2 | bytes 16 | tf_op jit(solution)/shard_map/psum | solution.py:128
  266.5 0.7 reshape.419
  267.3 3.3 %all-to-all-start = ((f32[4,1,2048]{2,1,0:T(1,128)}), f32[4,1,2048]{2,1,0:T(1,128)S(1)}, u32[]{:S(2)}, u32[]{:S(2)}) async-start(f32[4,1,2048]{2,1,0:T(1,128)} %reshape.419), calls=%async_computation | async-start | bytes 65536 | tf_op jit(solution)/shard_map/all_to_all | solution.py:146
  270.8 5.3 %all-to-all-done = f32[4,1,2048]{2,1,0:T(1,128)S(1)} async-done(((f32[4,1,2048]{2,1,0:T(1,128)}), f32[4,1,2048]{2,1,0:T(1,128)S(1)}, u32[]{:S(2)}, u32[]{:S(2)}) %all-to-all-start) | async-done | bytes 32800 | tf_op jit(solution)/shard_map/all_to_all | solution.py:146
  276.7 0.7 reduce.32
  278.1 0.7 subtract_add_fusion
  (89 shorter events, 10.2 us)
Async XLA Ops:
  0.6 21.3 %copy-start.7 = (s32[2]{0:T(128)S(1)}, s32[2]{0:T(128)}, u32[]{:S(2)}) copy-start(s32[2]{0:T(128)} %constant.238.clone.1) | copy-start | bytes 28
  0.6 19.9 %copy-start = (f32[1,1,3,4096]{3,1,2,0:T(1,128)S(1)}, f32[1,1,3,4096]{3,1,2,0:T(1,128)}, u32[]{:S(2)}) copy-start(f32[1,1,3,4096]{3,1,2,0:T(1,128)} %param.22) | copy-start | bytes 147460
  0.7 17.9 %copy-start.1 = (f32[1,1,4096]{2,1,0:T(1,128)S(1)}, f32[1,1,4096]{2,1,0:T(1,128)}, u32[]{:S(2)}) copy-start(f32[1,1,4096]{2,1,0:T(1,128)} %param.23) | copy-start | bytes 49156
  0.7 19.2 %copy-start.2 = (f32[1,1,4096]{2,1,0:T(1,128)S(1)}, f32[1,1,4096]{2,1,0:T(1,128)}, u32[]{:S(2)}) copy-start(f32[1,1,4096]{2,1,0:T(1,128)} %param.25) | copy-start | bytes 49156
  1.6 27.8 %copy-start.5 = (s32[1,1,1496]{2,1,0:T(1,128)S(1)}, s32[1,1,1496]{2,1,0:T(1,128)}, u32[]{:S(2)}) copy-start(s32[1,1,1496]{2,1,0:T(1,128)} %param.28) | copy-start | bytes 17956
  1.6 27.9 %copy-start.6 = (s32[1,1,1496]{2,1,0:T(1,128)S(1)}, s32[1,1,1496]{2,1,0:T(1,128)}, u32[]{:S(2)}) copy-start(s32[1,1,1496]{2,1,0:T(1,128)} %param.27) | copy-start | bytes 17956
  3.3 27.0 %collective-permute-start = (f32[1,1,6,4096]{3,2,1,0:T(8,128)S(1)}, f32[1,1,6,4096]{3,2,1,0:T(8,128)S(1)}, u32[]{:S(2)}, u32[]{:S(2)}) collective-permute-start(f32[1,1,6,4096]{3,2,1,0:T(8,128)S(1)} %fusion.37), channel_id=1, source_target_pairs={{0,4},{4,8},{8,12},{12,16},{16,20},{20,24},{24,28},{28,0},{1,5},{5... | collective-permute-start | bytes 294920 | tf_op jit(solution)/shard_map/ppermute | solution.py:24
  3.8 26.4 %collective-permute-start.1 = (f32[1,1,6,4096]{3,2,1,0:T(8,128)S(1)}, f32[1,1,6,4096]{3,2,1,0:T(8,128)S(1)}, u32[]{:S(2)}, u32[]{:S(2)}) collective-permute-start(f32[1,1,6,4096]{3,2,1,0:T(8,128)S(1)} %fusion.37), channel_id=1, source_target_pairs={{4,0},{8,4},{12,8},{16,12},{20,16},{24,20},{28,24},{0,28},{5,1},{9... | collective-permute-start | bytes 294920 | tf_op jit(solution)/shard_map/ppermute | solution.py:27
  10.9 256.3 %all-to-all-start.1 = ((f32[1,4,16]{2,0,1:T(1,128)}), f32[1,4,16]{2,0,1:T(1,128)S(1)}, u32[]{:S(2)}, u32[]{:S(2)}) async-start(f32[1,4,16]{2,0,1:T(1,128)} %bitcast.35), calls=%async_computation.1 | async-start | bytes 4096 | tf_op jit(solution)/shard_map/all_to_all | solution.py:147
  30.3 13.9 %collective-permute-start.2 = (f32[3,1,6,4096]{3,2,1,0:T(8,128)S(1)}, f32[3,1,6,4096]{3,2,1,0:T(8,128)S(1)}, u32[]{:S(2)}, u32[]{:S(2)}) collective-permute-start(f32[3,1,6,4096]{3,2,1,0:T(8,128)S(1)} %pad_maximum_fusion), channel_id=1, source_target_pairs={{0,1},{1,2},{2,3},{3,0},{4,5},{5,6},{6,7},{7,4},{8,9},{9,10},{10,1... | collective-permute-start | bytes 884744 | tf_op jit(solution)/shard_map/ppermute | solution.py:24
  32.4 17.6 %collective-permute-start.3 = (f32[3,1,6,4096]{3,2,1,0:T(8,128)S(1)}, f32[3,1,6,4096]{3,2,1,0:T(8,128)S(1)}, u32[]{:S(2)}, u32[]{:S(2)}) collective-permute-start(f32[3,1,6,4096]{3,2,1,0:T(8,128)S(1)} %pad_maximum_fusion), channel_id=1, source_target_pairs={{1,0},{2,1},{3,2},{0,3},{5,4},{6,5},{7,6},{4,7},{9,8},{10,9},{11,1... | collective-permute-start | bytes 884744 | tf_op jit(solution)/shard_map/ppermute | solution.py:27
  80.3 197.8 %copy-start.4 = (f32[1,1,4096]{2,1,0:T(1,128)S(1)}, f32[1,1,4096]{2,1,0:T(1,128)}, u32[]{:S(2)}) copy-start(f32[1,1,4096]{2,1,0:T(1,128)} %param.24) | copy-start | bytes 49156
  267.3 8.9 %all-to-all-start = ((f32[4,1,2048]{2,1,0:T(1,128)}), f32[4,1,2048]{2,1,0:T(1,128)S(1)}, u32[]{:S(2)}, u32[]{:S(2)}) async-start(f32[4,1,2048]{2,1,0:T(1,128)} %reshape.419), calls=%async_computation | async-start | bytes 65536 | tf_op jit(solution)/shard_map/all_to_all | solution.py:146
  270.8 8.0 %copy-start.3 = (f32[1,1,4096]{2,1,0:T(1,128)}, f32[1,1,4096]{2,1,0:T(1,128)S(1)}, u32[]{:S(2)}) copy-start(f32[1,1,4096]{2,1,0:T(1,128)S(1)} %reshape_squeeze.7) | copy-start | bytes 49156
where the time goes:
time: 280 us; the launch traced here: 279 us
  blocking collectives  182 us (65%)
  matrix products  24.5 us (9%)
  waiting for transfers between devices  21 us (8%)
  starting transfers between devices  16.2 us (6%)
  local copies, waits for them, and re-layouts  16 us (6%)
  other arithmetic  13.4 us (5%)
  between operations  5.56 us (2%)
    psum x1, blocking collectives, on_device(): lax.psum((jnp.sum(charge_row), jnp.sum(field / hardness_row), jnp.sum(1.0...  182 us
    dot_general x1, matrix products, pair_terms(): jnp.einsum('pij,cpj->cpi', kernel, far_atoms[3:5], precision=lax.Precisio...  23.9 us
    ppermute x2, waiting for transfers between devices, extended(): lax.ppermute(lax.slice_in_dim(block, block.shape[dim] - width, None, axis...  9.89 us
    ppermute x2, waiting for transfers between devices, extended(): lax.ppermute(lax.slice_in_dim(block, 0, width, axis=dim), axis, backward)  5.78 us
  transfers between devices with their start and end apart: 6, of which 3 were waited for; matrix products, arithmetic and copies ran while one was open for 17% of the time, Pallas kernels for 0%

commit v1 on v0

v1 whole, which is shorter than its diff:
```python
import jax
import jax.numpy as jnp
from jax import lax
from jax.sharding import PartitionSpec as P
from jax.experimental import pallas as pl
from jax.experimental.pallas import tpu as pltpu

TX = 2
TY = 4
TILE = 64


cell_edge = 8.0
cutoff = 10.0
soften = 0.5
kappa = 1.86
pair_group = 256


def shifted_from(block, axis, step):
    count = lax.axis_size(axis)
    pairs = [(i, (i + step) % count) for i in range(count)]
    return lax.ppermute(block, axis, pairs)


def neighbours(block):
    return [
        block,
        shifted_from(block, "brick", 1),
        shifted_from(block, "brick", -1),
        shifted_from(block, "plane", 1),
        shifted_from(block, "plane", -1),
    ]


def lookup(type_table, type_row):
    chosen = (
        type_row[None, :] == jnp.arange(type_table.shape[0], dtype=jnp.int32)[:, None]
    ).astype(type_table.dtype)
    return jnp.sum(type_table[:, None] * chosen, axis=0)


def candidates(blocks, tile_count):
    joined = jnp.stack(blocks, axis=1)
    offsets = jnp.zeros((6, 5), jnp.float32)
    offsets = offsets.at[0, 1].set(-TX * cell_edge).at[0, 2].set(TX * cell_edge)
    offsets = offsets.at[1, 3].set(-TY * cell_edge).at[1, 4].set(TY * cell_edge)
    joined = joined + offsets[:, :, None]
    return joined.reshape(6, 5 * tile_count, TILE)


LANES = 128


def sweep_kernel(near_ref, far_ref, count_ref, home_ref, cand_ref, out_ref, spread_ref, acc_ref):
    atom_count = home_ref.shape[0]
    tile_count = atom_count // TILE
    cand_tiles = cand_ref.shape[0]
    pair_cap = near_ref.shape[0]
    chunk = 512
    for q in range(4):
        for r in range(atom_count // chunk):
            column = home_ref[r * chunk:(r + 1) * chunk, q:q + 1]
            spread_ref[q, r * chunk:(r + 1) * chunk, :] = jnp.broadcast_to(column, (chunk, LANES))
    acc_ref[...] = jnp.zeros(acc_ref.shape, jnp.float32)
    total = count_ref[0]
    lane = lax.broadcasted_iota(jnp.int32, (1, LANES), 1)
    left = lane < TILE

    def body(k, carry):
        first = 2 * k
        second = jnp.minimum(first + 1, pair_cap - 1)
        has_second = first + 1 < total
        home_a = jnp.clip(near_ref[first], 0, tile_count - 1)
        cand_a = jnp.clip(far_ref[first], 0, cand_tiles - 1)
        home_b = jnp.clip(near_ref[second], 0, tile_count - 1)
        cand_b = jnp.clip(far_ref[second], 0, cand_tiles - 1)
        rows = jnp.where(left, cand_ref[cand_a], cand_ref[cand_b])
        base_a = pl.multiple_of(home_a * TILE, TILE)
        base_b = pl.multiple_of(home_b * TILE, TILE)

        def near_q(q):
            return jnp.where(
                left, spread_ref[q, pl.ds(base_a, TILE), :], spread_ref[q, pl.ds(base_b, TILE), :]
            )

        delta_x = near_q(0) - rows[0:1]
        delta_y = near_q(1) - rows[1:2]
        delta_z = near_q(2) - rows[2:3]
        dist_sq = delta_x * delta_x + delta_y * delta_y + delta_z * delta_z
        shifted = dist_sq + soften * soften
        inv_spacing = lax.rsqrt(shifted)
        spacing = shifted * inv_spacing
        inv_width = lax.rsqrt(near_q(3) + rows[3:4])
        taper = jnp.maximum(1.0 - dist_sq * (1.0 / (cutoff * cutoff)), 0.0)
        kernel = lax.erf(inv_width * spacing) * inv_spacing * (taper * taper)
        row_id = lax.broadcasted_iota(jnp.int32, (TILE, LANES), 0)
        lane_id = lax.broadcasted_iota(jnp.int32, (TILE, LANES), 1)
        self_a = (cand_a == home_a).astype(jnp.int32)
        self_b = (cand_b == home_b).astype(jnp.int32)
        self_half = jnp.where(lane_id < TILE, self_a, self_b)
        diagonal = (lane_id % TILE) == row_id
        kernel = jnp.where(diagonal & (self_half > 0), 0.0, kernel)
        keep_b = lane >= TILE + TILE * (1 - has_second.astype(jnp.int32))
        kernel_a = jnp.where(left, kernel, 0.0)
        kernel_b = jnp.where(keep_b, kernel, 0.0)
        for c in range(2):
            charge = rows[4 + c:5 + c]
            acc_ref[c, pl.ds(base_a, TILE), :] += kernel_a * charge
            acc_ref[c, pl.ds(base_b, TILE), :] += kernel_b * charge
        return carry

    lax.fori_loop(0, (total + 1) // 2, body, 0)
    ones = jnp.ones((8, LANES), jnp.float32)
    for c in range(2):
        summed = lax.dot_general(
            ones,
            acc_ref[c],
            (((1,), (1,)), ((), ())),
            precision=lax.Precision.HIGHEST,
            preferred_element_type=jnp.float32,
        )
        out_ref[c:c + 1, :] = summed[0:1]


def sweep(home_cols, cand_rows, near_list, far_list, pair_total):
    atom_count = home_cols.shape[0]
    smem = pl.BlockSpec(memory_space=pltpu.SMEM)
    vmem = pl.BlockSpec(memory_space=pltpu.VMEM)
    return pl.pallas_call(
        sweep_kernel,
        out_shape=jax.ShapeDtypeStruct((2, atom_count), jnp.float32),
        in_specs=[smem, smem, smem, vmem, vmem],
        out_specs=vmem,
        scratch_shapes=[
            pltpu.VMEM((4, atom_count, LANES), jnp.float32),
            pltpu.VMEM((2, atom_count, LANES), jnp.float32),
        ],
        compiler_params=pltpu.CompilerParams(vmem_limit_bytes=48 * 1024 * 1024),
    )(near_list, far_list, pair_total, home_cols, cand_rows)


def on_device(
    positions,
    aux,
    aux_prev,
    resid,
    types,
    pair_tiles,
    pair_cands,
    pair_count,
    owner_tile,
    electroneg,
    hardness,
    widths,
):
    atom_count = aux.shape[-1]
    tile_count = atom_count // TILE
    type_row = types.reshape(atom_count)
    negativity = lookup(electroneg, type_row)
    hardness_row = lookup(hardness, type_row)
    radius = lookup(widths, type_row)
    charge_row = aux.reshape(atom_count)
    resid_row = resid.reshape(atom_count)
    packed = jnp.concatenate(
        [positions.reshape(3, atom_count), charge_row[None], resid_row[None], radius[None]], axis=0
    )
    blocks = neighbours(packed)
    candidate = candidates(blocks, tile_count)
    cand_rows = jnp.concatenate(
        [candidate[:3], jnp.square(candidate[5:6]), candidate[3:5], jnp.zeros_like(candidate[:2])],
        axis=0,
    ).transpose(1, 0, 2)
    cand_rows = jnp.concatenate([cand_rows, cand_rows], axis=-1)
    home_cols = jnp.concatenate(
        [packed[:3], jnp.square(packed[5:6]), jnp.zeros_like(packed[:4])], axis=0
    ).T
    near_list = pair_tiles.reshape(-1)
    far_list = pair_cands.reshape(-1)
    pair_total = pair_count.reshape(1)
    totals = sweep(home_cols, cand_rows, near_list, far_list, pair_total)
    aux_field = totals[0].reshape(atom_count)
    resid_field = totals[1].reshape(atom_count)
    field = negativity + aux_field + resid_field
    global_sums = lax.psum(
        (jnp.sum(charge_row), jnp.sum(field / hardness_row), jnp.sum(1.0 / hardness_row)),
        ("brick", "plane"),
    )
    potential_level = (global_sums[0] + global_sums[1]) / global_sums[2]
    charges = (potential_level - field) / hardness_row
    stacked = jnp.stack([charge_row, charges]).reshape(2, tile_count, TILE)
    target = owner_tile.reshape(tile_count)
    planes = lax.axis_size("plane")
    quarter = tile_count // planes
    ranking = jnp.argsort(
        target // tile_count * tile_count + jnp.arange(tile_count, dtype=jnp.int32)
    )
    outgoing = jnp.take(stacked, ranking, axis=1).reshape(2, planes, quarter, TILE)
    slot_rows = (
        jnp.take(target % tile_count, ranking).astype(jnp.float32).reshape(1, planes, quarter)
    )
    arrived, arrived_slots = (
        lax.all_to_all(outgoing, "plane", split_axis=1, concat_axis=1, tiled=True),
        lax.all_to_all(slot_rows, "plane", split_axis=1, concat_axis=1, tiled=True),
    )
    arrived = arrived.reshape(2, tile_count, TILE)
    slot_ids = arrived_slots.reshape(tile_count).astype(jnp.int32)
    placer = (slot_ids[None, :] == jnp.arange(tile_count, dtype=jnp.int32)[:, None]).astype(
        jnp.float32
    )
    placed = jnp.einsum("sk,ckj->csj", placer, arrived, precision=lax.Precision.HIGHEST)
    previous = aux_prev.reshape(tile_count, TILE)
    next_aux = 2.0 * placed[0] - previous + kappa * (placed[1] - placed[0])
    return (charges.reshape(aux.shape), next_aux.reshape(aux.shape), resid_field.reshape(aux.shape))


def solution(mesh):
    in_specs = (
        P("brick", "plane", None, None),
        P("brick", "plane", None),
        P("brick", "plane", None),
        P("brick", "plane", None),
        P("brick", "plane", None),
        P("brick", "plane", None),
        P("brick", "plane", None),
        P("brick", "plane"),
        P("brick", "plane", None),
        P(),
        P(),
        P(),
    )
    out_specs = (P("brick", "plane", None), P("brick", "plane", None), P("brick", "plane", None))
    return jax.shard_map(
        on_device, mesh=mesh, in_specs=in_specs, out_specs=out_specs, check_vma=False
    )
```

time: 280 us -> 151 us (0.54)
  blocking collectives: 182 us -> 76.1 us
  matrix products: 24.5 us -> 0.24 us
  Pallas kernels: 0 us -> 18.8 us
  waiting for transfers between devices: 21 us -> 4.91 us
    psum x1, blocking collectives: 182 us -> 76.1 us  [on_device(): lax.psum((jnp.sum(charge_row), jnp.sum(field / hardness_row), jnp.sum(1.0...]
    dot_general x2 -> x0, matrix products: 24.3 us -> none  [the longest x1 23.9 us: pair_terms(): jnp.einsum('pij,cpj->cpi', kernel, far_atoms[3:5], precision=lax.Precisio...]
    pallas_call x0 -> x1, Pallas kernels: none -> 18.8 us  [sweep(): pl.pallas_call(sweep_kernel, out_shape=jax.ShapeDtypeStruct((2, atom_coun...]
    ppermute x4, waiting for transfers between devices: 15.7 us -> 0.01 us  [shifted_from(): return lax.ppermute(block, axis, pairs)]
  transfers between devices with their start and end apart: 6 -> 6, of which waited for: 3 -> 1; matrix products, arithmetic and copies ran while one was open for 17% -> 16% of each run, Pallas kernels for 0% -> 12%
where the time goes in v1:
time: 151 us; the launch traced here: 150 us
  blocking collectives  76.1 us (50%)
  Pallas kernels  18.8 us (12%)
  local copies, waits for them, and re-layouts  16.4 us (11%)
  starting transfers between devices  15 us (10%)
  other arithmetic  13.4 us (9%)
  between operations  5.53 us (4%)
  waiting for transfers between devices  4.91 us (3%)
    psum x1, blocking collectives, on_device(): lax.psum((jnp.sum(charge_row), jnp.sum(field / hardness_row), jnp.sum(1.0...  76.1 us
    pallas_call x1, Pallas kernels, sweep(): pl.pallas_call(sweep_kernel, out_shape=jax.ShapeDtypeStruct((2, atom_coun...  18.8 us
    ppermute x4, starting transfers between devices, shifted_from(): return lax.ppermute(block, axis, pairs)  7.72 us
    all_to_all x1, waiting for transfers between devices, on_device(): lax.all_to_all(outgoing, 'plane', split_axis=1, concat_axis=1, tiled=True)  4.9 us
    all_to_all x1, starting transfers between devices, on_device(): lax.all_to_all(slot_rows, 'plane', split_axis=1, concat_axis=1, tiled=True)  3.76 us
    all_to_all x1, starting transfers between devices, on_device(): lax.all_to_all(outgoing, 'plane', split_axis=1, concat_axis=1, tiled=True)  3.55 us
    another operation x5, local copies, waits for them, and re-layouts  3.12 us
  transfers between devices with their start and end apart: 6, of which 1 were waited for; matrix products, arithmetic and copies ran while one was open for 16% of the time, Pallas kernels for 12%

profile of v1, /device:TPU:0, one launch (start us, length us, event | category | flops | bytes accessed | tf_op | source)
XLA Modules:
  0.0 150.4 jit_solution(4893091097900328540)
XLA Ops:
  0.6 0.8 copy.65
  1.5 1.5 %select_reduce_fusion.2 = (f32[4096]{0:T(1024)}, f32[4096]{0:T(1024)}, f32[4096]{0:T(1024)S(1)}) fusion(f32[8]{0:T(128)} %param.29, s32[4096]{0:T(1024)} %bitcast.100, f32[8]{0:T(128)} %param.30, f32[8]{0:T(128)} %param.31), kind=kLoop, calls=%fused_computation.15 | loop fusion | flops 217088 | bytes 65632 | tf_op jit(solution)/shard_map/reduce_sum | solution.py:40
  3.0 1.4 pad_maximum_fusion.1
  4.9 2.9 %collective-permute-start.1 = (f32[6,4096]{1,0:T(8,128)}, f32[6,4096]{1,0:T(8,128)S(1)}, u32[]{:S(2)}, u32[]{:S(2)}) collective-permute-start(f32[6,4096]{1,0:T(8,128)} %pad_maximum_fusion.1), channel_id=1, source_target_pairs={{0,28},{4,0},{8,4},{12,8},{16,12},{20,16},{24,20},{28,24},{1,29},{... | collective-permute-start | bytes 294920 | tf_op jit(solution)/shard_map/ppermute | solution.py:23
  7.8 2.3 %collective-permute-start.2 = (f32[6,4096]{1,0:T(8,128)}, f32[6,4096]{1,0:T(8,128)S(1)}, u32[]{:S(2)}, u32[]{:S(2)}) collective-permute-start(f32[6,4096]{1,0:T(8,128)} %pad_maximum_fusion.1), channel_id=1, source_target_pairs={{0,1},{1,2},{2,3},{3,0},{4,5},{5,6},{6,7},{7,4},{8,9},{9,10},{10,1... | collective-permute-start | bytes 294920 | tf_op jit(solution)/shard_map/ppermute | solution.py:23
  10.1 2.0 %collective-permute-start.3 = (f32[6,4096]{1,0:T(8,128)}, f32[6,4096]{1,0:T(8,128)S(1)}, u32[]{:S(2)}, u32[]{:S(2)}) collective-permute-start(f32[6,4096]{1,0:T(8,128)} %pad_maximum_fusion.1), channel_id=1, source_target_pairs={{0,3},{1,0},{2,1},{3,2},{4,7},{5,4},{6,5},{7,6},{8,11},{9,8},{10,9... | collective-permute-start | bytes 294920 | tf_op jit(solution)/shard_map/ppermute | solution.py:23
  12.2 0.7 and_select_fusion
  12.8 2.0 %sort.17 = (s32[64]{0:T(128)}, s32[64]{0:T(128)S(1)}) sort(s32[64]{0:T(128)S(1)} %get-tuple-element.71, s32[64]{0:T(128)S(1)} %iota.30), dimensions={0}, to_apply=%region_10.0 | sort | flops 384 | bytes 1024 | tf_op jit(solution)/shard_map/jit(argsort)/sort | solution.py:195
  14.9 0.8 gather_fusion.1
  15.7 0.7 convert_element_type.28
  16.3 3.8 %all-to-all-start.1 = ((f32[1,4,16]{2,0,1:T(1,128)}), f32[1,4,16]{2,0,1:T(1,128)}, u32[]{:S(2)}, u32[]{:S(2)}) async-start(f32[1,4,16]{2,0,1:T(1,128)} %bitcast.31), calls=%async_computation.1 | async-start | bytes 4096 | tf_op jit(solution)/shard_map/all_to_all | solution.py:204
  20.1 0.8 bitcast_dynamic-update-slice_fusion.4
  21.0 0.6 fusion.13
  22.2 0.6 and_reduce_fusion
  22.9 1.3 scatter.14
  24.2 1.9 %dynamic-slice.29 = f32[1,1]{0,1:T(1,128)} dynamic-slice(f32[6,5]{0,1:T(8,128)S(1)} %scatter.14, s32[]{:T(128)} %bitcast.14, s32[]{:T(128)} %bitcast.15), dynamic_slice_sizes={1,1} | dynamic-slice | bytes 12 | tf_op jit(solution)/shard_map/dynamic-slice.17
  27.3 1.3 scatter.15
  28.6 0.6 pad.23.clone
  31.3 1.3 fusion.10
  32.6 0.7 stack.32
  34.5 0.9 fusion
  36.6 1.0 square.27
  38.6 18.8 %shard_map.139 = f32[2,4096]{1,0:T(2,128)S(1)} custom-call(s32[1496]{0:T(1024)S(1)} %reduce.14.near_ref, s32[1496]{0:T(1024)S(1)} %reduce.15.far_ref, s32[1]{0:T(128)} %bitcast.76.count_ref, f32[4096,8]{1,0:T(8,128)S(1)} %bitcast.77, f32[320,8,128]{2,1,0:T(8,128)S(1)} %pad_maximum_fusion.cand_ref), custom_call_target="tpu_custom_call" | custom-call | tf_op jit(solution)/shard_map/pallas_call | solution.py:130
  57.4 0.6 divide_reduce_fusion
  59.3 76.1 %all-reduce = (f32[]{:T(128)}, f32[]{:T(128)}) all-reduce(f32[]{:T(128)S(6)} %add.83, f32[]{:T(128)} %get-tuple-element.55), channel_id=1, replica_groups=mesh['brick'=8,'plane'=4] {'brick','plane'}, use_global_device_ids=true, to_apply=%region_1.0 | all-reduce | flops 2 | bytes 16 | tf_op jit(solution)/shard_map/psum | solution.py:185
  137.0 0.8 gather_fusion
  137.8 0.7 reshape.354
  138.6 3.6 %all-to-all-start = ((f32[4,1,2048]{2,1,0:T(1,128)}), f32[4,1,2048]{2,1,0:T(1,128)S(1)}, u32[]{:S(2)}, u32[]{:S(2)}) async-start(f32[4,1,2048]{2,1,0:T(1,128)} %reshape.354), calls=%async_computation | async-start | bytes 65536 | tf_op jit(solution)/shard_map/all_to_all | solution.py:203
  142.1 0.7 convert_reduce_fusion
  142.9 4.9 %all-to-all-done = f32[4,1,2048]{2,1,0:T(1,128)S(1)} async-done(((f32[4,1,2048]{2,1,0:T(1,128)}), f32[4,1,2048]{2,1,0:T(1,128)S(1)}, u32[]{:S(2)}, u32[]{:S(2)}) %all-to-all-start) | async-done | bytes 32800 | tf_op jit(solution)/shard_map/all_to_all | solution.py:203
  148.3 0.7 reduce.32
  149.7 0.7 fusion.6
  (78 shorter events, 7.4 us)
Async XLA Ops:
  0.6 21.6 %copy-start.10 = (s32[2]{0:T(128)S(1)}, s32[2]{0:T(128)}, u32[]{:S(2)}) copy-start(s32[2]{0:T(128)} %constant.172.clone.1) | copy-start | bytes 28
  4.4 29.7 %collective-permute-start = (f32[6,4096]{1,0:T(8,128)}, f32[6,4096]{1,0:T(8,128)S(1)}, u32[]{:S(2)}, u32[]{:S(2)}) collective-permute-start(f32[6,4096]{1,0:T(8,128)} %pad_maximum_fusion.1), channel_id=1, source_target_pairs={{0,4},{4,8},{8,12},{12,16},{16,20},{20,24},{24,28},{28,0},{1,5},{5... | collective-permute-start | bytes 294920 | tf_op jit(solution)/shard_map/ppermute | solution.py:23
  4.9 29.2 %collective-permute-start.1 = (f32[6,4096]{1,0:T(8,128)}, f32[6,4096]{1,0:T(8,128)S(1)}, u32[]{:S(2)}, u32[]{:S(2)}) collective-permute-start(f32[6,4096]{1,0:T(8,128)} %pad_maximum_fusion.1), channel_id=1, source_target_pairs={{0,28},{4,0},{8,4},{12,8},{16,12},{20,16},{24,20},{28,24},{1,29},{... | collective-permute-start | bytes 294920 | tf_op jit(solution)/shard_map/ppermute | solution.py:23
  7.8 26.4 %collective-permute-start.2 = (f32[6,4096]{1,0:T(8,128)}, f32[6,4096]{1,0:T(8,128)S(1)}, u32[]{:S(2)}, u32[]{:S(2)}) collective-permute-start(f32[6,4096]{1,0:T(8,128)} %pad_maximum_fusion.1), channel_id=1, source_target_pairs={{0,1},{1,2},{2,3},{3,0},{4,5},{5,6},{6,7},{7,4},{8,9},{9,10},{10,1... | collective-permute-start | bytes 294920 | tf_op jit(solution)/shard_map/ppermute | solution.py:23
  10.1 24.1 %collective-permute-start.3 = (f32[6,4096]{1,0:T(8,128)}, f32[6,4096]{1,0:T(8,128)S(1)}, u32[]{:S(2)}, u32[]{:S(2)}) collective-permute-start(f32[6,4096]{1,0:T(8,128)} %pad_maximum_fusion.1), channel_id=1, source_target_pairs={{0,3},{1,0},{2,1},{3,2},{4,7},{5,4},{6,5},{7,6},{8,11},{9,8},{10,9... | collective-permute-start | bytes 294920 | tf_op jit(solution)/shard_map/ppermute | solution.py:23
  14.9 14.4 %copy-start.5 = (s32[1024]{0:T(1024)}, s32[1024]{0:T(1024)S(1)}, u32[]{:S(2)}) copy-start(s32[1024]{0:T(1024)S(1)} %pad_clamp_fusion) | copy-start | bytes 12292
  16.3 122.2 %all-to-all-start.1 = ((f32[1,4,16]{2,0,1:T(1,128)}), f32[1,4,16]{2,0,1:T(1,128)}, u32[]{:S(2)}, u32[]{:S(2)}) async-start(f32[1,4,16]{2,0,1:T(1,128)} %bitcast.31), calls=%async_computation.1 | async-start | bytes 4096 | tf_op jit(solution)/shard_map/all_to_all | solution.py:204
  20.9 9.1 %copy-start.6 = (s32[1,1,1496]{2,1,0:T(1,128)S(1)}, s32[1,1,1496]{2,1,0:T(1,128)}, u32[]{:S(2)}) copy-start(s32[1,1,1496]{2,1,0:T(1,128)} %param.25) | copy-start | bytes 17956
  20.9 9.1 %copy-start.7 = (s32[1,1,1496]{2,1,0:T(1,128)S(1)}, s32[1,1,1496]{2,1,0:T(1,128)}, u32[]{:S(2)}) copy-start(s32[1,1,1496]{2,1,0:T(1,128)} %param.26) | copy-start | bytes 17956
  20.9 10.3 %copy-start.2 = (f32[1,1,4096]{2,1,0:T(1,128)S(1)}, f32[1,1,4096]{2,1,0:T(1,128)}, u32[]{:S(2)}) copy-start(f32[1,1,4096]{2,1,0:T(1,128)} %param.21) | copy-start | bytes 49156
  35.7 1.9 %copy-start.9 = (f32[8]{0:T(128)S(1)}, f32[8]{0:T(128)}, u32[]{:S(2)}) copy-start(f32[8]{0:T(128)} %pad.23.clone) | copy-start | bytes 100
  38.6 18.9 %copy-start = (f32[4096]{0:T(1024)S(1)}, f32[4096]{0:T(1024)}, u32[]{:S(2)}) copy-start(f32[4096]{0:T(1024)} %get-tuple-element.57) | copy-start | bytes 49156
  38.6 18.9 %copy-start.1 = (f32[4096]{0:T(1024)S(1)}, f32[4096]{0:T(1024)}, u32[]{:S(2)}) copy-start(f32[4096]{0:T(1024)} %get-tuple-element.58) | copy-start | bytes 49156
  38.6 98.3 %copy-start.3 = (f32[1,64,64]{2,0,1:T(1,128)S(1)}, f32[1,64,64]{2,0,1:T(1,128)}, u32[]{:S(2)}) copy-start(f32[1,64,64]{2,0,1:T(1,128)} %stack.32) | copy-start | bytes 49156
  38.6 99.2 %copy-start.8 = (pred[4,16]{1,0:T(4,128)(4,1)S(1)}, pred[4,16]{1,0:T(4,128)(4,1)}, u32[]{:S(2)}) copy-start(pred[4,16]{1,0:T(4,128)(4,1)} %broadcast_in_dim.38) | copy-start | bytes 196
  57.4 92.4 %copy-start.4 = (f32[1,1,4096]{2,1,0:T(1,128)S(1)}, f32[1,1,4096]{2,1,0:T(1,128)}, u32[]{:S(2)}) copy-start(f32[1,1,4096]{2,1,0:T(1,128)} %param.22) | copy-start | bytes 49156
  138.6 9.2 %all-to-all-start = ((f32[4,1,2048]{2,1,0:T(1,128)}), f32[4,1,2048]{2,1,0:T(1,128)S(1)}, u32[]{:S(2)}, u32[]{:S(2)}) async-start(f32[4,1,2048]{2,1,0:T(1,128)} %reshape.354), calls=%async_computation | async-start | bytes 65536 | tf_op jit(solution)/shard_map/all_to_all | solution.py:203

commit v2 on v1

--- a/solution.py
+++ b/solution.py
@@ -182,35 +182,34 @@
     aux_field = totals[0].reshape(atom_count)
     resid_field = totals[1].reshape(atom_count)
     field = negativity + aux_field + resid_field
-    global_sums = lax.psum(
-        (jnp.sum(charge_row), jnp.sum(field / hardness_row), jnp.sum(1.0 / hardness_row)),
-        ("brick", "plane"),
-    )
+    planes = lax.axis_size("plane")
+    devices = lax.axis_size("brick") * planes
+    target = owner_tile.reshape(tile_count)
+    placer = (
+        target[:, None] == jnp.arange(planes * tile_count, dtype=jnp.int32)[None, :]
+    ).astype(jnp.float32)
+
+    def to_owners(rows):
+        tiles = rows.reshape(rows.shape[0], tile_count, TILE)
+        spread = jnp.einsum("tv,ctj->cvj", placer, tiles, precision=lax.Precision.HIGHEST)
+        spread = spread.reshape(rows.shape[0], planes, tile_count, TILE)
+        arrived = lax.all_to_all(spread, "plane", split_axis=1, concat_axis=1, tiled=True)
+        return jnp.sum(arrived, axis=1)
+
+    early = to_owners(jnp.stack([charge_row, hardness_row]))
+    local_sums = jnp.stack(
+        [jnp.sum(charge_row), jnp.sum(field / hardness_row), jnp.sum(1.0 / hardness_row)]
+    )
+    sums_out = jnp.broadcast_to(jnp.pad(local_sums, (0, 5))[None, :], (devices, 8))
+    sums_in = lax.all_to_all(sums_out, ("brick", "plane"), split_axis=0, concat_axis=0, tiled=True)
+    late = to_owners(field[None])
+    global_sums = jnp.sum(sums_in, axis=0)
     potential_level = (global_sums[0] + global_sums[1]) / global_sums[2]
     charges = (potential_level - field) / hardness_row
-    stacked = jnp.stack([charge_row, charges]).reshape(2, tile_count, TILE)
-    target = owner_tile.reshape(tile_count)
-    planes = lax.axis_size("plane")
-    quarter = tile_count // planes
-    ranking = jnp.argsort(
-        target // tile_count * tile_count + jnp.arange(tile_count, dtype=jnp.int32)
-    )
-    outgoing = jnp.take(stacked, ranking, axis=1).reshape(2, planes, quarter, TILE)
-    slot_rows = (
-        jnp.take(target % tile_count, ranking).astype(jnp.float32).reshape(1, planes, quarter)
-    )
-    arrived, arrived_slots = (
-        lax.all_to_all(outgoing, "plane", split_axis=1, concat_axis=1, tiled=True),
-        lax.all_to_all(slot_rows, "plane", split_axis=1, concat_axis=1, tiled=True),
-    )
-    arrived = arrived.reshape(2, tile_count, TILE)
-    slot_ids = arrived_slots.reshape(tile_count).astype(jnp.int32)
-    placer = (slot_ids[None, :] == jnp.arange(tile_count, dtype=jnp.int32)[:, None]).astype(
-        jnp.float32
-    )
-    placed = jnp.einsum("sk,ckj->csj", placer, arrived, precision=lax.Precision.HIGHEST)
+    placed_aux = early[0]
+    placed_charges = (potential_level - late[0]) / early[1]
     previous = aux_prev.reshape(tile_count, TILE)
-    next_aux = 2.0 * placed[0] - previous + kappa * (placed[1] - placed[0])
+    next_aux = 2.0 * placed_aux - previous + kappa * (placed_charges - placed_aux)
     return (charges.reshape(aux.shape), next_aux.reshape(aux.shape), resid_field.reshape(aux.shape))
 
 

time: 151 us -> 125 us (0.83)
  blocking collectives: 76.1 us -> 0 us
  starting transfers between devices: 15 us -> 57.5 us
  waiting for transfers between devices: 4.91 us -> 13.3 us
  Pallas kernels: 18.8 us -> 14.7 us
  local copies, waits for them, and re-layouts: 16.4 us -> 19.5 us
    psum x1 -> x0, blocking collectives: 76.1 us -> none  [on_device(): lax.psum((jnp.sum(charge_row), jnp.sum(field / hardness_row), jnp.sum(1.0...]
    all_to_all x2 -> x3, starting transfers between devices: 7.31 us -> 49.8 us  [the longest x1 43.2 us: on_device(): lax.all_to_all(sums_out, ('brick', 'plane'), split_axis=0, concat_axis=0,...]
    all_to_all x2 -> x3, waiting for transfers between devices: 4.9 us -> 13.3 us  [the longest x2 7.3 us: to_owners(): lax.all_to_all(spread, 'plane', split_axis=1, concat_axis=1, tiled=True)]
    pallas_call x1, Pallas kernels: 18.8 us -> 14.7 us  [sweep(): pl.pallas_call(sweep_kernel, out_shape=jax.ShapeDtypeStruct((2, atom_coun...]
    unnamed x29 -> x31, local copies, waits for them, and re-layouts: 2.29 us -> 6.06 us
    sort x1 -> x0, other arithmetic: 2.04 us -> none  [on_device(): jnp.argsort(target // tile_count * tile_count + jnp.arange(tile_count, dt...]
    another operation x3, other arithmetic: 0.72 us -> 2.58 us  [the longest x1 1.94 us: on_device(): jnp.stack([jnp.sum(charge_row), jnp.sum(field / hardness_row), jnp.sum(1....]
    gather x2 -> x0, local copies, waits for them, and re-layouts: 1.56 us -> none  [the longest x1 0.78 us: on_device(): jnp.take(stacked, ranking, axis=1).reshape(2, planes, quarter, TILE)]
  transfers between devices with their start and end apart: 6 -> 7, of which waited for: 1 -> 3; matrix products, arithmetic and copies ran while one was open for 16% -> 16% of each run, Pallas kernels for 12% -> 0%
where the time goes in v2:
time: 125 us; the launch traced here: 124 us
  starting transfers between devices  57.5 us (46%)
  local copies, waits for them, and re-layouts  19.5 us (16%)
  Pallas kernels  14.7 us (12%)
  waiting for transfers between devices  13.3 us (11%)
  other arithmetic  13 us (10%)
  between operations  5.07 us (4%)
    all_to_all x1, starting transfers between devices, on_device(): lax.all_to_all(sums_out, ('brick', 'plane'), split_axis=0, concat_axis=0,...  43.2 us
    pallas_call x1, Pallas kernels, sweep(): pl.pallas_call(sweep_kernel, out_shape=jax.ShapeDtypeStruct((2, atom_coun...  14.7 us
    ppermute x4, starting transfers between devices, shifted_from(): return lax.ppermute(block, axis, pairs)  7.72 us
    all_to_all x2, waiting for transfers between devices, to_owners(): lax.all_to_all(spread, 'plane', split_axis=1, concat_axis=1, tiled=True)  7.3 us
    all_to_all x2, starting transfers between devices, to_owners(): lax.all_to_all(spread, 'plane', split_axis=1, concat_axis=1, tiled=True)  6.61 us
    unnamed x31, local copies, waits for them, and re-layouts  6.06 us
    all_to_all x1, waiting for transfers between devices, on_device(): lax.all_to_all(sums_out, ('brick', 'plane'), split_axis=0, concat_axis=0,...  5.95 us
    another operation x5, local copies, waits for them, and re-layouts  3.16 us
  transfers between devices with their start and end apart: 7, of which 3 were waited for; matrix products, arithmetic and copies ran while one was open for 16% of the time, Pallas kernels for 0%

profile of v2, /device:TPU:0, one launch (start us, length us, event | category | flops | bytes accessed | tf_op | source)
XLA Modules:
  0.0 124.2 jit_solution(10749996264999300731)
XLA Ops:
  0.6 0.8 copy.99
  1.5 0.9 select_reduce_fusion.2
  2.4 1.4 %pad_maximum_fusion.1 = f32[6,4096]{1,0:T(8,128)} fusion(f32[1,4096]{1,0:T(1,128)S(1)} %bitcast.78, f32[1,4096]{1,0:T(1,128)} %bitcast.88, f32[1,4096]{1,0:T(1,128)} %bitcast.84, f32[3,4096]{1,0:T(4,128)S(1)} %bitcast.73), kind=kLoop, calls=%fused_computation.6 | loop fusion | flops 73728 | bytes 196608 | tf_op jit(solution)/shard_map/concatenate | solution.py:165
  4.3 2.9 %collective-permute-start.1 = (f32[6,4096]{1,0:T(8,128)}, f32[6,4096]{1,0:T(8,128)}, u32[]{:S(2)}, u32[]{:S(2)}) collective-permute-start(f32[6,4096]{1,0:T(8,128)} %pad_maximum_fusion.1), channel_id=1, source_target_pairs={{0,28},{4,0},{8,4},{12,8},{16,12},{20,16},{24,20},{28,24},{1,29},{... | collective-permute-start | bytes 294920 | tf_op jit(solution)/shard_map/ppermute | solution.py:23
  7.2 2.3 %collective-permute-start.2 = (f32[6,4096]{1,0:T(8,128)}, f32[6,4096]{1,0:T(8,128)}, u32[]{:S(2)}, u32[]{:S(2)}) collective-permute-start(f32[6,4096]{1,0:T(8,128)} %pad_maximum_fusion.1), channel_id=1, source_target_pairs={{0,1},{1,2},{2,3},{3,0},{4,5},{5,6},{6,7},{7,4},{8,9},{9,10},{10,1... | collective-permute-start | bytes 294920 | tf_op jit(solution)/shard_map/ppermute | solution.py:23
  9.6 2.0 %collective-permute-start.3 = (f32[6,4096]{1,0:T(8,128)}, f32[6,4096]{1,0:T(8,128)S(1)}, u32[]{:S(2)}, u32[]{:S(2)}) collective-permute-start(f32[6,4096]{1,0:T(8,128)} %pad_maximum_fusion.1), channel_id=1, source_target_pairs={{0,3},{1,0},{2,1},{3,2},{4,7},{5,4},{6,5},{7,6},{8,11},{9,8},{10,9... | collective-permute-start | bytes 294920 | tf_op jit(solution)/shard_map/ppermute | solution.py:23
  11.6 0.8 bitcast_dynamic-update-slice_fusion.4
  13.0 0.7 fusion.18
  14.2 1.9 %fusion.15 = (f32[4096]{0:T(1024)S(1)}, f32[]{:T(128)}) fusion(f32[1,1,4096]{2,1,0:T(1,128)} %param.21, f32[]{:T(128)} %broadcast.134), kind=kLoop, calls=%fused_computation.46 | loop fusion | flops 4095 | bytes 32776 | tf_op args[1]
  16.6 1.4 %scatter.14 = f32[6,5]{0,1:T(8,128)S(1)} dynamic-update-slice(f32[6,5]{0,1:T(8,128)S(1)} %broadcast.100, f32[1,1]{0,1:T(1,128)} %constant.124.clone.1, s32[]{:T(128)} %bitcast.12, s32[]{:T(128)} %bitcast.13) | dynamic-update-slice | bytes 12 | tf_op jit(solution)/shard_map/scatter | solution.py:46
  18.0 1.9 %dynamic-slice.29 = f32[1,1]{0,1:T(1,128)} dynamic-slice(f32[6,5]{0,1:T(8,128)S(1)} %scatter.14, s32[]{:T(128)} %bitcast.15, s32[]{:T(128)} %bitcast.16), dynamic_slice_sizes={1,1} | dynamic-slice | bytes 12 | tf_op jit(solution)/shard_map/dynamic-slice.17
  19.9 0.9 convolution_bitcast_fusion
  22.8 1.3 %scatter.15 = f32[6,5]{0,1:T(8,128)S(1)} dynamic-update-slice(f32[6,5]{0,1:T(8,128)S(1)} %scatter.14, f32[1,1]{0,1:T(1,128)S(6)} %select.14, s32[]{:T(128)} %bitcast.15, s32[]{:T(128)} %bitcast.16) | dynamic-update-slice | bytes 12 | tf_op jit(solution)/shard_map/scatter | solution.py:46
  26.1 0.7 reduce_sum.100
  26.9 0.8 reshape.321
  28.0 0.9 bitcast_dynamic-update-slice_fusion.3
  29.0 0.9 bitcast_dynamic-update-slice_fusion.2
  29.9 0.9 bitcast_dynamic-update-slice_fusion.1
  31.1 0.9 fusion
  33.2 1.0 square.27
  35.2 14.7 %shard_map.139 = f32[2,4096]{1,0:T(2,128)S(1)} custom-call(s32[1496]{0:T(1024)S(1)} %reduce.16.near_ref, s32[1496]{0:T(1024)S(1)} %reduce.17.far_ref, s32[1]{0:T(128)} %bitcast.70.count_ref, f32[4096,8]{1,0:T(8,128)S(1)} %bitcast.71, f32[320,8,128]{2,1,0:T(8,128)S(1)} %pad_maximum_fusion.cand_ref), custom_call_target="tpu_custom_call" | custom-call | tf_op jit(solution)/shard_map/pallas_call | solution.py:130
  50.8 1.9 %select_maximum_fusion = f32[8]{0:T(128)S(1)} fusion(f32[1]{0:T(128)} %bitcast.22, f32[1]{0:T(128)} %bitcast.21, f32[1]{0:T(128)} %bitcast), kind=kLoop, calls=%fused_computation.38 | loop fusion | flops 48 | bytes 44 | tf_op jit(solution)/shard_map/stack | solution.py:200
  53.4 43.2 %all-to-all-start = ((f32[32,1,8]{2,1,0:T(1,128)}), f32[32,1,8]{2,1,0:T(1,128)S(1)}, u32[]{:S(2)}, u32[]{:S(2)}) async-start(f32[32,1,8]{2,1,0:T(1,128)} %broadcast_in_dim.8), calls=%async_computation | async-start | bytes 32768 | tf_op jit(solution)/shard_map/all_to_all | solution.py:204
  97.0 0.7 reshape.323
  97.7 6.0 %all-to-all-done = f32[32,1,8]{2,1,0:T(1,128)S(1)} async-done(((f32[32,1,8]{2,1,0:T(1,128)}), f32[32,1,8]{2,1,0:T(1,128)S(1)}, u32[]{:S(2)}, u32[]{:S(2)}) %all-to-all-start) | async-done | bytes 1056 | tf_op jit(solution)/shard_map/all_to_all | solution.py:204
  103.7 3.3 %all-to-all-start.2 = ((f32[4,1,4096]{2,1,0:T(1,128)}), f32[4,1,4096]{2,1,0:T(1,128)S(1)}, u32[]{:S(2)}, u32[]{:S(2)}) async-start(f32[4,1,4096]{2,1,0:T(1,128)} %reshape.323), calls=%async_computation.2 | async-start | bytes 131072 | tf_op jit(solution)/shard_map/all_to_all | solution.py:196
  109.6 3.1 %all-to-all-done.2 = f32[4,1,4096]{2,1,0:T(1,128)S(1)} async-done(((f32[4,1,4096]{2,1,0:T(1,128)}), f32[4,1,4096]{2,1,0:T(1,128)S(1)}, u32[]{:S(2)}, u32[]{:S(2)}) %all-to-all-start.2) | async-done | bytes 65568 | tf_op jit(solution)/shard_map/all_to_all | solution.py:196
  112.7 3.3 %all-to-all-start.1 = ((f32[4,1,8192]{2,1,0:T(1,128)}), f32[4,1,8192]{2,1,0:T(1,128)S(1)}, u32[]{:S(2)}, u32[]{:S(2)}) async-start(f32[4,1,8192]{2,1,0:T(1,128)} %reshape.321), calls=%async_computation.1 | async-start | bytes 262144 | tf_op jit(solution)/shard_map/all_to_all | solution.py:196
  116.5 0.8 reduce.35
  117.7 4.2 %all-to-all-done.1 = f32[4,1,8192]{2,1,0:T(1,128)S(1)} async-done(((f32[4,1,8192]{2,1,0:T(1,128)}), f32[4,1,8192]{2,1,0:T(1,128)S(1)}, u32[]{:S(2)}, u32[]{:S(2)}) %all-to-all-start.1) | async-done | bytes 131104 | tf_op jit(solution)/shard_map/all_to_all | solution.py:196
  121.9 1.0 reduce.34
  123.5 0.7 fusion.12
  (85 shorter events, 10.7 us)
Async XLA Ops:
  0.6 20.2 %copy-start.10 = (s32[2]{0:T(128)S(1)}, s32[2]{0:T(128)}, u32[]{:S(2)}) copy-start(s32[2]{0:T(128)} %constant.127.clone.1) | copy-start | bytes 28
  2.4 22.9 %copy-start.2 = (f32[4096]{0:T(1024)}, f32[4096]{0:T(1024)S(1)}, u32[]{:S(2)}) copy-start(f32[4096]{0:T(1024)S(1)} %get-tuple-element.58) | copy-start | bytes 49156
  2.4 23.7 %copy-start = (f32[4096]{0:T(1024)}, f32[4096]{0:T(1024)S(1)}, u32[]{:S(2)}) copy-start(f32[4096]{0:T(1024)S(1)} %get-tuple-element.57) | copy-start | bytes 49156
  3.9 24.2 %collective-permute-start = (f32[6,4096]{1,0:T(8,128)}, f32[6,4096]{1,0:T(8,128)}, u32[]{:S(2)}, u32[]{:S(2)}) collective-permute-start(f32[6,4096]{1,0:T(8,128)} %pad_maximum_fusion.1), channel_id=1, source_target_pairs={{0,4},{4,8},{8,12},{12,16},{16,20},{20,24},{24,28},{28,0},{1,5},{5... | collective-permute-start | bytes 294920 | tf_op jit(solution)/shard_map/ppermute | solution.py:23
  4.3 24.6 %collective-permute-start.1 = (f32[6,4096]{1,0:T(8,128)}, f32[6,4096]{1,0:T(8,128)}, u32[]{:S(2)}, u32[]{:S(2)}) collective-permute-start(f32[6,4096]{1,0:T(8,128)} %pad_maximum_fusion.1), channel_id=1, source_target_pairs={{0,28},{4,0},{8,4},{12,8},{16,12},{20,16},{24,20},{28,24},{1,29},{... | collective-permute-start | bytes 294920 | tf_op jit(solution)/shard_map/ppermute | solution.py:23
  7.2 22.7 %collective-permute-start.2 = (f32[6,4096]{1,0:T(8,128)}, f32[6,4096]{1,0:T(8,128)}, u32[]{:S(2)}, u32[]{:S(2)}) collective-permute-start(f32[6,4096]{1,0:T(8,128)} %pad_maximum_fusion.1), channel_id=1, source_target_pairs={{0,1},{1,2},{2,3},{3,0},{4,5},{5,6},{6,7},{7,4},{8,9},{9,10},{10,1... | collective-permute-start | bytes 294920 | tf_op jit(solution)/shard_map/ppermute | solution.py:23
  9.6 21.3 %collective-permute-start.3 = (f32[6,4096]{1,0:T(8,128)}, f32[6,4096]{1,0:T(8,128)S(1)}, u32[]{:S(2)}, u32[]{:S(2)}) collective-permute-start(f32[6,4096]{1,0:T(8,128)} %pad_maximum_fusion.1), channel_id=1, source_target_pairs={{0,3},{1,0},{2,1},{3,2},{4,7},{5,4},{6,5},{7,6},{8,11},{9,8},{10,9... | collective-permute-start | bytes 294920 | tf_op jit(solution)/shard_map/ppermute | solution.py:23
  16.5 8.8 %copy-start.6 = (s32[1,1,1496]{2,1,0:T(1,128)S(1)}, s32[1,1,1496]{2,1,0:T(1,128)}, u32[]{:S(2)}) copy-start(s32[1,1,1496]{2,1,0:T(1,128)} %param.25) | copy-start | bytes 17956
  16.5 8.8 %copy-start.7 = (s32[1,1,1496]{2,1,0:T(1,128)S(1)}, s32[1,1,1496]{2,1,0:T(1,128)}, u32[]{:S(2)}) copy-start(s32[1,1,1496]{2,1,0:T(1,128)} %param.26) | copy-start | bytes 17956
  32.3 1.9 %copy-start.9 = (f32[8]{0:T(128)S(1)}, f32[8]{0:T(128)}, u32[]{:S(2)}) copy-start(f32[8]{0:T(128)} %pad.31.clone) | copy-start | bytes 100
  35.2 15.0 %copy-start.1 = (f32[4096]{0:T(1024)S(1)}, f32[4096]{0:T(1024)}, u32[]{:S(2)}) copy-start(f32[4096]{0:T(1024)} %copy-done) | copy-start | bytes 49156
  35.2 15.0 %copy-start.3 = (f32[4096]{0:T(1024)S(1)}, f32[4096]{0:T(1024)}, u32[]{:S(2)}) copy-start(f32[4096]{0:T(1024)} %copy-done.2) | copy-start | bytes 49156
  35.2 61.4 %copy-start.4 = (f32[64,64]{1,0:T(8,128)S(1)}, f32[64,64]{1,0:T(8,128)}, u32[]{:S(2)}) copy-start(f32[64,64]{1,0:T(8,128)} %reduce_sum.100) | copy-start | bytes 49156
  35.2 61.4 %copy-start.8 = (s32[1,1,64]{2,1,0:T(1,128)S(1)}, s32[1,1,64]{2,1,0:T(1,128)}, u32[]{:S(2)}) copy-start(s32[1,1,64]{2,1,0:T(1,128)} %param.28) | copy-start | bytes 772
  53.4 50.3 %all-to-all-start = ((f32[32,1,8]{2,1,0:T(1,128)}), f32[32,1,8]{2,1,0:T(1,128)S(1)}, u32[]{:S(2)}, u32[]{:S(2)}) async-start(f32[32,1,8]{2,1,0:T(1,128)} %broadcast_in_dim.8), calls=%async_computation | async-start | bytes 32768 | tf_op jit(solution)/shard_map/all_to_all | solution.py:204
  97.0 26.5 %copy-start.5 = (f32[1,1,4096]{2,1,0:T(1,128)S(1)}, f32[1,1,4096]{2,1,0:T(1,128)}, u32[]{:S(2)}) copy-start(f32[1,1,4096]{2,1,0:T(1,128)} %param.22) | copy-start | bytes 49156
  103.7 9.0 %all-to-all-start.2 = ((f32[4,1,4096]{2,1,0:T(1,128)}), f32[4,1,4096]{2,1,0:T(1,128)S(1)}, u32[]{:S(2)}, u32[]{:S(2)}) async-start(f32[4,1,4096]{2,1,0:T(1,128)} %reshape.323), calls=%async_computation.2 | async-start | bytes 131072 | tf_op jit(solution)/shard_map/all_to_all | solution.py:196
  112.7 9.2 %all-to-all-start.1 = ((f32[4,1,8192]{2,1,0:T(1,128)}), f32[4,1,8192]{2,1,0:T(1,128)S(1)}, u32[]{:S(2)}, u32[]{:S(2)}) async-start(f32[4,1,8192]{2,1,0:T(1,128)} %reshape.321), calls=%async_computation.1 | async-start | bytes 262144 | tf_op jit(solution)/shard_map/all_to_all | solution.py:196

commit v3 on v2

--- a/solution.py
+++ b/solution.py
@@ -1,3 +1,4 @@
+import numpy as np
 import jax
 import jax.numpy as jnp
 from jax import lax
@@ -42,10 +43,12 @@
 
 def candidates(blocks, tile_count):
     joined = jnp.stack(blocks, axis=1)
-    offsets = jnp.zeros((6, 5), jnp.float32)
-    offsets = offsets.at[0, 1].set(-TX * cell_edge).at[0, 2].set(TX * cell_edge)
-    offsets = offsets.at[1, 3].set(-TY * cell_edge).at[1, 4].set(TY * cell_edge)
-    joined = joined + offsets[:, :, None]
+    offsets = np.zeros((6, 5, 1), np.float32)
+    offsets[0, 1] = -TX * cell_edge
+    offsets[0, 2] = TX * cell_edge
+    offsets[1, 3] = -TY * cell_edge
+    offsets[1, 4] = TY * cell_edge
+    joined = joined + offsets
     return joined.reshape(6, 5 * tile_count, TILE)
 
 
@@ -196,18 +199,17 @@
         arrived = lax.all_to_all(spread, "plane", split_axis=1, concat_axis=1, tiled=True)
         return jnp.sum(arrived, axis=1)
 
-    early = to_owners(jnp.stack([charge_row, hardness_row]))
     local_sums = jnp.stack(
         [jnp.sum(charge_row), jnp.sum(field / hardness_row), jnp.sum(1.0 / hardness_row)]
     )
     sums_out = jnp.broadcast_to(jnp.pad(local_sums, (0, 5))[None, :], (devices, 8))
     sums_in = lax.all_to_all(sums_out, ("brick", "plane"), split_axis=0, concat_axis=0, tiled=True)
-    late = to_owners(field[None])
+    placed = to_owners(jnp.stack([charge_row, hardness_row, field]))
     global_sums = jnp.sum(sums_in, axis=0)
     potential_level = (global_sums[0] + global_sums[1]) / global_sums[2]
     charges = (potential_level - field) / hardness_row
-    placed_aux = early[0]
-    placed_charges = (potential_level - late[0]) / early[1]
+    placed_aux = placed[0]
+    placed_charges = (potential_level - placed[2]) / placed[1]
     previous = aux_prev.reshape(tile_count, TILE)
     next_aux = 2.0 * placed_aux - previous + kappa * (placed_charges - placed_aux)
     return (charges.reshape(aux.shape), next_aux.reshape(aux.shape), resid_field.reshape(aux.shape))

time: 125 us -> 106 us (0.85)
  local copies, waits for them, and re-layouts: 19.5 us -> 10.2 us
  starting transfers between devices: 57.5 us -> 50.2 us
  Pallas kernels: 14.7 us -> 18.8 us
  waiting for transfers between devices: 13.3 us -> 10.7 us
  between operations: 5.07 us -> 3.69 us
    pallas_call x1, Pallas kernels: 14.7 us -> 18.8 us  [sweep(): pl.pallas_call(sweep_kernel, out_shape=jax.ShapeDtypeStruct((2, atom_coun...]
    all_to_all x1, starting transfers between devices: 43.2 us -> 39.1 us  [on_device(): lax.all_to_all(sums_out, ('brick', 'plane'), split_axis=0, concat_axis=0,...]
    unnamed x31, local copies, waits for them, and re-layouts: 6.06 us -> 2.61 us
    all_to_all x2 -> x1, starting transfers between devices: 6.61 us -> 3.36 us  [to_owners(): lax.all_to_all(spread, 'plane', split_axis=1, concat_axis=1, tiled=True)]
    scatter x4 -> x0, local copies, waits for them, and re-layouts: 2.93 us -> none  [the longest x2 2.68 us: candidates(): offsets = offsets.at[0, 1].set(-TX * cell_edge).at[0, 2].set(TX * cell_edge)]
    all_to_all x2 -> x1, waiting for transfers between devices: 7.3 us -> 5.05 us  [to_owners(): lax.all_to_all(spread, 'plane', split_axis=1, concat_axis=1, tiled=True)]
    another operation x9 -> x6, local copies, waits for them, and re-layouts: 3.46 us -> 1.67 us  [on_device(): placed = to_owners(jnp.stack([charge_row, hardness_row, field]))]
  transfers between devices with their start and end apart: 7 -> 6, of which waited for: 3 -> 2; matrix products, arithmetic and copies ran while one was open for 16% -> 7% of each run, Pallas kernels for 0% -> 0%
where the time goes in v3:
time: 106 us
  starting transfers between devices  50.2 us (47%)
  Pallas kernels  18.8 us (18%)
  other arithmetic  11.8 us (11%)
  waiting for transfers between devices  10.7 us (10%)
  local copies, waits for them, and re-layouts  10.2 us (10%)
  between operations  3.69 us (3%)
    all_to_all x1, starting transfers between devices, on_device(): lax.all_to_all(sums_out, ('brick', 'plane'), split_axis=0, concat_axis=0,...  39.1 us
    pallas_call x1, Pallas kernels, sweep(): pl.pallas_call(sweep_kernel, out_shape=jax.ShapeDtypeStruct((2, atom_coun...  18.8 us
    ppermute x4, starting transfers between devices, shifted_from(): return lax.ppermute(block, axis, pairs)  7.72 us
    all_to_all x1, waiting for transfers between devices, on_device(): lax.all_to_all(sums_out, ('brick', 'plane'), split_axis=0, concat_axis=0,...  5.64 us
    all_to_all x1, waiting for transfers between devices, to_owners(): lax.all_to_all(spread, 'plane', split_axis=1, concat_axis=1, tiled=True)  5.05 us
    all_to_all x1, starting transfers between devices, to_owners(): lax.all_to_all(spread, 'plane', split_axis=1, concat_axis=1, tiled=True)  3.36 us
    unnamed x31, local copies, waits for them, and re-layouts  2.61 us
    unnamed x4, other arithmetic  2.14 us
  transfers between devices with their start and end apart: 6, of which 2 were waited for; matrix products, arithmetic and copies ran while one was open for 7% of the time, Pallas kernels for 0%

profile of v3, /device:TPU:0, one launch (start us, length us, event | category | flops | bytes accessed | tf_op | source)
XLA Modules:
  0.0 105.7 jit_solution(17395335669192006911)
XLA Ops:
  0.6 0.8 copy.94
  1.5 1.5 %select_reduce_fusion.2 = (f32[4096]{0:T(1024)}, f32[4096]{0:T(1024)S(1)}, f32[4096]{0:T(1024)S(1)}) fusion(f32[8]{0:T(128)} %param.22, s32[4096]{0:T(1024)} %bitcast.75, f32[8]{0:T(128)} %param.23, f32[8]{0:T(128)} %param.24), kind=kLoop, calls=%fused_computation.13 | loop fusion | flops 217088 | bytes 65632 | tf_op jit(solution)/shard_map/reduce_sum | solution.py:41
  3.0 1.4 %pad_maximum_fusion.1 = f32[6,4096]{1,0:T(8,128)} fusion(f32[1,4096]{1,0:T(1,128)S(1)} %bitcast.62, f32[1,4096]{1,0:T(1,128)} %bitcast.73, f32[1,4096]{1,0:T(1,128)} %bitcast.69, f32[3,4096]{1,0:T(4,128)S(1)} %bitcast.58), kind=kLoop, calls=%fused_computation.5 | loop fusion | flops 73728 | bytes 196608 | tf_op jit(solution)/shard_map/concatenate | solution.py:168
  4.4 0.5 collective-permute-start
  4.9 2.9 %collective-permute-start.1 = (f32[6,4096]{1,0:T(8,128)}, f32[6,4096]{1,0:T(8,128)S(1)}, u32[]{:S(2)}, u32[]{:S(2)}) collective-permute-start(f32[6,4096]{1,0:T(8,128)} %pad_maximum_fusion.1), channel_id=1, source_target_pairs={{0,28},{4,0},{8,4},{12,8},{16,12},{20,16},{24,20},{28,24},{1,29},{... | collective-permute-start | bytes 294920 | tf_op jit(solution)/shard_map/ppermute | solution.py:24
  7.8 2.3 %collective-permute-start.2 = (f32[6,4096]{1,0:T(8,128)}, f32[6,4096]{1,0:T(8,128)S(1)}, u32[]{:S(2)}, u32[]{:S(2)}) collective-permute-start(f32[6,4096]{1,0:T(8,128)} %pad_maximum_fusion.1), channel_id=1, source_target_pairs={{0,1},{1,2},{2,3},{3,0},{4,5},{5,6},{6,7},{7,4},{8,9},{9,10},{10,1... | collective-permute-start | bytes 294920 | tf_op jit(solution)/shard_map/ppermute | solution.py:24
  10.1 2.0 %collective-permute-start.3 = (f32[6,4096]{1,0:T(8,128)}, f32[6,4096]{1,0:T(8,128)S(1)}, u32[]{:S(2)}, u32[]{:S(2)}) collective-permute-start(f32[6,4096]{1,0:T(8,128)} %pad_maximum_fusion.1), channel_id=1, source_target_pairs={{0,3},{1,0},{2,1},{3,2},{4,7},{5,4},{6,5},{7,6},{8,11},{9,8},{10,9... | collective-permute-start | bytes 294920 | tf_op jit(solution)/shard_map/ppermute | solution.py:24
  12.1 0.8 bitcast_dynamic-update-slice_fusion.4
  13.0 0.6 pad.16.clone
  13.8 0.6 copy.69
  15.3 0.7 copy.77
  15.9 0.5 broadcast.72
  16.5 1.3 %fusion.16 = (f32[4096]{0:T(1024)S(1)}, f32[]{:T(128)}) fusion(f32[1,1,4096]{2,1,0:T(1,128)S(1)} %copy-done.3, f32[]{:T(128)} %broadcast.72), kind=kLoop, calls=%fused_computation.45 | loop fusion | flops 4095 | bytes 32776 | tf_op args[1]
  17.8 0.7 copy.76
  18.9 0.9 fusion.5
  20.2 0.3 copy.72
  21.0 1.0 square.27
  22.0 0.6 maximum_bitcast_fusion
  22.6 0.4 pad_maximum_fusion.cand_ref
  23.1 18.8 %shard_map.148 = f32[2,4096]{1,0:T(2,128)S(1)} custom-call(s32[1496]{0:T(1024)S(1)} %reduce.2.near_ref, s32[1496]{0:T(1024)S(1)} %reduce.3.far_ref, s32[1]{0:T(128)} %bitcast.55.count_ref, f32[4096,8]{1,0:T(8,128)S(1)} %bitcast.56, f32[320,8,128]{2,1,0:T(8,128)S(1)} %pad_maximum_fusion.cand_ref), custom_call_target="tpu_custom_call" | custom-call | tf_op jit(solution)/shard_map/pallas_call | solution.py:133
  42.1 0.6 fusion.14
  42.7 2.0 %select_maximum_fusion = f32[8]{0:T(128)S(1)} fusion(f32[1]{0:T(128)} %bitcast.17, f32[1]{0:T(128)} %bitcast.16, f32[1]{0:T(128)} %bitcast), kind=kLoop, calls=%fused_computation.40 | loop fusion | flops 48 | bytes 44 | tf_op jit(solution)/shard_map/stack | solution.py:202
  44.7 0.6 broadcast_in_dim.8
  45.3 39.1 %all-to-all-start = ((f32[32,1,8]{2,1,0:T(1,128)}), f32[32,1,8]{2,1,0:T(1,128)S(1)}, u32[]{:S(2)}, u32[]{:S(2)}) async-start(f32[32,1,8]{2,1,0:T(1,128)} %broadcast_in_dim.8), calls=%async_computation | async-start | bytes 32768 | tf_op jit(solution)/shard_map/all_to_all | solution.py:206
  85.0 0.9 reshape.177
  85.9 5.6 %all-to-all-done = f32[32,1,8]{2,1,0:T(1,128)S(1)} async-done(((f32[32,1,8]{2,1,0:T(1,128)}), f32[32,1,8]{2,1,0:T(1,128)S(1)}, u32[]{:S(2)}, u32[]{:S(2)}) %all-to-all-start) | async-done | bytes 1056 | tf_op jit(solution)/shard_map/all_to_all | solution.py:206
  91.6 3.4 %all-to-all-start.1 = ((f32[4,1,12288]{2,1,0:T(1,128)}), f32[4,1,12288]{2,1,0:T(1,128)S(1)}, u32[]{:S(2)}, u32[]{:S(2)}) async-start(f32[4,1,12288]{2,1,0:T(1,128)} %reshape.177), calls=%async_computation.1 | async-start | bytes 393216 | tf_op jit(solution)/shard_map/all_to_all | solution.py:199
  95.0 0.6 fusion.17
  97.6 5.0 %all-to-all-done.1 = f32[4,1,12288]{2,1,0:T(1,128)S(1)} async-done(((f32[4,1,12288]{2,1,0:T(1,128)}), f32[4,1,12288]{2,1,0:T(1,128)S(1)}, u32[]{:S(2)}, u32[]{:S(2)}) %all-to-all-start.1) | async-done | bytes 196640 | tf_op jit(solution)/shard_map/all_to_all | solution.py:199
  102.6 0.5 broadcast.73
  103.1 1.2 %reduce.15 = f32[4,12288]{1,0:T(4,128)S(1)} reduce(f32[4,1,12288]{2,1,0:T(1,128)S(1)} %all-to-all-done.1, f32[]{:T(128)} %broadcast.73), dimensions={1}, to_apply=%all_to_all.8.reduce_sub_computation | reduce | bytes 393220 | tf_op jit(solution)/shard_map/all_to_all | solution.py:199
  105.0 0.7 fusion.13
  (63 shorter events, 3.0 us)
Async XLA Ops:
  3.0 12.2 %copy-start = (f32[4096]{0:T(1024)}, f32[4096]{0:T(1024)S(1)}, u32[]{:S(2)}) copy-start(f32[4096]{0:T(1024)S(1)} %get-tuple-element.8) | copy-start | bytes 49156
  4.4 14.1 %collective-permute-start = (f32[6,4096]{1,0:T(8,128)}, f32[6,4096]{1,0:T(8,128)S(1)}, u32[]{:S(2)}, u32[]{:S(2)}) collective-permute-start(f32[6,4096]{1,0:T(8,128)} %pad_maximum_fusion.1), channel_id=1, source_target_pairs={{0,4},{4,8},{8,12},{12,16},{16,20},{20,24},{24,28},{28,0},{1,5},{5... | collective-permute-start | bytes 294920 | tf_op jit(solution)/shard_map/ppermute | solution.py:24
  4.9 13.7 %collective-permute-start.1 = (f32[6,4096]{1,0:T(8,128)}, f32[6,4096]{1,0:T(8,128)S(1)}, u32[]{:S(2)}, u32[]{:S(2)}) collective-permute-start(f32[6,4096]{1,0:T(8,128)} %pad_maximum_fusion.1), channel_id=1, source_target_pairs={{0,28},{4,0},{8,4},{12,8},{16,12},{20,16},{24,20},{28,24},{1,29},{... | collective-permute-start | bytes 294920 | tf_op jit(solution)/shard_map/ppermute | solution.py:24
  7.8 10.8 %collective-permute-start.2 = (f32[6,4096]{1,0:T(8,128)}, f32[6,4096]{1,0:T(8,128)S(1)}, u32[]{:S(2)}, u32[]{:S(2)}) collective-permute-start(f32[6,4096]{1,0:T(8,128)} %pad_maximum_fusion.1), channel_id=1, source_target_pairs={{0,1},{1,2},{2,3},{3,0},{4,5},{5,6},{6,7},{7,4},{8,9},{9,10},{10,1... | collective-permute-start | bytes 294920 | tf_op jit(solution)/shard_map/ppermute | solution.py:24
  10.1 8.5 %collective-permute-start.3 = (f32[6,4096]{1,0:T(8,128)}, f32[6,4096]{1,0:T(8,128)S(1)}, u32[]{:S(2)}, u32[]{:S(2)}) collective-permute-start(f32[6,4096]{1,0:T(8,128)} %pad_maximum_fusion.1), channel_id=1, source_target_pairs={{0,3},{1,0},{2,1},{3,2},{4,7},{5,4},{6,5},{7,6},{8,11},{9,8},{10,9... | collective-permute-start | bytes 294920 | tf_op jit(solution)/shard_map/ppermute | solution.py:24
  12.9 1.5 %copy-start.7 = (s32[1,1,1496]{2,1,0:T(1,128)S(1)}, s32[1,1,1496]{2,1,0:T(1,128)}, u32[]{:S(2)}) copy-start(s32[1,1,1496]{2,1,0:T(1,128)} %param.18) | copy-start | bytes 17956
  13.0 1.5 %copy-start.8 = (s32[1,1,1496]{2,1,0:T(1,128)S(1)}, s32[1,1,1496]{2,1,0:T(1,128)}, u32[]{:S(2)}) copy-start(s32[1,1,1496]{2,1,0:T(1,128)} %param.19) | copy-start | bytes 17956
  13.0 3.5 %copy-start.3 = (f32[1,1,4096]{2,1,0:T(1,128)S(1)}, f32[1,1,4096]{2,1,0:T(1,128)}, u32[]{:S(2)}) copy-start(f32[1,1,4096]{2,1,0:T(1,128)} %param.14) | copy-start | bytes 49156
  13.8 4.8 %copy-start.9 = (f32[6,5]{0,1:T(8,128)S(1)}, f32[6,5]{0,1:T(8,128)}, u32[]{:S(2)}) copy-start(f32[6,5]{0,1:T(8,128)} %constant.29) | copy-start | bytes 364
  20.2 1.9 %copy-start.11 = (f32[8]{0:T(128)S(1)}, f32[8]{0:T(128)}, u32[]{:S(2)}) copy-start(f32[8]{0:T(128)} %pad.16.clone) | copy-start | bytes 100
  23.0 18.8 %copy-start.2 = (f32[4096]{0:T(1024)S(1)}, f32[4096]{0:T(1024)}, u32[]{:S(2)}) copy-start(f32[4096]{0:T(1024)} %get-tuple-element.7) | copy-start | bytes 49156
  23.0 19.0 %copy-start.1 = (f32[4096]{0:T(1024)S(1)}, f32[4096]{0:T(1024)}, u32[]{:S(2)}) copy-start(f32[4096]{0:T(1024)} %copy-done) | copy-start | bytes 49156
  23.0 61.4 %copy-start.4 = (f32[1,64,64]{1,2,0:T(8,128)S(1)}, f32[1,64,64]{1,2,0:T(8,128)}, u32[]{:S(2)}) copy-start(f32[1,64,64]{1,2,0:T(8,128)} %copy.77) | copy-start | bytes 49156
  23.0 61.4 %copy-start.5 = (f32[1,64,64]{1,2,0:T(8,128)S(1)}, f32[1,64,64]{1,2,0:T(8,128)}, u32[]{:S(2)}) copy-start(f32[1,64,64]{1,2,0:T(8,128)} %copy.76) | copy-start | bytes 49156
  23.0 61.4 %copy-start.10 = (s32[1,1,64]{2,1,0:T(1,128)S(1)}, s32[1,1,64]{2,1,0:T(1,128)}, u32[]{:S(2)}) copy-start(s32[1,1,64]{2,1,0:T(1,128)} %param.21) | copy-start | bytes 772
  45.3 46.3 %all-to-all-start = ((f32[32,1,8]{2,1,0:T(1,128)}), f32[32,1,8]{2,1,0:T(1,128)S(1)}, u32[]{:S(2)}, u32[]{:S(2)}) async-start(f32[32,1,8]{2,1,0:T(1,128)} %broadcast_in_dim.8), calls=%async_computation | async-start | bytes 32768 | tf_op jit(solution)/shard_map/all_to_all | solution.py:206
  85.0 20.0 %copy-start.6 = (f32[1,1,4096]{2,1,0:T(1,128)S(1)}, f32[1,1,4096]{2,1,0:T(1,128)}, u32[]{:S(2)}) copy-start(f32[1,1,4096]{2,1,0:T(1,128)} %param.15) | copy-start | bytes 49156
  91.6 11.1 %all-to-all-start.1 = ((f32[4,1,12288]{2,1,0:T(1,128)}), f32[4,1,12288]{2,1,0:T(1,128)S(1)}, u32[]{:S(2)}, u32[]{:S(2)}) async-start(f32[4,1,12288]{2,1,0:T(1,128)} %reshape.177), calls=%async_computation.1 | async-start | bytes 393216 | tf_op jit(solution)/shard_map/all_to_all | solution.py:199

commit v4 on v3

--- a/solution.py
+++ b/solution.py
@@ -69,16 +69,21 @@
     total = count_ref[0]
     lane = lax.broadcasted_iota(jnp.int32, (1, LANES), 1)
     left = lane < TILE
-
-    def body(k, carry):
-        first = 2 * k
+    lane_full = lax.broadcasted_iota(jnp.int32, (TILE, LANES), 1)
+    left_full = lane_full < TILE
+    right_full = jnp.logical_not(left_full)
+    diagonal = (lane_full % TILE) == lax.broadcasted_iota(jnp.int32, (TILE, LANES), 0)
+
+    def pair_kernel(first):
         second = jnp.minimum(first + 1, pair_cap - 1)
-        has_second = first + 1 < total
+        has_first = (first < total).astype(jnp.float32)
+        has_second = (first + 1 < total).astype(jnp.float32)
+        first = jnp.minimum(first, pair_cap - 1)
         home_a = jnp.clip(near_ref[first], 0, tile_count - 1)
         cand_a = jnp.clip(far_ref[first], 0, cand_tiles - 1)
         home_b = jnp.clip(near_ref[second], 0, tile_count - 1)
         cand_b = jnp.clip(far_ref[second], 0, cand_tiles - 1)
-        rows = jnp.where(left, cand_ref[cand_a], cand_ref[cand_b])
+        rows = jnp.where(left, cand_ref[cand_a] * has_first, cand_ref[cand_b] * has_second)
         base_a = pl.multiple_of(home_a * TILE, TILE)
         base_b = pl.multiple_of(home_b * TILE, TILE)
 
@@ -97,23 +102,27 @@
         inv_width = lax.rsqrt(near_q(3) + rows[3:4])
         taper = jnp.maximum(1.0 - dist_sq * (1.0 / (cutoff * cutoff)), 0.0)
         kernel = lax.erf(inv_width * spacing) * inv_spacing * (taper * taper)
-        row_id = lax.broadcasted_iota(jnp.int32, (TILE, LANES), 0)
-        lane_id = lax.broadcasted_iota(jnp.int32, (TILE, LANES), 1)
-        self_a = (cand_a == home_a).astype(jnp.int32)
-        self_b = (cand_b == home_b).astype(jnp.int32)
-        self_half = jnp.where(lane_id < TILE, self_a, self_b)
-        diagonal = (lane_id % TILE) == row_id
+        self_half = jnp.where(
+            left, (cand_a == home_a).astype(jnp.int32), (cand_b == home_b).astype(jnp.int32)
+        )
         kernel = jnp.where(diagonal & (self_half > 0), 0.0, kernel)
-        keep_b = lane >= TILE + TILE * (1 - has_second.astype(jnp.int32))
-        kernel_a = jnp.where(left, kernel, 0.0)
-        kernel_b = jnp.where(keep_b, kernel, 0.0)
+        return kernel, rows, base_a, base_b
+
+    def accumulate(kernel, rows, base_a, base_b):
         for c in range(2):
-            charge = rows[4 + c:5 + c]
-            acc_ref[c, pl.ds(base_a, TILE), :] += kernel_a * charge
-            acc_ref[c, pl.ds(base_b, TILE), :] += kernel_b * charge
+            contribution = kernel * rows[4 + c:5 + c]
+            slot_a = acc_ref.at[c, pl.ds(base_a, TILE), :]
+            pltpu.store(slot_a, slot_a[...] + contribution, mask=left_full)
+            slot_b = acc_ref.at[c, pl.ds(base_b, TILE), :]
+            pltpu.store(slot_b, slot_b[...] + contribution, mask=right_full)
+
+    def body(k, carry):
+        parts = [pair_kernel(8 * k + 2 * u) for u in range(4)]
+        for part in parts:
+            accumulate(*part)
         return carry
 
-    lax.fori_loop(0, (total + 1) // 2, body, 0)
+    lax.fori_loop(0, (total + 7) // 8, body, 0)
     ones = jnp.ones((8, LANES), jnp.float32)
     for c in range(2):
         summed = lax.dot_general(

time: 106 us -> 92.2 us (0.87)
  starting transfers between devices: 50.2 us -> 39.6 us
  Pallas kernels: 18.8 us -> 15.2 us
    all_to_all x1, starting transfers between devices: 39.1 us -> 28.5 us  [on_device(): lax.all_to_all(sums_out, ('brick', 'plane'), split_axis=0, concat_axis=0,...]
    pallas_call x1, Pallas kernels: 18.8 us -> 15.2 us  [sweep(): pl.pallas_call(sweep_kernel, out_shape=jax.ShapeDtypeStruct((2, atom_coun...]
  transfers between devices with their start and end apart: 6 -> 6, of which waited for: 2 -> 2; matrix products, arithmetic and copies ran while one was open for 7% -> 8% of each run, Pallas kernels for 0% -> 0%
where the time goes in v4:
time: 92.2 us; the launch traced here: 91.5 us
  starting transfers between devices  39.6 us (43%)
  Pallas kernels  15.2 us (16%)
  other arithmetic  11.8 us (13%)
  waiting for transfers between devices  10.7 us (12%)
  local copies, waits for them, and re-layouts  10.2 us (11%)
  between operations  3.69 us (4%)
    all_to_all x1, starting transfers between devices, on_device(): lax.all_to_all(sums_out, ('brick', 'plane'), split_axis=0, concat_axis=0,...  28.5 us
    pallas_call x1, Pallas kernels, sweep(): pl.pallas_call(sweep_kernel, out_shape=jax.ShapeDtypeStruct((2, atom_coun...  15.2 us
    ppermute x4, starting transfers between devices, shifted_from(): return lax.ppermute(block, axis, pairs)  7.72 us
    all_to_all x1, waiting for transfers between devices, on_device(): lax.all_to_all(sums_out, ('brick', 'plane'), split_axis=0, concat_axis=0,...  5.64 us
    all_to_all x1, waiting for transfers between devices, to_owners(): lax.all_to_all(spread, 'plane', split_axis=1, concat_axis=1, tiled=True)  5.05 us
    all_to_all x1, starting transfers between devices, to_owners(): lax.all_to_all(spread, 'plane', split_axis=1, concat_axis=1, tiled=True)  3.36 us
    unnamed x31, local copies, waits for them, and re-layouts  2.61 us
    unnamed x4, other arithmetic  2.14 us
  transfers between devices with their start and end apart: 6, of which 2 were waited for; matrix products, arithmetic and copies ran while one was open for 8% of the time, Pallas kernels for 0%

profile of v4, /device:TPU:0, one launch (start us, length us, event | category | flops | bytes accessed | tf_op | source)
XLA Modules:
  0.0 91.5 jit_solution(12217252203482646590)
XLA Ops:
  0.6 0.8 copy.94
  1.5 1.5 %select_reduce_fusion.2 = (f32[4096]{0:T(1024)}, f32[4096]{0:T(1024)S(1)}, f32[4096]{0:T(1024)S(1)}) fusion(f32[8]{0:T(128)} %param.22, s32[4096]{0:T(1024)} %bitcast.75, f32[8]{0:T(128)} %param.23, f32[8]{0:T(128)} %param.24), kind=kLoop, calls=%fused_computation.13 | loop fusion | flops 217088 | bytes 65632 | tf_op jit(solution)/shard_map/reduce_sum | solution.py:41
  3.0 1.4 %pad_maximum_fusion.1 = f32[6,4096]{1,0:T(8,128)} fusion(f32[1,4096]{1,0:T(1,128)S(1)} %bitcast.62, f32[1,4096]{1,0:T(1,128)} %bitcast.73, f32[1,4096]{1,0:T(1,128)} %bitcast.69, f32[3,4096]{1,0:T(4,128)S(1)} %bitcast.58), kind=kLoop, calls=%fused_computation.5 | loop fusion | flops 73728 | bytes 196608 | tf_op jit(solution)/shard_map/concatenate | solution.py:177
  4.4 0.5 collective-permute-start
  4.9 2.9 %collective-permute-start.1 = (f32[6,4096]{1,0:T(8,128)}, f32[6,4096]{1,0:T(8,128)S(1)}, u32[]{:S(2)}, u32[]{:S(2)}) collective-permute-start(f32[6,4096]{1,0:T(8,128)} %pad_maximum_fusion.1), channel_id=1, source_target_pairs={{0,28},{4,0},{8,4},{12,8},{16,12},{20,16},{24,20},{28,24},{1,29},{... | collective-permute-start | bytes 294920 | tf_op jit(solution)/shard_map/ppermute | solution.py:24
  7.8 2.3 %collective-permute-start.2 = (f32[6,4096]{1,0:T(8,128)}, f32[6,4096]{1,0:T(8,128)S(1)}, u32[]{:S(2)}, u32[]{:S(2)}) collective-permute-start(f32[6,4096]{1,0:T(8,128)} %pad_maximum_fusion.1), channel_id=1, source_target_pairs={{0,1},{1,2},{2,3},{3,0},{4,5},{5,6},{6,7},{7,4},{8,9},{9,10},{10,1... | collective-permute-start | bytes 294920 | tf_op jit(solution)/shard_map/ppermute | solution.py:24
  10.1 2.0 %collective-permute-start.3 = (f32[6,4096]{1,0:T(8,128)}, f32[6,4096]{1,0:T(8,128)S(1)}, u32[]{:S(2)}, u32[]{:S(2)}) collective-permute-start(f32[6,4096]{1,0:T(8,128)} %pad_maximum_fusion.1), channel_id=1, source_target_pairs={{0,3},{1,0},{2,1},{3,2},{4,7},{5,4},{6,5},{7,6},{8,11},{9,8},{10,9... | collective-permute-start | bytes 294920 | tf_op jit(solution)/shard_map/ppermute | solution.py:24
  12.1 0.8 bitcast_dynamic-update-slice_fusion.4
  13.0 0.6 pad.16.clone
  13.8 0.6 copy.69
  15.3 0.7 copy.77
  15.9 0.5 broadcast.72
  16.5 1.3 %fusion.16 = (f32[4096]{0:T(1024)S(1)}, f32[]{:T(128)}) fusion(f32[1,1,4096]{2,1,0:T(1,128)S(1)} %copy-done.3, f32[]{:T(128)} %broadcast.72), kind=kLoop, calls=%fused_computation.45 | loop fusion | flops 4095 | bytes 32776 | tf_op args[1]
  17.8 0.7 copy.76
  18.9 0.9 fusion.5
  20.2 0.3 copy.72
  21.0 1.0 %square.27 = f32[1,320,64]{2,1,0:T(8,128)S(1)} reshape(f32[5,4096]{1,0:T(8,128)} %fusion.5) | data formatting | bytes 163840 | tf_op jit(solution)/shard_map/square | solution.py:183
  22.0 0.6 maximum_bitcast_fusion
  22.6 0.4 pad_maximum_fusion.cand_ref
  23.1 15.2 %shard_map.148 = f32[2,4096]{1,0:T(2,128)S(1)} custom-call(s32[1496]{0:T(1024)S(1)} %reduce.2.near_ref, s32[1496]{0:T(1024)S(1)} %reduce.3.far_ref, s32[1]{0:T(128)} %bitcast.55.count_ref, f32[4096,8]{1,0:T(8,128)S(1)} %bitcast.56, f32[320,8,128]{2,1,0:T(8,128)S(1)} %pad_maximum_fusion.cand_ref), custom_call_target="tpu_custom_call" | custom-call | tf_op jit(solution)/shard_map/pallas_call | solution.py:142
  38.5 0.6 fusion.14
  39.1 2.0 %select_maximum_fusion = f32[8]{0:T(128)S(1)} fusion(f32[1]{0:T(128)} %bitcast.17, f32[1]{0:T(128)} %bitcast.16, f32[1]{0:T(128)} %bitcast), kind=kLoop, calls=%fused_computation.40 | loop fusion | flops 48 | bytes 44 | tf_op jit(solution)/shard_map/stack | solution.py:211
  41.1 0.6 broadcast_in_dim.8
  41.7 28.5 %all-to-all-start = ((f32[32,1,8]{2,1,0:T(1,128)}), f32[32,1,8]{2,1,0:T(1,128)S(1)}, u32[]{:S(2)}, u32[]{:S(2)}) async-start(f32[32,1,8]{2,1,0:T(1,128)} %broadcast_in_dim.8), calls=%async_computation | async-start | bytes 32768 | tf_op jit(solution)/shard_map/all_to_all | solution.py:215
  70.9 0.9 reshape.177
  71.8 5.6 %all-to-all-done = f32[32,1,8]{2,1,0:T(1,128)S(1)} async-done(((f32[32,1,8]{2,1,0:T(1,128)}), f32[32,1,8]{2,1,0:T(1,128)S(1)}, u32[]{:S(2)}, u32[]{:S(2)}) %all-to-all-start) | async-done | bytes 1056 | tf_op jit(solution)/shard_map/all_to_all | solution.py:215
  77.4 3.4 %all-to-all-start.1 = ((f32[4,1,12288]{2,1,0:T(1,128)}), f32[4,1,12288]{2,1,0:T(1,128)S(1)}, u32[]{:S(2)}, u32[]{:S(2)}) async-start(f32[4,1,12288]{2,1,0:T(1,128)} %reshape.177), calls=%async_computation.1 | async-start | bytes 393216 | tf_op jit(solution)/shard_map/all_to_all | solution.py:208
  80.8 0.6 fusion.17
  83.4 5.0 %all-to-all-done.1 = f32[4,1,12288]{2,1,0:T(1,128)S(1)} async-done(((f32[4,1,12288]{2,1,0:T(1,128)}), f32[4,1,12288]{2,1,0:T(1,128)S(1)}, u32[]{:S(2)}, u32[]{:S(2)}) %all-to-all-start.1) | async-done | bytes 196640 | tf_op jit(solution)/shard_map/all_to_all | solution.py:208
  88.5 0.5 broadcast.73
  89.0 1.2 %reduce.15 = f32[4,12288]{1,0:T(4,128)S(1)} reduce(f32[4,1,12288]{2,1,0:T(1,128)S(1)} %all-to-all-done.1, f32[]{:T(128)} %broadcast.73), dimensions={1}, to_apply=%all_to_all.8.reduce_sub_computation | reduce | bytes 393220 | tf_op jit(solution)/shard_map/all_to_all | solution.py:208
  90.8 0.7 fusion.13
  (63 shorter events, 3.0 us)
Async XLA Ops:
  3.0 12.2 %copy-start = (f32[4096]{0:T(1024)}, f32[4096]{0:T(1024)S(1)}, u32[]{:S(2)}) copy-start(f32[4096]{0:T(1024)S(1)} %get-tuple-element.8) | copy-start | bytes 49156
  4.4 14.1 %collective-permute-start = (f32[6,4096]{1,0:T(8,128)}, f32[6,4096]{1,0:T(8,128)S(1)}, u32[]{:S(2)}, u32[]{:S(2)}) collective-permute-start(f32[6,4096]{1,0:T(8,128)} %pad_maximum_fusion.1), channel_id=1, source_target_pairs={{0,4},{4,8},{8,12},{12,16},{16,20},{20,24},{24,28},{28,0},{1,5},{5... | collective-permute-start | bytes 294920 | tf_op jit(solution)/shard_map/ppermute | solution.py:24
  4.9 13.7 %collective-permute-start.1 = (f32[6,4096]{1,0:T(8,128)}, f32[6,4096]{1,0:T(8,128)S(1)}, u32[]{:S(2)}, u32[]{:S(2)}) collective-permute-start(f32[6,4096]{1,0:T(8,128)} %pad_maximum_fusion.1), channel_id=1, source_target_pairs={{0,28},{4,0},{8,4},{12,8},{16,12},{20,16},{24,20},{28,24},{1,29},{... | collective-permute-start | bytes 294920 | tf_op jit(solution)/shard_map/ppermute | solution.py:24
  7.8 10.8 %collective-permute-start.2 = (f32[6,4096]{1,0:T(8,128)}, f32[6,4096]{1,0:T(8,128)S(1)}, u32[]{:S(2)}, u32[]{:S(2)}) collective-permute-start(f32[6,4096]{1,0:T(8,128)} %pad_maximum_fusion.1), channel_id=1, source_target_pairs={{0,1},{1,2},{2,3},{3,0},{4,5},{5,6},{6,7},{7,4},{8,9},{9,10},{10,1... | collective-permute-start | bytes 294920 | tf_op jit(solution)/shard_map/ppermute | solution.py:24
  10.1 8.5 %collective-permute-start.3 = (f32[6,4096]{1,0:T(8,128)}, f32[6,4096]{1,0:T(8,128)S(1)}, u32[]{:S(2)}, u32[]{:S(2)}) collective-permute-start(f32[6,4096]{1,0:T(8,128)} %pad_maximum_fusion.1), channel_id=1, source_target_pairs={{0,3},{1,0},{2,1},{3,2},{4,7},{5,4},{6,5},{7,6},{8,11},{9,8},{10,9... | collective-permute-start | bytes 294920 | tf_op jit(solution)/shard_map/ppermute | solution.py:24
  12.9 1.5 %copy-start.7 = (s32[1,1,1496]{2,1,0:T(1,128)S(1)}, s32[1,1,1496]{2,1,0:T(1,128)}, u32[]{:S(2)}) copy-start(s32[1,1,1496]{2,1,0:T(1,128)} %param.18) | copy-start | bytes 17956
  13.0 1.5 %copy-start.8 = (s32[1,1,1496]{2,1,0:T(1,128)S(1)}, s32[1,1,1496]{2,1,0:T(1,128)}, u32[]{:S(2)}) copy-start(s32[1,1,1496]{2,1,0:T(1,128)} %param.19) | copy-start | bytes 17956
  13.0 3.5 %copy-start.3 = (f32[1,1,4096]{2,1,0:T(1,128)S(1)}, f32[1,1,4096]{2,1,0:T(1,128)}, u32[]{:S(2)}) copy-start(f32[1,1,4096]{2,1,0:T(1,128)} %param.14) | copy-start | bytes 49156
  13.8 4.8 %copy-start.9 = (f32[6,5]{0,1:T(8,128)S(1)}, f32[6,5]{0,1:T(8,128)}, u32[]{:S(2)}) copy-start(f32[6,5]{0,1:T(8,128)} %constant.29) | copy-start | bytes 364
  20.2 1.9 %copy-start.11 = (f32[8]{0:T(128)S(1)}, f32[8]{0:T(128)}, u32[]{:S(2)}) copy-start(f32[8]{0:T(128)} %pad.16.clone) | copy-start | bytes 100
  23.0 15.3 %copy-start.2 = (f32[4096]{0:T(1024)S(1)}, f32[4096]{0:T(1024)}, u32[]{:S(2)}) copy-start(f32[4096]{0:T(1024)} %get-tuple-element.7) | copy-start | bytes 49156
  23.0 15.5 %copy-start.1 = (f32[4096]{0:T(1024)S(1)}, f32[4096]{0:T(1024)}, u32[]{:S(2)}) copy-start(f32[4096]{0:T(1024)} %copy-done) | copy-start | bytes 49156
  23.0 47.3 %copy-start.4 = (f32[1,64,64]{1,2,0:T(8,128)S(1)}, f32[1,64,64]{1,2,0:T(8,128)}, u32[]{:S(2)}) copy-start(f32[1,64,64]{1,2,0:T(8,128)} %copy.77) | copy-start | bytes 49156
  23.0 47.3 %copy-start.5 = (f32[1,64,64]{1,2,0:T(8,128)S(1)}, f32[1,64,64]{1,2,0:T(8,128)}, u32[]{:S(2)}) copy-start(f32[1,64,64]{1,2,0:T(8,128)} %copy.76) | copy-start | bytes 49156
  23.0 47.3 %copy-start.10 = (s32[1,1,64]{2,1,0:T(1,128)S(1)}, s32[1,1,64]{2,1,0:T(1,128)}, u32[]{:S(2)}) copy-start(s32[1,1,64]{2,1,0:T(1,128)} %param.21) | copy-start | bytes 772
  41.7 35.7 %all-to-all-start = ((f32[32,1,8]{2,1,0:T(1,128)}), f32[32,1,8]{2,1,0:T(1,128)S(1)}, u32[]{:S(2)}, u32[]{:S(2)}) async-start(f32[32,1,8]{2,1,0:T(1,128)} %broadcast_in_dim.8), calls=%async_computation | async-start | bytes 32768 | tf_op jit(solution)/shard_map/all_to_all | solution.py:215
  70.9 20.0 %copy-start.6 = (f32[1,1,4096]{2,1,0:T(1,128)S(1)}, f32[1,1,4096]{2,1,0:T(1,128)}, u32[]{:S(2)}) copy-start(f32[1,1,4096]{2,1,0:T(1,128)} %param.15) | copy-start | bytes 49156
  77.4 11.1 %all-to-all-start.1 = ((f32[4,1,12288]{2,1,0:T(1,128)}), f32[4,1,12288]{2,1,0:T(1,128)S(1)}, u32[]{:S(2)}, u32[]{:S(2)}) async-start(f32[4,1,12288]{2,1,0:T(1,128)} %reshape.177), calls=%async_computation.1 | async-start | bytes 393216 | tf_op jit(solution)/shard_map/all_to_all | solution.py:208

commit v5 on v4

--- a/solution.py
+++ b/solution.py
@@ -197,16 +197,24 @@
     planes = lax.axis_size("plane")
     devices = lax.axis_size("brick") * planes
     target = owner_tile.reshape(tile_count)
-    placer = (
-        target[:, None] == jnp.arange(planes * tile_count, dtype=jnp.int32)[None, :]
-    ).astype(jnp.float32)
+    plane_index = lax.axis_index("plane")
 
     def to_owners(rows):
         tiles = rows.reshape(rows.shape[0], tile_count, TILE)
-        spread = jnp.einsum("tv,ctj->cvj", placer, tiles, precision=lax.Precision.HIGHEST)
-        spread = spread.reshape(rows.shape[0], planes, tile_count, TILE)
-        arrived = lax.all_to_all(spread, "plane", split_axis=1, concat_axis=1, tiled=True)
-        return jnp.sum(arrived, axis=1)
+        total = None
+        for step in range(planes):
+            owner = (plane_index + step) % planes
+            local_target = target - owner * tile_count
+            placer = (
+                local_target[:, None] == jnp.arange(tile_count, dtype=jnp.int32)[None, :]
+            ).astype(jnp.float32)
+            part = jnp.einsum("ts,ctj->csj", placer, tiles, precision=lax.Precision.HIGHEST)
+            if step:
+                part = lax.ppermute(
+                    part, "plane", [(i, (i + step) % planes) for i in range(planes)]
+                )
+            total = part if total is None else total + part
+        return total
 
     local_sums = jnp.stack(
         [jnp.sum(charge_row), jnp.sum(field / hardness_row), jnp.sum(1.0 / hardness_row)]

time: 92.2 us -> 87 us (0.944)
  waiting for transfers between devices: 10.7 us -> 3.31 us
  starting transfers between devices: 39.6 us -> 42.6 us
  local copies, waits for them, and re-layouts: 10.2 us -> 8.56 us
    all_to_all x1 -> x0, waiting for transfers between devices: 5.05 us -> none  [to_owners(): lax.all_to_all(spread, 'plane', split_axis=1, concat_axis=1, tiled=True)]
    ppermute x0 -> x3, starting transfers between devices: none -> 4.92 us  [to_owners(): lax.ppermute(part, 'plane', [(i, (i + step) % planes) for i in range(plan...]
    all_to_all x1 -> x0, starting transfers between devices: 3.36 us -> none  [to_owners(): lax.all_to_all(spread, 'plane', split_axis=1, concat_axis=1, tiled=True)]
    all_to_all x1, waiting for transfers between devices: 5.64 us -> 3.29 us  [on_device(): lax.all_to_all(sums_out, ('brick', 'plane'), split_axis=0, concat_axis=0,...]
    slice x4, local copies, waits for them, and re-layouts: 0.57 us -> 2.13 us  [on_device(): candidate[3:5]]
    all_to_all x1, starting transfers between devices: 28.5 us -> 30 us  [on_device(): lax.all_to_all(sums_out, ('brick', 'plane'), split_axis=0, concat_axis=0,...]
    sub x0 -> x1, other arithmetic: none -> 1.27 us  [to_owners(): local_target = target - owner * tile_count]
    another operation x6, local copies, waits for them, and re-layouts: 1.67 us -> 0.44 us  [on_device(): placed = to_owners(jnp.stack([charge_row, hardness_row, field]))]
  transfers between devices with their start and end apart: 6 -> 8, of which waited for: 2 -> 1; matrix products, arithmetic and copies ran while one was open for 8% -> 12% of each run, Pallas kernels for 0% -> 0%
where the time goes in v5:
time: 87 us; the launch traced here: 86.2 us
  starting transfers between devices  42.6 us (49%)
  Pallas kernels  15.2 us (17%)
  other arithmetic  11.8 us (14%)
  local copies, waits for them, and re-layouts  8.56 us (10%)
  between operations  3.7 us (4%)
  waiting for transfers between devices  3.31 us (4%)
  matrix products  0.99 us (1%)
    all_to_all x1, starting transfers between devices, on_device(): lax.all_to_all(sums_out, ('brick', 'plane'), split_axis=0, concat_axis=0,...  30 us
    pallas_call x1, Pallas kernels, sweep(): pl.pallas_call(sweep_kernel, out_shape=jax.ShapeDtypeStruct((2, atom_coun...  15.2 us
    ppermute x4, starting transfers between devices, shifted_from(): return lax.ppermute(block, axis, pairs)  7.72 us
    ppermute x3, starting transfers between devices, to_owners(): lax.ppermute(part, 'plane', [(i, (i + step) % planes) for i in range(plan...  4.92 us
    all_to_all x1, waiting for transfers between devices, on_device(): lax.all_to_all(sums_out, ('brick', 'plane'), split_axis=0, concat_axis=0,...  3.29 us
    slice x4, local copies, waits for them, and re-layouts, on_device(): candidate[3:5]  2.13 us
    unnamed x4, other arithmetic  2.13 us
    another operation x1, other arithmetic, on_device(): jnp.stack([jnp.sum(charge_row), jnp.sum(field / hardness_row), jnp.sum(1....  2.01 us
  transfers between devices with their start and end apart: 8, of which 1 were waited for; matrix products, arithmetic and copies ran while one was open for 12% of the time, Pallas kernels for 0%

profile of v5, /device:TPU:0, one launch (start us, length us, event | category | flops | bytes accessed | tf_op | source)
XLA Modules:
  0.0 86.2 jit_solution(18371763419476218144)
XLA Ops:
  0.6 0.8 copy.74
  1.5 0.9 %select_reduce_fusion.2 = (f32[4096]{0:T(1024)S(1)}, f32[4096]{0:T(1024)S(1)}, f32[4096]{0:T(1024)S(1)}) fusion(f32[8]{0:T(128)} %param.22, s32[4096]{0:T(1024)} %bitcast.95, f32[8]{0:T(128)} %param.23, f32[8]{0:T(128)} %param.24), kind=kLoop, calls=%fused_computation.19 | loop fusion | flops 217088 | bytes 65632 | tf_op jit(solution)/shard_map/reduce_sum | solution.py:41
  2.4 1.4 %pad_maximum_fusion.1 = f32[6,4096]{1,0:T(8,128)} fusion(f32[1,4096]{1,0:T(1,128)S(1)} %bitcast.82, f32[1,4096]{1,0:T(1,128)} %bitcast.93, f32[1,4096]{1,0:T(1,128)} %bitcast.89, f32[3,4096]{1,0:T(4,128)S(1)} %bitcast.78), kind=kLoop, calls=%fused_computation.11 | loop fusion | flops 73728 | bytes 196608 | tf_op jit(solution)/shard_map/concatenate | solution.py:177
  3.8 0.5 collective-permute-start
  4.3 2.9 %collective-permute-start.1 = (f32[6,4096]{1,0:T(8,128)}, f32[6,4096]{1,0:T(8,128)S(1)}, u32[]{:S(2)}, u32[]{:S(2)}) collective-permute-start(f32[6,4096]{1,0:T(8,128)} %pad_maximum_fusion.1), channel_id=1, source_target_pairs={{0,28},{4,0},{8,4},{12,8},{16,12},{20,16},{24,20},{28,24},{1,29},{... | collective-permute-start | bytes 294920 | tf_op jit(solution)/shard_map/ppermute | solution.py:24
  7.2 2.3 %collective-permute-start.2 = (f32[6,4096]{1,0:T(8,128)}, f32[6,4096]{1,0:T(8,128)S(1)}, u32[]{:S(2)}, u32[]{:S(2)}) collective-permute-start(f32[6,4096]{1,0:T(8,128)} %pad_maximum_fusion.1), channel_id=1, source_target_pairs={{0,1},{1,2},{2,3},{3,0},{4,5},{5,6},{6,7},{7,4},{8,9},{9,10},{10,1... | collective-permute-start | bytes 294920 | tf_op jit(solution)/shard_map/ppermute | solution.py:24
  9.5 2.0 %collective-permute-start.3 = (f32[6,4096]{1,0:T(8,128)}, f32[6,4096]{1,0:T(8,128)S(1)}, u32[]{:S(2)}, u32[]{:S(2)}) collective-permute-start(f32[6,4096]{1,0:T(8,128)} %pad_maximum_fusion.1), channel_id=1, source_target_pairs={{0,3},{1,0},{2,1},{3,2},{4,7},{5,4},{6,5},{7,6},{8,11},{9,8},{10,9... | collective-permute-start | bytes 294920 | tf_op jit(solution)/shard_map/ppermute | solution.py:24
  11.5 0.8 bitcast_dynamic-update-slice_fusion.4
  12.5 0.6 pad.16.clone
  13.2 0.6 copy.56
  14.7 1.3 %subtract_bitcast_fusion.3 = (s32[64]{0:T(128)}, s32[64]{0:T(128)}, s32[64]{0:T(128)}, s32[64]{0:T(128)}) fusion(s32[1,1,64]{2,1,0:T(1,128)} %param.21, s32[]{:T(128)S(6)} %mul.74, s32[]{:T(128)S(6)} %mul.75, s32[]{:T(128)S(6)} %mul.77, s32[]{:T(128)S(6)} %mul.76), kind=kLoop, calls=%fused_computation.57 | loop fusion | flops 256 | bytes 1296 | tf_op jit(solution)/shard_map/sub | solution.py:207
  16.0 0.5 broadcast.100
  16.5 1.3 %fusion.26 = (f32[4096]{0:T(1024)S(1)}, f32[]{:T(128)}) fusion(f32[1,1,4096]{2,1,0:T(1,128)S(1)} %copy-done, f32[]{:T(128)} %broadcast.100), kind=kLoop, calls=%fused_computation.63 | loop fusion | flops 4095 | bytes 32776 | tf_op args[1]
  18.2 0.7 slice.55
  19.0 0.9 %fusion.3 = f32[5,4096]{1,0:T(8,128)} fusion(f32[6,5,4096]{2,0,1:T(8,128)S(1)} %broadcast_add_fusion), kind=kLoop, calls=%fused_computation.23 | loop fusion | flops 20480 | bytes 163840 | tf_op jit(solution)/shard_map/square | solution.py:183
  20.2 0.3 copy.59
  20.5 1.0 %copy.58 = f32[2,5,4096]{2,1,0:T(8,128)S(1)} copy(f32[2,5,4096]{2,0,1:T(2,128)} %slice.55) | data formatting | bytes 327680 | tf_op jit(solution)/shard_map/slice | solution.py:183
  21.7 0.3 copy.61
  22.0 1.0 %square.27 = f32[1,320,64]{2,1,0:T(8,128)S(1)} reshape(f32[5,4096]{1,0:T(8,128)} %fusion.3) | data formatting | bytes 163840 | tf_op jit(solution)/shard_map/square | solution.py:183
  23.0 0.6 maximum_bitcast_fusion
  23.5 0.4 pad_maximum_fusion.cand_ref
  24.0 15.2 %shard_map.148 = f32[2,4096]{1,0:T(2,128)S(1)} custom-call(s32[1496]{0:T(1024)S(1)} %reduce.2.near_ref, s32[1496]{0:T(1024)S(1)} %reduce.3.far_ref, s32[1]{0:T(128)} %bitcast.76.count_ref, f32[4096,8]{1,0:T(8,128)S(1)} %bitcast.77, f32[320,8,128]{2,1,0:T(8,128)S(1)} %pad_maximum_fusion.cand_ref), custom_call_target="tpu_custom_call" | custom-call | tf_op jit(solution)/shard_map/pallas_call | solution.py:142
  40.0 1.2 %collective-permute-start.5 = (f32[3,64,64]{1,2,0:T(8,128)S(1)}, f32[3,64,64]{1,2,0:T(8,128)S(1)}, u32[]{:S(2)}, u32[]{:S(2)}) collective-permute-start(f32[3,64,64]{1,2,0:T(8,128)S(1)} %convolution_bitcast_fusion.1), channel_id=1, source_target_pairs={{0,2},{1,3},{2,0},{3,1},{4,6},{5,7},{6,4},{7,5},{8,10},{9,11},{10,... | collective-permute-start | bytes 147464 | tf_op jit(solution)/shard_map/ppermute | solution.py:213
  41.2 0.6 fusion.21
  41.8 2.0 %select_maximum_fusion = f32[8]{0:T(128)S(1)} fusion(f32[1]{0:T(128)} %bitcast.17, f32[1]{0:T(128)} %bitcast.16, f32[1]{0:T(128)} %bitcast), kind=kLoop, calls=%fused_computation.51 | loop fusion | flops 48 | bytes 44 | tf_op jit(solution)/shard_map/stack | solution.py:219
  43.8 0.6 broadcast_in_dim.8
  44.4 30.0 %all-to-all-start = ((f32[32,1,8]{2,1,0:T(1,128)}), f32[32,1,8]{2,1,0:T(1,128)S(1)}, u32[]{:S(2)}, u32[]{:S(2)}) async-start(f32[32,1,8]{2,1,0:T(1,128)} %broadcast_in_dim.8), calls=%async_computation | async-start | bytes 32768 | tf_op jit(solution)/shard_map/all_to_all | solution.py:223
  74.7 3.7 %collective-permute-start.6 = (f32[3,64,64]{1,2,0:T(8,128)S(1)}, f32[3,64,64]{1,2,0:T(8,128)S(1)}, u32[]{:S(2)}, u32[]{:S(2)}) collective-permute-start(f32[3,64,64]{1,2,0:T(8,128)S(1)} %convolution_bitcast_fusion), channel_id=1, source_target_pairs={{0,3},{1,0},{2,1},{3,2},{4,7},{5,4},{6,5},{7,6},{8,11},{9,8},{10,9... | collective-permute-start | bytes 147464 | tf_op jit(solution)/shard_map/ppermute | solution.py:213
  78.4 3.3 %all-to-all-done = f32[32,1,8]{2,1,0:T(1,128)S(1)} async-done(((f32[32,1,8]{2,1,0:T(1,128)}), f32[32,1,8]{2,1,0:T(1,128)S(1)}, u32[]{:S(2)}, u32[]{:S(2)}) %all-to-all-start) | async-done | bytes 1056 | tf_op jit(solution)/shard_map/all_to_all | solution.py:223
  81.7 0.6 fusion.27
  84.3 0.6 fusion.16
  85.6 0.6 subtract_add_fusion
  (61 shorter events, 2.9 us)
Async XLA Ops:
  3.8 14.1 %collective-permute-start = (f32[6,4096]{1,0:T(8,128)}, f32[6,4096]{1,0:T(8,128)S(1)}, u32[]{:S(2)}, u32[]{:S(2)}) collective-permute-start(f32[6,4096]{1,0:T(8,128)} %pad_maximum_fusion.1), channel_id=1, source_target_pairs={{0,4},{4,8},{8,12},{12,16},{16,20},{20,24},{24,28},{28,0},{1,5},{5... | collective-permute-start | bytes 294920 | tf_op jit(solution)/shard_map/ppermute | solution.py:24
  4.3 13.6 %collective-permute-start.1 = (f32[6,4096]{1,0:T(8,128)}, f32[6,4096]{1,0:T(8,128)S(1)}, u32[]{:S(2)}, u32[]{:S(2)}) collective-permute-start(f32[6,4096]{1,0:T(8,128)} %pad_maximum_fusion.1), channel_id=1, source_target_pairs={{0,28},{4,0},{8,4},{12,8},{16,12},{20,16},{24,20},{28,24},{1,29},{... | collective-permute-start | bytes 294920 | tf_op jit(solution)/shard_map/ppermute | solution.py:24
  7.2 10.8 %collective-permute-start.2 = (f32[6,4096]{1,0:T(8,128)}, f32[6,4096]{1,0:T(8,128)S(1)}, u32[]{:S(2)}, u32[]{:S(2)}) collective-permute-start(f32[6,4096]{1,0:T(8,128)} %pad_maximum_fusion.1), channel_id=1, source_target_pairs={{0,1},{1,2},{2,3},{3,0},{4,5},{5,6},{6,7},{7,4},{8,9},{9,10},{10,1... | collective-permute-start | bytes 294920 | tf_op jit(solution)/shard_map/ppermute | solution.py:24
  9.5 8.5 %collective-permute-start.3 = (f32[6,4096]{1,0:T(8,128)}, f32[6,4096]{1,0:T(8,128)S(1)}, u32[]{:S(2)}, u32[]{:S(2)}) collective-permute-start(f32[6,4096]{1,0:T(8,128)} %pad_maximum_fusion.1), channel_id=1, source_target_pairs={{0,3},{1,0},{2,1},{3,2},{4,7},{5,4},{6,5},{7,6},{8,11},{9,8},{10,9... | collective-permute-start | bytes 294920 | tf_op jit(solution)/shard_map/ppermute | solution.py:24
  12.3 1.5 %copy-start.2 = (s32[1,1,1496]{2,1,0:T(1,128)S(1)}, s32[1,1,1496]{2,1,0:T(1,128)}, u32[]{:S(2)}) copy-start(s32[1,1,1496]{2,1,0:T(1,128)} %param.18) | copy-start | bytes 17956
  12.4 1.5 %copy-start.3 = (s32[1,1,1496]{2,1,0:T(1,128)S(1)}, s32[1,1,1496]{2,1,0:T(1,128)}, u32[]{:S(2)}) copy-start(s32[1,1,1496]{2,1,0:T(1,128)} %param.19) | copy-start | bytes 17956
  12.4 4.1 %copy-start = (f32[1,1,4096]{2,1,0:T(1,128)S(1)}, f32[1,1,4096]{2,1,0:T(1,128)}, u32[]{:S(2)}) copy-start(f32[1,1,4096]{2,1,0:T(1,128)} %param.14) | copy-start | bytes 49156
  13.8 4.2 %copy-start.4 = (f32[6,5]{0,1:T(8,128)S(1)}, f32[6,5]{0,1:T(8,128)}, u32[]{:S(2)}) copy-start(f32[6,5]{0,1:T(8,128)} %constant.65) | copy-start | bytes 364
  20.2 2.8 %copy-start.9 = (f32[8]{0:T(128)S(1)}, f32[8]{0:T(128)}, u32[]{:S(2)}) copy-start(f32[8]{0:T(128)} %pad.16.clone) | copy-start | bytes 100
  23.9 15.5 %copy-start.8 = (s32[64]{0:T(128)S(1)}, s32[64]{0:T(128)}, u32[]{:S(2)}) copy-start(s32[64]{0:T(128)} %get-tuple-element.18) | copy-start | bytes 772
  23.9 15.8 %copy-start.7 = (s32[64]{0:T(128)S(1)}, s32[64]{0:T(128)}, u32[]{:S(2)}) copy-start(s32[64]{0:T(128)} %get-tuple-element.20) | copy-start | bytes 772
  24.0 50.5 %copy-start.6 = (s32[64]{0:T(128)S(1)}, s32[64]{0:T(128)}, u32[]{:S(2)}) copy-start(s32[64]{0:T(128)} %get-tuple-element.19) | copy-start | bytes 772
  24.0 61.0 %copy-start.5 = (s32[64]{0:T(128)S(1)}, s32[64]{0:T(128)}, u32[]{:S(2)}) copy-start(s32[64]{0:T(128)} %get-tuple-element.17) | copy-start | bytes 772
  39.2 46.4 %copy-start.1 = (f32[1,1,4096]{2,1,0:T(1,128)S(1)}, f32[1,1,4096]{2,1,0:T(1,128)}, u32[]{:S(2)}) copy-start(f32[1,1,4096]{2,1,0:T(1,128)} %param.15) | copy-start | bytes 49156
  39.7 45.3 %collective-permute-start.4 = (f32[3,64,64]{1,2,0:T(8,128)S(1)}, f32[3,64,64]{1,2,0:T(8,128)S(1)}, u32[]{:S(2)}, u32[]{:S(2)}) collective-permute-start(f32[3,64,64]{1,2,0:T(8,128)S(1)} %convolution_bitcast_fusion.2), channel_id=1, source_target_pairs={{0,1},{1,2},{2,3},{3,0},{4,5},{5,6},{6,7},{7,4},{8,9},{9,10},{10,1... | collective-permute-start | bytes 147464 | tf_op jit(solution)/shard_map/ppermute | solution.py:213
  40.0 44.9 %collective-permute-start.5 = (f32[3,64,64]{1,2,0:T(8,128)S(1)}, f32[3,64,64]{1,2,0:T(8,128)S(1)}, u32[]{:S(2)}, u32[]{:S(2)}) collective-permute-start(f32[3,64,64]{1,2,0:T(8,128)S(1)} %convolution_bitcast_fusion.1), channel_id=1, source_target_pairs={{0,2},{1,3},{2,0},{3,1},{4,6},{5,7},{6,4},{7,5},{8,10},{9,11},{10,... | collective-permute-start | bytes 147464 | tf_op jit(solution)/shard_map/ppermute | solution.py:213
  44.4 37.2 %all-to-all-start = ((f32[32,1,8]{2,1,0:T(1,128)}), f32[32,1,8]{2,1,0:T(1,128)S(1)}, u32[]{:S(2)}, u32[]{:S(2)}) async-start(f32[32,1,8]{2,1,0:T(1,128)} %broadcast_in_dim.8), calls=%async_computation | async-start | bytes 32768 | tf_op jit(solution)/shard_map/all_to_all | solution.py:223
  74.7 10.3 %collective-permute-start.6 = (f32[3,64,64]{1,2,0:T(8,128)S(1)}, f32[3,64,64]{1,2,0:T(8,128)S(1)}, u32[]{:S(2)}, u32[]{:S(2)}) collective-permute-start(f32[3,64,64]{1,2,0:T(8,128)S(1)} %convolution_bitcast_fusion), channel_id=1, source_target_pairs={{0,3},{1,0},{2,1},{3,2},{4,7},{5,4},{6,5},{7,6},{8,11},{9,8},{10,9... | collective-permute-start | bytes 147464 | tf_op jit(solution)/shard_map/ppermute | solution.py:213

commit v6 on v5

--- a/solution.py
+++ b/solution.py
@@ -55,16 +55,34 @@
 LANES = 128
 
 
-def sweep_kernel(near_ref, far_ref, count_ref, home_ref, cand_ref, out_ref, spread_ref, acc_ref):
-    atom_count = home_ref.shape[0]
+def sweep_kernel(near_ref, far_ref, count_ref, *refs):
+    block_refs = refs[:5]
+    out_ref, cand_ref, spread_ref, acc_ref = refs[5:]
+    rows_per_block = block_refs[0].shape[0]
+    atom_count = rows_per_block * LANES
     tile_count = atom_count // TILE
-    cand_tiles = cand_ref.shape[0]
+    cand_tiles = 5 * tile_count
     pair_cap = near_ref.shape[0]
-    chunk = 512
-    for q in range(4):
-        for r in range(atom_count // chunk):
-            column = home_ref[r * chunk:(r + 1) * chunk, q:q + 1]
-            spread_ref[q, r * chunk:(r + 1) * chunk, :] = jnp.broadcast_to(column, (chunk, LANES))
+    sublane = lax.broadcasted_iota(jnp.int32, (8, LANES), 0)
+    shifts = ((0.0, 0.0), (-TX * cell_edge, 0.0), (TX * cell_edge, 0.0),
+              (0.0, -TY * cell_edge), (0.0, TY * cell_edge))
+    for k, (shift_x, shift_y) in enumerate(shifts):
+        values = block_refs[k][...]
+        if shift_x or shift_y:
+            offset = jnp.where(sublane == 0, shift_x, jnp.where(sublane == 1, shift_y, 0.0))
+            values = values + offset[None]
+        cand_ref[k * rows_per_block:(k + 1) * rows_per_block] = values
+
+    def spread_row(r, carry):
+        columns = jnp.transpose(block_refs[0][r])
+        start = pl.multiple_of(r * LANES, LANES)
+        for q in range(4):
+            spread_ref[q, pl.ds(start, LANES), :] = jnp.broadcast_to(
+                columns[:, q:q + 1], (LANES, LANES)
+            )
+        return carry
+
+    lax.fori_loop(0, rows_per_block, spread_row, 0)
     acc_ref[...] = jnp.zeros(acc_ref.shape, jnp.float32)
     total = count_ref[0]
     lane = lax.broadcasted_iota(jnp.int32, (1, LANES), 1)
@@ -83,7 +101,11 @@
         cand_a = jnp.clip(far_ref[first], 0, cand_tiles - 1)
         home_b = jnp.clip(near_ref[second], 0, tile_count - 1)
         cand_b = jnp.clip(far_ref[second], 0, cand_tiles - 1)
-        rows = jnp.where(left, cand_ref[cand_a] * has_first, cand_ref[cand_b] * has_second)
+        row_a = cand_ref[cand_a // 2]
+        row_a = jnp.where(cand_a % 2 == 1, pltpu.roll(row_a, TILE, 1), row_a)
+        row_b = cand_ref[cand_b // 2]
+        row_b = jnp.where(cand_b % 2 == 0, pltpu.roll(row_b, TILE, 1), row_b)
+        rows = jnp.where(left, row_a * has_first, row_b * has_second)
         base_a = pl.multiple_of(home_a * TILE, TILE)
         base_b = pl.multiple_of(home_b * TILE, TILE)
 
@@ -135,21 +157,23 @@
         out_ref[c:c + 1, :] = summed[0:1]
 
 
-def sweep(home_cols, cand_rows, near_list, far_list, pair_total):
-    atom_count = home_cols.shape[0]
+def sweep(blocks, near_list, far_list, pair_total):
+    rows_per_block = blocks[0].shape[0]
+    atom_count = rows_per_block * LANES
     smem = pl.BlockSpec(memory_space=pltpu.SMEM)
     vmem = pl.BlockSpec(memory_space=pltpu.VMEM)
     return pl.pallas_call(
         sweep_kernel,
         out_shape=jax.ShapeDtypeStruct((2, atom_count), jnp.float32),
-        in_specs=[smem, smem, smem, vmem, vmem],
+        in_specs=[smem, smem, smem] + [vmem] * 5,
         out_specs=vmem,
         scratch_shapes=[
+            pltpu.VMEM((5 * rows_per_block, 8, LANES), jnp.float32),
             pltpu.VMEM((4, atom_count, LANES), jnp.float32),
             pltpu.VMEM((2, atom_count, LANES), jnp.float32),
         ],
         compiler_params=pltpu.CompilerParams(vmem_limit_bytes=48 * 1024 * 1024),
-    )(near_list, far_list, pair_total, home_cols, cand_rows)
+    )(near_list, far_list, pair_total, *blocks)
 
 
 def on_device(
@@ -175,22 +199,21 @@
     charge_row = aux.reshape(atom_count)
     resid_row = resid.reshape(atom_count)
     packed = jnp.concatenate(
-        [positions.reshape(3, atom_count), charge_row[None], resid_row[None], radius[None]], axis=0
-    )
+        [
+            positions.reshape(3, atom_count),
+            jnp.square(radius)[None],
+            charge_row[None],
+            resid_row[None],
+            jnp.zeros((2, atom_count), jnp.float32),
+        ],
+        axis=0,
+    )
+    packed = packed.reshape(8, atom_count // LANES, LANES).transpose(1, 0, 2)
     blocks = neighbours(packed)
-    candidate = candidates(blocks, tile_count)
-    cand_rows = jnp.concatenate(
-        [candidate[:3], jnp.square(candidate[5:6]), candidate[3:5], jnp.zeros_like(candidate[:2])],
-        axis=0,
-    ).transpose(1, 0, 2)
-    cand_rows = jnp.concatenate([cand_rows, cand_rows], axis=-1)
-    home_cols = jnp.concatenate(
-        [packed[:3], jnp.square(packed[5:6]), jnp.zeros_like(packed[:4])], axis=0
-    ).T
     near_list = pair_tiles.reshape(-1)
     far_list = pair_cands.reshape(-1)
     pair_total = pair_count.reshape(1)
-    totals = sweep(home_cols, cand_rows, near_list, far_list, pair_total)
+    totals = sweep(blocks, near_list, far_list, pair_total)
     aux_field = totals[0].reshape(atom_count)
     resid_field = totals[1].reshape(atom_count)
     field = negativity + aux_field + resid_field

time: 87 us -> 101 us (1.16)
  starting transfers between devices: 42.6 us -> 59.8 us
  other arithmetic: 11.8 us -> 5.56 us
  Pallas kernels: 15.2 us -> 18.5 us
  waiting for transfers between devices: 3.31 us -> 4.53 us
  local copies, waits for them, and re-layouts: 8.56 us -> 7.41 us
    all_to_all x1, starting transfers between devices: 30 us -> 47.1 us  [on_device(): lax.all_to_all(sums_out, ('brick', 'plane'), split_axis=0, concat_axis=0,...]
    pallas_call x1, Pallas kernels: 15.2 us -> 18.5 us  [sweep(): pl.pallas_call(sweep_kernel, out_shape=jax.ShapeDtypeStruct((2, atom_coun...]
    ppermute x3, waiting for transfers between devices: 0.01 us -> 3.07 us  [to_owners(): lax.ppermute(part, 'plane', [(i, (i + step) % planes) for i in range(plan...]
    unnamed x25 -> x21, local copies, waits for them, and re-layouts: 1.43 us -> 4.45 us
    slice x8 -> x0, local copies, waits for them, and re-layouts: 2.86 us -> none  [the longest x4 2.13 us: on_device(): candidate[3:5]]
    all_to_all x1, waiting for transfers between devices: 3.29 us -> 1.36 us  [on_device(): lax.all_to_all(sums_out, ('brick', 'plane'), split_axis=0, concat_axis=0,...]
    concatenate x3 -> x0, other arithmetic: 1.92 us -> none  [the longest x1 1.44 us: on_device(): jnp.concatenate([positions.reshape(3, atom_count), charge_row[None], resi...]
    sub x1, other arithmetic: 1.27 us -> 0.01 us  [to_owners(): local_target = target - owner * tile_count]
  transfers between devices with their start and end apart: 8 -> 8, of which waited for: 1 -> 3; matrix products, arithmetic and copies ran while one was open for 12% -> 4% of each run, Pallas kernels for 0% -> 0%
where the time goes in v6:
time: 101 us; the launch traced here: 100 us
  starting transfers between devices  59.8 us (59%)
  Pallas kernels  18.5 us (18%)
  local copies, waits for them, and re-layouts  7.41 us (7%)
  other arithmetic  5.56 us (6%)
  waiting for transfers between devices  4.53 us (4%)
  between operations  3.46 us (3%)
    all_to_all x1, starting transfers between devices, on_device(): lax.all_to_all(sums_out, ('brick', 'plane'), split_axis=0, concat_axis=0,...  47.1 us
    pallas_call x1, Pallas kernels, sweep(): pl.pallas_call(sweep_kernel, out_shape=jax.ShapeDtypeStruct((2, atom_coun...  18.5 us
    ppermute x4, starting transfers between devices, shifted_from(): return lax.ppermute(block, axis, pairs)  7.78 us
    ppermute x3, starting transfers between devices, to_owners(): lax.ppermute(part, 'plane', [(i, (i + step) % planes) for i in range(plan...  4.86 us
    unnamed x21, local copies, waits for them, and re-layouts  4.45 us
    ppermute x3, waiting for transfers between devices, to_owners(): lax.ppermute(part, 'plane', [(i, (i + step) % planes) for i in range(plan...  3.07 us
  transfers between devices with their start and end apart: 8, of which 3 were waited for; matrix products, arithmetic and copies ran while one was open for 4% of the time, Pallas kernels for 0%

profile of v6, /device:TPU:0, one launch (start us, length us, event | category | flops | bytes accessed | tf_op | source)
XLA Modules:
  0.0 100.3 jit_solution(5733111995741265896)
XLA Ops:
  0.6 0.8 copy.28
  1.5 0.6 copy-done.6
  2.2 0.2 select_reduce_fusion.2
  2.4 0.7 copy-done
  3.1 0.1 concatenate.14
  3.2 0.5 collective-permute-start
  3.8 2.9 %collective-permute-start.1 = (f32[32,8,128]{2,1,0:T(8,128)S(1)}, f32[32,8,128]{2,1,0:T(8,128)S(1)}, u32[]{:S(2)}, u32[]{:S(2)}) collective-permute-start(f32[32,8,128]{2,1,0:T(8,128)S(1)} %bitcast.63), channel_id=1, source_target_pairs={{0,28},{4,0},{8,4},{12,8},{16,12},{20,16},{24,20},{28,24},{1,29},{... | collective-permute-start | bytes 393224 | tf_op jit(solution)/shard_map/ppermute | solution.py:24
  6.7 2.3 %collective-permute-start.2 = (f32[32,8,128]{2,1,0:T(8,128)S(1)}, f32[32,8,128]{2,1,0:T(8,128)S(1)}, u32[]{:S(2)}, u32[]{:S(2)}) collective-permute-start(f32[32,8,128]{2,1,0:T(8,128)S(1)} %bitcast.64), channel_id=1, source_target_pairs={{0,1},{1,2},{2,3},{3,0},{4,5},{5,6},{6,7},{7,4},{8,9},{9,10},{10,1... | collective-permute-start | bytes 393224 | tf_op jit(solution)/shard_map/ppermute | solution.py:24
  9.0 2.0 %collective-permute-start.3 = (f32[32,8,128]{2,1,0:T(8,128)S(1)}, f32[32,8,128]{2,1,0:T(8,128)S(1)}, u32[]{:S(2)}, u32[]{:S(2)}) collective-permute-start(f32[32,8,128]{2,1,0:T(8,128)S(1)} %bitcast.65), channel_id=1, source_target_pairs={{0,3},{1,0},{2,1},{3,2},{4,7},{5,4},{6,5},{7,6},{8,11},{9,8},{10,9... | collective-permute-start | bytes 393224 | tf_op jit(solution)/shard_map/ppermute | solution.py:24
  11.0 0.7 copy-done.4
  11.7 0.7 copy-done.5
  13.1 0.5 broadcast.96
  13.6 1.3 %fusion.25 = (f32[4096]{0:T(1024)S(1)}, f32[]{:T(128)}) fusion(f32[1,1,4096]{2,1,0:T(1,128)S(1)} %copy-done, f32[]{:T(128)} %broadcast.96), kind=kLoop, calls=%fused_computation.50 | loop fusion | flops 4095 | bytes 32776 | tf_op args[1]
  15.2 0.6 copy-done.9
  15.8 0.1 collective-permute-done.3.refs_4_
  15.9 18.5 %shard_map.139 = f32[2,4096]{1,0:T(2,128)S(1)} custom-call(s32[1496]{0:T(1024)S(1)} %reduce.2.near_ref, s32[1496]{0:T(1024)S(1)} %reduce.3.far_ref, s32[1]{0:T(128)} %bitcast.61.count_ref, f32[32,8,128]{2,1,0:T(8,128)S(1)} %bitcast.66, f32[32,8,128]{2,1,0:T(8,128)S(1)} %collective-permute-done.refs_1_, f32[32,8,128]{2,1,0:T(8,128)S(1)} %collective-permute-done.1.refs_2_, ...), custom_call_target="tpu_custom_call" | custom-call | tf_op jit(solution)/shard_map/pallas_call | solution.py:165
  34.5 0.6 fusion.20
  35.1 2.0 %select_maximum_fusion = f32[8]{0:T(128)S(1)} fusion(f32[1]{0:T(128)} %bitcast.11, f32[1]{0:T(128)} %bitcast.10, f32[1]{0:T(128)} %bitcast), kind=kLoop, calls=%fused_computation.38 | loop fusion | flops 48 | bytes 44 | tf_op jit(solution)/shard_map/stack | solution.py:242
  37.1 0.6 broadcast_in_dim.5
  37.7 47.1 %all-to-all-start = ((f32[32,1,8]{2,1,0:T(1,128)}), f32[32,1,8]{2,1,0:T(1,128)S(1)}, u32[]{:S(2)}, u32[]{:S(2)}) async-start(f32[32,1,8]{2,1,0:T(1,128)} %broadcast_in_dim.5), calls=%async_computation | async-start | bytes 32768 | tf_op jit(solution)/shard_map/all_to_all | solution.py:246
  85.0 0.3 convolution_bitcast_fusion
  85.3 3.7 %collective-permute-start.6 = (f32[3,64,64]{1,2,0:T(8,128)S(1)}, f32[3,64,64]{1,2,0:T(8,128)S(1)}, u32[]{:S(2)}, u32[]{:S(2)}) collective-permute-start(f32[3,64,64]{1,2,0:T(8,128)S(1)} %convolution_bitcast_fusion), channel_id=1, source_target_pairs={{0,3},{1,0},{2,1},{3,2},{4,7},{5,4},{6,5},{7,6},{8,11},{9,8},{10,9... | collective-permute-start | bytes 147464 | tf_op jit(solution)/shard_map/ppermute | solution.py:236
  89.0 0.2 convolution_bitcast_fusion.1
  89.3 0.2 convolution_bitcast_fusion.2
  89.5 1.1 %collective-permute-start.4 = (f32[3,64,64]{1,2,0:T(8,128)S(1)}, f32[3,64,64]{1,2,0:T(8,128)S(1)}, u32[]{:S(2)}, u32[]{:S(2)}) collective-permute-start(f32[3,64,64]{1,2,0:T(8,128)S(1)} %convolution_bitcast_fusion.2), channel_id=1, source_target_pairs={{0,1},{1,2},{2,3},{3,0},{4,5},{5,6},{6,7},{7,4},{8,9},{9,10},{10,1... | collective-permute-start | bytes 147464 | tf_op jit(solution)/shard_map/ppermute | solution.py:236
  90.7 1.4 %all-to-all-done = f32[32,1,8]{2,1,0:T(1,128)S(1)} async-done(((f32[32,1,8]{2,1,0:T(1,128)}), f32[32,1,8]{2,1,0:T(1,128)S(1)}, u32[]{:S(2)}, u32[]{:S(2)}) %all-to-all-start) | async-done | bytes 1056 | tf_op jit(solution)/shard_map/all_to_all | solution.py:246
  92.1 0.6 fusion.26
  94.6 0.6 fusion.15
  95.3 3.1 %collective-permute-done.5 = f32[3,64,64]{1,2,0:T(8,128)S(1)} collective-permute-done((f32[3,64,64]{1,2,0:T(8,128)S(1)}, f32[3,64,64]{1,2,0:T(8,128)S(1)}, u32[]{:S(2)}, u32[]{:S(2)}) %collective-permute-start.5) | collective-permute-done | bytes 49184 | tf_op jit(solution)/shard_map/ppermute | solution.py:236
  98.4 0.3 fusion.2
  99.0 0.6 copy-done.3
  99.6 0.6 subtract_add_fusion
  (38 shorter events, 1.1 us)
Async XLA Ops:
  0.6 0.9 copy-start.2
  1.5 0.7 copy-start.6
  1.5 0.7 copy-start.7
  1.5 0.7 copy-start.8
  2.4 0.7 copy-start
  2.4 0.7 copy-start.1
  3.2 12.5 %collective-permute-start = (f32[32,8,128]{2,1,0:T(8,128)S(1)}, f32[32,8,128]{2,1,0:T(8,128)S(1)}, u32[]{:S(2)}, u32[]{:S(2)}) collective-permute-start(f32[32,8,128]{2,1,0:T(8,128)S(1)} %bitcast.62), channel_id=1, source_target_pairs={{0,4},{4,8},{8,12},{12,16},{16,20},{20,24},{24,28},{28,0},{1,5},{5... | collective-permute-start | bytes 393224 | tf_op jit(solution)/shard_map/ppermute | solution.py:24
  3.8 12.0 %collective-permute-start.1 = (f32[32,8,128]{2,1,0:T(8,128)S(1)}, f32[32,8,128]{2,1,0:T(8,128)S(1)}, u32[]{:S(2)}, u32[]{:S(2)}) collective-permute-start(f32[32,8,128]{2,1,0:T(8,128)S(1)} %bitcast.63), channel_id=1, source_target_pairs={{0,28},{4,0},{8,4},{12,8},{16,12},{20,16},{24,20},{28,24},{1,29},{... | collective-permute-start | bytes 393224 | tf_op jit(solution)/shard_map/ppermute | solution.py:24
  6.7 9.1 %collective-permute-start.2 = (f32[32,8,128]{2,1,0:T(8,128)S(1)}, f32[32,8,128]{2,1,0:T(8,128)S(1)}, u32[]{:S(2)}, u32[]{:S(2)}) collective-permute-start(f32[32,8,128]{2,1,0:T(8,128)S(1)} %bitcast.64), channel_id=1, source_target_pairs={{0,1},{1,2},{2,3},{3,0},{4,5},{5,6},{6,7},{7,4},{8,9},{9,10},{10,1... | collective-permute-start | bytes 393224 | tf_op jit(solution)/shard_map/ppermute | solution.py:24
  9.0 6.9 %collective-permute-start.3 = (f32[32,8,128]{2,1,0:T(8,128)S(1)}, f32[32,8,128]{2,1,0:T(8,128)S(1)}, u32[]{:S(2)}, u32[]{:S(2)}) collective-permute-start(f32[32,8,128]{2,1,0:T(8,128)S(1)} %bitcast.65), channel_id=1, source_target_pairs={{0,3},{1,0},{2,1},{3,2},{4,7},{5,4},{6,5},{7,6},{8,11},{9,8},{10,9... | collective-permute-start | bytes 393224 | tf_op jit(solution)/shard_map/ppermute | solution.py:24
  11.0 0.7 copy-start.4
  11.7 0.7 copy-start.5
  15.1 0.7 copy-start.9
  37.7 54.3 %all-to-all-start = ((f32[32,1,8]{2,1,0:T(1,128)}), f32[32,1,8]{2,1,0:T(1,128)S(1)}, u32[]{:S(2)}, u32[]{:S(2)}) async-start(f32[32,1,8]{2,1,0:T(1,128)} %broadcast_in_dim.5), calls=%async_computation | async-start | bytes 32768 | tf_op jit(solution)/shard_map/all_to_all | solution.py:246
  85.3 10.0 %collective-permute-start.6 = (f32[3,64,64]{1,2,0:T(8,128)S(1)}, f32[3,64,64]{1,2,0:T(8,128)S(1)}, u32[]{:S(2)}, u32[]{:S(2)}) collective-permute-start(f32[3,64,64]{1,2,0:T(8,128)S(1)} %convolution_bitcast_fusion), channel_id=1, source_target_pairs={{0,3},{1,0},{2,1},{3,2},{4,7},{5,4},{6,5},{7,6},{8,11},{9,8},{10,9... | collective-permute-start | bytes 147464 | tf_op jit(solution)/shard_map/ppermute | solution.py:236
  89.2 9.2 %collective-permute-start.5 = (f32[3,64,64]{1,2,0:T(8,128)S(1)}, f32[3,64,64]{1,2,0:T(8,128)S(1)}, u32[]{:S(2)}, u32[]{:S(2)}) collective-permute-start(f32[3,64,64]{1,2,0:T(8,128)S(1)} %convolution_bitcast_fusion.1), channel_id=1, source_target_pairs={{0,2},{1,3},{2,0},{3,1},{4,6},{5,7},{6,4},{7,5},{8,10},{9,11},{10,... | collective-permute-start | bytes 147464 | tf_op jit(solution)/shard_map/ppermute | solution.py:236
  89.5 8.8 %collective-permute-start.4 = (f32[3,64,64]{1,2,0:T(8,128)S(1)}, f32[3,64,64]{1,2,0:T(8,128)S(1)}, u32[]{:S(2)}, u32[]{:S(2)}) collective-permute-start(f32[3,64,64]{1,2,0:T(8,128)S(1)} %convolution_bitcast_fusion.2), channel_id=1, source_target_pairs={{0,1},{1,2},{2,3},{3,0},{4,5},{5,6},{6,7},{7,4},{8,9},{9,10},{10,1... | collective-permute-start | bytes 147464 | tf_op jit(solution)/shard_map/ppermute | solution.py:236
  98.9 0.7 copy-start.3

commit v7 on v6

--- a/solution.py
+++ b/solution.py
@@ -55,7 +55,7 @@
 LANES = 128
 
 
-def sweep_kernel(near_ref, far_ref, count_ref, *refs):
+def sweep_kernel(near_ref, far_ref, count_ref, home_ref, *refs):
     block_refs = refs[:5]
     out_ref, cand_ref, spread_ref, acc_ref = refs[5:]
     rows_per_block = block_refs[0].shape[0]
@@ -64,25 +64,28 @@
     cand_tiles = 5 * tile_count
     pair_cap = near_ref.shape[0]
     sublane = lax.broadcasted_iota(jnp.int32, (8, LANES), 0)
+    left_rows = lax.broadcasted_iota(jnp.int32, (8, LANES), 1) < TILE
     shifts = ((0.0, 0.0), (-TX * cell_edge, 0.0), (TX * cell_edge, 0.0),
               (0.0, -TY * cell_edge), (0.0, TY * cell_edge))
-    for k, (shift_x, shift_y) in enumerate(shifts):
-        values = block_refs[k][...]
-        if shift_x or shift_y:
-            offset = jnp.where(sublane == 0, shift_x, jnp.where(sublane == 1, shift_y, 0.0))
-            values = values + offset[None]
-        cand_ref[k * rows_per_block:(k + 1) * rows_per_block] = values
-
-    def spread_row(r, carry):
-        columns = jnp.transpose(block_refs[0][r])
-        start = pl.multiple_of(r * LANES, LANES)
-        for q in range(4):
-            spread_ref[q, pl.ds(start, LANES), :] = jnp.broadcast_to(
-                columns[:, q:q + 1], (LANES, LANES)
-            )
+
+    def build_rows(r, carry):
+        for k, (shift_x, shift_y) in enumerate(shifts):
+            values = block_refs[k][r]
+            if shift_x or shift_y:
+                values = values + jnp.where(
+                    sublane == 0, shift_x, jnp.where(sublane == 1, shift_y, 0.0)
+                )
+            rolled = pltpu.roll(values, TILE, 1)
+            cand_ref[k * tile_count + 2 * r] = jnp.where(left_rows, values, rolled)
+            cand_ref[k * tile_count + 2 * r + 1] = jnp.where(left_rows, rolled, values)
         return carry
 
-    lax.fori_loop(0, rows_per_block, spread_row, 0)
+    lax.fori_loop(0, rows_per_block, build_rows, 0)
+    chunk = 512
+    for q in range(4):
+        for r in range(atom_count // chunk):
+            column = home_ref[r * chunk:(r + 1) * chunk, q:q + 1]
+            spread_ref[q, r * chunk:(r + 1) * chunk, :] = jnp.broadcast_to(column, (chunk, LANES))
     acc_ref[...] = jnp.zeros(acc_ref.shape, jnp.float32)
     total = count_ref[0]
     lane = lax.broadcasted_iota(jnp.int32, (1, LANES), 1)
@@ -101,11 +104,7 @@
         cand_a = jnp.clip(far_ref[first], 0, cand_tiles - 1)
         home_b = jnp.clip(near_ref[second], 0, tile_count - 1)
         cand_b = jnp.clip(far_ref[second], 0, cand_tiles - 1)
-        row_a = cand_ref[cand_a // 2]
-        row_a = jnp.where(cand_a % 2 == 1, pltpu.roll(row_a, TILE, 1), row_a)
-        row_b = cand_ref[cand_b // 2]
-        row_b = jnp.where(cand_b % 2 == 0, pltpu.roll(row_b, TILE, 1), row_b)
-        rows = jnp.where(left, row_a * has_first, row_b * has_second)
+        rows = jnp.where(left, cand_ref[cand_a] * has_first, cand_ref[cand_b] * has_second)
         base_a = pl.multiple_of(home_a * TILE, TILE)
         base_b = pl.multiple_of(home_b * TILE, TILE)
 
@@ -157,7 +156,7 @@
         out_ref[c:c + 1, :] = summed[0:1]
 
 
-def sweep(blocks, near_list, far_list, pair_total):
+def sweep(home_cols, blocks, near_list, far_list, pair_total):
     rows_per_block = blocks[0].shape[0]
     atom_count = rows_per_block * LANES
     smem = pl.BlockSpec(memory_space=pltpu.SMEM)
@@ -165,15 +164,15 @@
     return pl.pallas_call(
         sweep_kernel,
         out_shape=jax.ShapeDtypeStruct((2, atom_count), jnp.float32),
-        in_specs=[smem, smem, smem] + [vmem] * 5,
+        in_specs=[smem, smem, smem] + [vmem] * 6,
         out_specs=vmem,
         scratch_shapes=[
-            pltpu.VMEM((5 * rows_per_block, 8, LANES), jnp.float32),
+            pltpu.VMEM((10 * rows_per_block, 8, LANES), jnp.float32),
             pltpu.VMEM((4, atom_count, LANES), jnp.float32),
             pltpu.VMEM((2, atom_count, LANES), jnp.float32),
         ],
         compiler_params=pltpu.CompilerParams(vmem_limit_bytes=48 * 1024 * 1024),
-    )(near_list, far_list, pair_total, *blocks)
+    )(near_list, far_list, pair_total, home_cols, *blocks)
 
 
 def on_device(
@@ -208,12 +207,13 @@
         ],
         axis=0,
     )
+    home_cols = packed.T
     packed = packed.reshape(8, atom_count // LANES, LANES).transpose(1, 0, 2)
     blocks = neighbours(packed)
     near_list = pair_tiles.reshape(-1)
     far_list = pair_cands.reshape(-1)
     pair_total = pair_count.reshape(1)
-    totals = sweep(blocks, near_list, far_list, pair_total)
+    totals = sweep(home_cols, blocks, near_list, far_list, pair_total)
     aux_field = totals[0].reshape(atom_count)
     resid_field = totals[1].reshape(atom_count)
     field = negativity + aux_field + resid_field

time: 101 us -> 82.6 us (0.82)
  starting transfers between devices: 59.8 us -> 42.6 us
  Pallas kernels: 18.5 us -> 16.1 us
  other arithmetic: 5.56 us -> 7.68 us
    all_to_all x1, starting transfers between devices: 47.1 us -> 30 us  [on_device(): lax.all_to_all(sums_out, ('brick', 'plane'), split_axis=0, concat_axis=0,...]
    unnamed x21 -> x8, local copies, waits for them, and re-layouts: 4.45 us -> 1.38 us
    pallas_call x1, Pallas kernels: 18.5 us -> 16.1 us  [sweep(): pl.pallas_call(sweep_kernel, out_shape=jax.ShapeDtypeStruct((2, atom_coun...]
    concatenate x2 -> x4, local copies, waits for them, and re-layouts: 0.97 us -> 3.15 us  [on_device(): jnp.concatenate([positions.reshape(3, atom_count), jnp.square(radius)[Non...]
    unnamed x3, other arithmetic: 1.33 us -> 2.71 us
  transfers between devices with their start and end apart: 8 -> 8, of which waited for: 3 -> 2; matrix products, arithmetic and copies ran while one was open for 4% -> 10% of each run, Pallas kernels for 0% -> 0%
where the time goes in v7:
time: 82.6 us; the launch traced here: 81.9 us
  starting transfers between devices  42.6 us (52%)
  Pallas kernels  16.1 us (19%)
  other arithmetic  7.68 us (9%)
  local copies, waits for them, and re-layouts  6.55 us (8%)
  waiting for transfers between devices  4.43 us (5%)
  between operations  3.51 us (4%)
  matrix products  1 us (1%)
    all_to_all x1, starting transfers between devices, on_device(): lax.all_to_all(sums_out, ('brick', 'plane'), split_axis=0, concat_axis=0,...  30 us
    pallas_call x1, Pallas kernels, sweep(): pl.pallas_call(sweep_kernel, out_shape=jax.ShapeDtypeStruct((2, atom_coun...  16.1 us
    ppermute x4, starting transfers between devices, shifted_from(): return lax.ppermute(block, axis, pairs)  7.78 us
    ppermute x3, starting transfers between devices, to_owners(): lax.ppermute(part, 'plane', [(i, (i + step) % planes) for i in range(plan...  4.86 us
    concatenate x4, local copies, waits for them, and re-layouts, on_device(): jnp.concatenate([positions.reshape(3, atom_count), jnp.square(radius)[Non...  3.15 us
    ppermute x3, waiting for transfers between devices, to_owners(): lax.ppermute(part, 'plane', [(i, (i + step) % planes) for i in range(plan...  3.07 us
    unnamed x3, other arithmetic  2.71 us
    another operation x1, other arithmetic, on_device(): jnp.stack([jnp.sum(charge_row), jnp.sum(field / hardness_row), jnp.sum(1....  2.01 us
  transfers between devices with their start and end apart: 8, of which 2 were waited for; matrix products, arithmetic and copies ran while one was open for 10% of the time, Pallas kernels for 0%

profile of v7, /device:TPU:0, one launch (start us, length us, event | category | flops | bytes accessed | tf_op | source)
XLA Modules:
  0.0 81.9 jit_solution(12905390955449456352)
XLA Ops:
  0.7 0.9 %select_reduce_fusion.2 = (f32[4096]{0:T(1024)S(1)}, f32[4096]{0:T(1024)S(1)}, f32[4096]{0:T(1024)S(1)}) fusion(f32[8]{0:T(128)} %param.21, s32[4096]{0:T(1024)} %bitcast.88, f32[8]{0:T(128)} %param.22, f32[8]{0:T(128)} %param.23), kind=kLoop, calls=%fused_computation.9 | loop fusion | flops 217088 | bytes 65632 | tf_op jit(solution)/shard_map/reduce_sum | solution.py:41
  1.6 0.8 %copy.42 = f32[3,32,128]{2,0,1:T(4,128)S(1)} copy(f32[3,32,128]{2,1,0:T(8,128)} %bitcast.79) | data formatting | bytes 98304 | tf_op jit(solution)/shard_map/concatenate | solution.py:200
  2.4 0.9 %concatenate.17 = f32[8,32,128]{2,0,1:T(8,128)S(1)} concatenate(f32[3,32,128]{2,0,1:T(4,128)S(1)} %copy.42, f32[1,32,128]{2,0,1:T(1,128)S(1)} %bitcast.80, f32[1,32,128]{2,0,1:T(1,128)} %bitcast.82, f32[1,32,128]{2,0,1:T(1,128)} %bitcast.84, f32[2,32,128]{2,0,1:T(2,128)S(1)} %broadcast_in_dim.7), dimensions={0} | concatenate | bytes 262144 | tf_op jit(solution)/shard_map/concatenate | solution.py:200
  3.3 0.5 collective-permute-start
  3.8 2.9 %collective-permute-start.1 = (f32[32,8,128]{2,1,0:T(8,128)S(1)}, f32[32,8,128]{2,1,0:T(8,128)S(1)}, u32[]{:S(2)}, u32[]{:S(2)}) collective-permute-start(f32[32,8,128]{2,1,0:T(8,128)S(1)} %bitcast.71), channel_id=1, source_target_pairs={{0,28},{4,0},{8,4},{12,8},{16,12},{20,16},{24,20},{28,24},{1,29},{... | collective-permute-start | bytes 393224 | tf_op jit(solution)/shard_map/ppermute | solution.py:24
  6.8 2.3 %collective-permute-start.2 = (f32[32,8,128]{2,1,0:T(8,128)S(1)}, f32[32,8,128]{2,1,0:T(8,128)S(1)}, u32[]{:S(2)}, u32[]{:S(2)}) collective-permute-start(f32[32,8,128]{2,1,0:T(8,128)S(1)} %bitcast.72), channel_id=1, source_target_pairs={{0,1},{1,2},{2,3},{3,0},{4,5},{5,6},{6,7},{7,4},{8,9},{9,10},{10,1... | collective-permute-start | bytes 393224 | tf_op jit(solution)/shard_map/ppermute | solution.py:24
  9.0 2.0 %collective-permute-start.3 = (f32[32,8,128]{2,1,0:T(8,128)S(1)}, f32[32,8,128]{2,1,0:T(8,128)S(1)}, u32[]{:S(2)}, u32[]{:S(2)}) collective-permute-start(f32[32,8,128]{2,1,0:T(8,128)S(1)} %bitcast.73), channel_id=1, source_target_pairs={{0,3},{1,0},{2,1},{3,2},{4,7},{5,4},{6,5},{7,6},{8,11},{9,8},{10,9... | collective-permute-start | bytes 393224 | tf_op jit(solution)/shard_map/ppermute | solution.py:24
  11.1 0.8 %copy.55 = f32[1,1,3,4096]{3,2,1,0:T(4,128)S(1)} copy(f32[1,1,3,4096]{3,1,2,0:T(1,128)} %param.12) | data formatting | bytes 98304
  11.9 0.7 reduce.2.near_ref
  12.7 0.7 reduce.3.far_ref
  14.0 0.9 %concatenate.13 = f32[8,4096]{1,0:T(8,128)S(1)} concatenate(f32[3,4096]{1,0:T(4,128)S(1)} %bitcast.75, f32[1,4096]{1,0:T(1,128)S(1)} %bitcast.81, f32[1,4096]{1,0:T(1,128)} %bitcast.83, f32[1,4096]{1,0:T(1,128)} %bitcast.85, f32[2,4096]{1,0:T(2,128)S(1)} %broadcast_in_dim.6), dimensions={0} | concatenate | bytes 262144 | tf_op jit(solution)/shard_map/concatenate | solution.py:200
  14.9 0.6 copy.41
  15.5 0.5 broadcast.96
  16.0 1.3 %fusion.25 = (f32[4096]{0:T(1024)S(1)}, f32[]{:T(128)}) fusion(f32[1,1,4096]{2,1,0:T(1,128)S(1)} %copy-done, f32[]{:T(128)} %broadcast.96), kind=kLoop, calls=%fused_computation.51 | loop fusion | flops 4095 | bytes 32776 | tf_op args[1]
  17.7 16.1 %shard_map.139 = f32[2,4096]{1,0:T(2,128)S(1)} custom-call(s32[1496]{0:T(1024)S(1)} %reduce.2.near_ref, s32[1496]{0:T(1024)S(1)} %reduce.3.far_ref, s32[1]{0:T(128)} %bitcast.68.count_ref, f32[4096,8]{1,0:T(8,128)S(1)} %bitcast.69, f32[32,8,128]{2,1,0:T(8,128)S(1)} %bitcast.74, f32[32,8,128]{2,1,0:T(8,128)S(1)} %collective-permute-done.refs_1_, ...), custom_call_target="tpu_custom_call" | custom-call | tf_op jit(solution)/shard_map/pallas_call | solution.py:164
  33.9 0.6 fusion.20
  34.5 2.0 %select_maximum_fusion = f32[8]{0:T(128)S(1)} fusion(f32[1]{0:T(128)} %bitcast.15, f32[1]{0:T(128)} %bitcast.14, f32[1]{0:T(128)} %bitcast), kind=kLoop, calls=%fused_computation.39 | loop fusion | flops 48 | bytes 44 | tf_op jit(solution)/shard_map/stack | solution.py:242
  36.5 0.6 broadcast_in_dim.8
  37.1 30.0 %all-to-all-start = ((f32[32,1,8]{2,1,0:T(1,128)}), f32[32,1,8]{2,1,0:T(1,128)S(1)}, u32[]{:S(2)}, u32[]{:S(2)}) async-start(f32[32,1,8]{2,1,0:T(1,128)} %broadcast_in_dim.8), calls=%async_computation | async-start | bytes 32768 | tf_op jit(solution)/shard_map/all_to_all | solution.py:246
  67.3 0.3 convolution_bitcast_fusion
  67.5 3.7 %collective-permute-start.6 = (f32[3,64,64]{1,2,0:T(8,128)S(1)}, f32[3,64,64]{1,2,0:T(8,128)S(1)}, u32[]{:S(2)}, u32[]{:S(2)}) collective-permute-start(f32[3,64,64]{1,2,0:T(8,128)S(1)} %convolution_bitcast_fusion), channel_id=1, source_target_pairs={{0,3},{1,0},{2,1},{3,2},{4,7},{5,4},{6,5},{7,6},{8,11},{9,8},{10,9... | collective-permute-start | bytes 147464 | tf_op jit(solution)/shard_map/ppermute | solution.py:236
  71.2 0.2 convolution_bitcast_fusion.1
  71.5 0.3 convolution_bitcast_fusion.2
  71.8 1.1 %collective-permute-start.4 = (f32[3,64,64]{1,2,0:T(8,128)S(1)}, f32[3,64,64]{1,2,0:T(8,128)S(1)}, u32[]{:S(2)}, u32[]{:S(2)}) collective-permute-start(f32[3,64,64]{1,2,0:T(8,128)S(1)} %convolution_bitcast_fusion.2), channel_id=1, source_target_pairs={{0,1},{1,2},{2,3},{3,0},{4,5},{5,6},{6,7},{7,4},{8,9},{9,10},{10,1... | collective-permute-start | bytes 147464 | tf_op jit(solution)/shard_map/ppermute | solution.py:236
  72.9 1.4 %all-to-all-done = f32[32,1,8]{2,1,0:T(1,128)S(1)} async-done(((f32[32,1,8]{2,1,0:T(1,128)}), f32[32,1,8]{2,1,0:T(1,128)S(1)}, u32[]{:S(2)}, u32[]{:S(2)}) %all-to-all-start) | async-done | bytes 1056 | tf_op jit(solution)/shard_map/all_to_all | solution.py:246
  74.3 0.6 fusion.26
  76.9 0.6 fusion.15
  77.5 3.1 %collective-permute-done.5 = f32[3,64,64]{1,2,0:T(8,128)S(1)} collective-permute-done((f32[3,64,64]{1,2,0:T(8,128)S(1)}, f32[3,64,64]{1,2,0:T(8,128)S(1)}, u32[]{:S(2)}, u32[]{:S(2)}) %collective-permute-start.5) | collective-permute-done | bytes 49184 | tf_op jit(solution)/shard_map/ppermute | solution.py:236
  80.6 0.2 fusion.2
  81.0 0.1 mul.83
  81.1 0.1 mul.80
  81.2 0.6 subtract_add_fusion
  (28 shorter events, 0.9 us)
Async XLA Ops:
  0.6 15.4 %copy-start = (f32[1,1,4096]{2,1,0:T(1,128)S(1)}, f32[1,1,4096]{2,1,0:T(1,128)}, u32[]{:S(2)}) copy-start(f32[1,1,4096]{2,1,0:T(1,128)} %param.13) | copy-start | bytes 49156
  0.6 17.0 %copy-start.2 = (s32[1,1,64]{2,1,0:T(1,128)S(1)}, s32[1,1,64]{2,1,0:T(1,128)}, u32[]{:S(2)}) copy-start(s32[1,1,64]{2,1,0:T(1,128)} %param.20) | copy-start | bytes 772
  3.3 14.4 %collective-permute-start = (f32[32,8,128]{2,1,0:T(8,128)S(1)}, f32[32,8,128]{2,1,0:T(8,128)S(1)}, u32[]{:S(2)}, u32[]{:S(2)}) collective-permute-start(f32[32,8,128]{2,1,0:T(8,128)S(1)} %bitcast.70), channel_id=1, source_target_pairs={{0,4},{4,8},{8,12},{12,16},{16,20},{20,24},{24,28},{28,0},{1,5},{5... | collective-permute-start | bytes 393224 | tf_op jit(solution)/shard_map/ppermute | solution.py:24
  3.8 13.8 %collective-permute-start.1 = (f32[32,8,128]{2,1,0:T(8,128)S(1)}, f32[32,8,128]{2,1,0:T(8,128)S(1)}, u32[]{:S(2)}, u32[]{:S(2)}) collective-permute-start(f32[32,8,128]{2,1,0:T(8,128)S(1)} %bitcast.71), channel_id=1, source_target_pairs={{0,28},{4,0},{8,4},{12,8},{16,12},{20,16},{24,20},{28,24},{1,29},{... | collective-permute-start | bytes 393224 | tf_op jit(solution)/shard_map/ppermute | solution.py:24
  6.8 10.9 %collective-permute-start.2 = (f32[32,8,128]{2,1,0:T(8,128)S(1)}, f32[32,8,128]{2,1,0:T(8,128)S(1)}, u32[]{:S(2)}, u32[]{:S(2)}) collective-permute-start(f32[32,8,128]{2,1,0:T(8,128)S(1)} %bitcast.72), channel_id=1, source_target_pairs={{0,1},{1,2},{2,3},{3,0},{4,5},{5,6},{6,7},{7,4},{8,9},{9,10},{10,1... | collective-permute-start | bytes 393224 | tf_op jit(solution)/shard_map/ppermute | solution.py:24
  9.0 8.6 %collective-permute-start.3 = (f32[32,8,128]{2,1,0:T(8,128)S(1)}, f32[32,8,128]{2,1,0:T(8,128)S(1)}, u32[]{:S(2)}, u32[]{:S(2)}) collective-permute-start(f32[32,8,128]{2,1,0:T(8,128)S(1)} %bitcast.73), channel_id=1, source_target_pairs={{0,3},{1,0},{2,1},{3,2},{4,7},{5,4},{6,5},{7,6},{8,11},{9,8},{10,9... | collective-permute-start | bytes 393224 | tf_op jit(solution)/shard_map/ppermute | solution.py:24
  17.7 63.5 %copy-start.1 = (f32[1,1,4096]{2,1,0:T(1,128)S(1)}, f32[1,1,4096]{2,1,0:T(1,128)}, u32[]{:S(2)}) copy-start(f32[1,1,4096]{2,1,0:T(1,128)} %param.14) | copy-start | bytes 49156
  37.1 37.1 %all-to-all-start = ((f32[32,1,8]{2,1,0:T(1,128)}), f32[32,1,8]{2,1,0:T(1,128)S(1)}, u32[]{:S(2)}, u32[]{:S(2)}) async-start(f32[32,1,8]{2,1,0:T(1,128)} %broadcast_in_dim.8), calls=%async_computation | async-start | bytes 32768 | tf_op jit(solution)/shard_map/all_to_all | solution.py:246
  67.5 10.0 %collective-permute-start.6 = (f32[3,64,64]{1,2,0:T(8,128)S(1)}, f32[3,64,64]{1,2,0:T(8,128)S(1)}, u32[]{:S(2)}, u32[]{:S(2)}) collective-permute-start(f32[3,64,64]{1,2,0:T(8,128)S(1)} %convolution_bitcast_fusion), channel_id=1, source_target_pairs={{0,3},{1,0},{2,1},{3,2},{4,7},{5,4},{6,5},{7,6},{8,11},{9,8},{10,9... | collective-permute-start | bytes 147464 | tf_op jit(solution)/shard_map/ppermute | solution.py:236
  71.5 9.2 %collective-permute-start.5 = (f32[3,64,64]{1,2,0:T(8,128)S(1)}, f32[3,64,64]{1,2,0:T(8,128)S(1)}, u32[]{:S(2)}, u32[]{:S(2)}) collective-permute-start(f32[3,64,64]{1,2,0:T(8,128)S(1)} %convolution_bitcast_fusion.1), channel_id=1, source_target_pairs={{0,2},{1,3},{2,0},{3,1},{4,6},{5,7},{6,4},{7,5},{8,10},{9,11},{10,... | collective-permute-start | bytes 147464 | tf_op jit(solution)/shard_map/ppermute | solution.py:236
  71.8 8.8 %collective-permute-start.4 = (f32[3,64,64]{1,2,0:T(8,128)S(1)}, f32[3,64,64]{1,2,0:T(8,128)S(1)}, u32[]{:S(2)}, u32[]{:S(2)}) collective-permute-start(f32[3,64,64]{1,2,0:T(8,128)S(1)} %convolution_bitcast_fusion.2), channel_id=1, source_target_pairs={{0,1},{1,2},{2,3},{3,0},{4,5},{5,6},{6,7},{7,4},{8,9},{9,10},{10,1... | collective-permute-start | bytes 147464 | tf_op jit(solution)/shard_map/ppermute | solution.py:236

commit v8 on v7

--- a/solution.py
+++ b/solution.py
@@ -62,7 +62,7 @@
     atom_count = rows_per_block * LANES
     tile_count = atom_count // TILE
     cand_tiles = 5 * tile_count
-    pair_cap = near_ref.shape[0]
+    pair_cap = near_ref.shape[-1]
     sublane = lax.broadcasted_iota(jnp.int32, (8, LANES), 0)
     left_rows = lax.broadcasted_iota(jnp.int32, (8, LANES), 1) < TILE
     shifts = ((0.0, 0.0), (-TX * cell_edge, 0.0), (TX * cell_edge, 0.0),
@@ -87,7 +87,7 @@
             column = home_ref[r * chunk:(r + 1) * chunk, q:q + 1]
             spread_ref[q, r * chunk:(r + 1) * chunk, :] = jnp.broadcast_to(column, (chunk, LANES))
     acc_ref[...] = jnp.zeros(acc_ref.shape, jnp.float32)
-    total = count_ref[0]
+    total = count_ref[0, 0]
     lane = lax.broadcasted_iota(jnp.int32, (1, LANES), 1)
     left = lane < TILE
     lane_full = lax.broadcasted_iota(jnp.int32, (TILE, LANES), 1)
@@ -100,10 +100,10 @@
         has_first = (first < total).astype(jnp.float32)
         has_second = (first + 1 < total).astype(jnp.float32)
         first = jnp.minimum(first, pair_cap - 1)
-        home_a = jnp.clip(near_ref[first], 0, tile_count - 1)
-        cand_a = jnp.clip(far_ref[first], 0, cand_tiles - 1)
-        home_b = jnp.clip(near_ref[second], 0, tile_count - 1)
-        cand_b = jnp.clip(far_ref[second], 0, cand_tiles - 1)
+        home_a = jnp.clip(near_ref[0, 0, first], 0, tile_count - 1)
+        cand_a = jnp.clip(far_ref[0, 0, first], 0, cand_tiles - 1)
+        home_b = jnp.clip(near_ref[0, 0, second], 0, tile_count - 1)
+        cand_b = jnp.clip(far_ref[0, 0, second], 0, cand_tiles - 1)
         rows = jnp.where(left, cand_ref[cand_a] * has_first, cand_ref[cand_b] * has_second)
         base_a = pl.multiple_of(home_a * TILE, TILE)
         base_b = pl.multiple_of(home_b * TILE, TILE)
@@ -138,12 +138,12 @@
             pltpu.store(slot_b, slot_b[...] + contribution, mask=right_full)
 
     def body(k, carry):
-        parts = [pair_kernel(8 * k + 2 * u) for u in range(4)]
+        parts = [pair_kernel(16 * k + 2 * u) for u in range(8)]
         for part in parts:
             accumulate(*part)
         return carry
 
-    lax.fori_loop(0, (total + 7) // 8, body, 0)
+    lax.fori_loop(0, (total + 15) // 16, body, 0)
     ones = jnp.ones((8, LANES), jnp.float32)
     for c in range(2):
         summed = lax.dot_general(
@@ -210,10 +210,7 @@
     home_cols = packed.T
     packed = packed.reshape(8, atom_count // LANES, LANES).transpose(1, 0, 2)
     blocks = neighbours(packed)
-    near_list = pair_tiles.reshape(-1)
-    far_list = pair_cands.reshape(-1)
-    pair_total = pair_count.reshape(1)
-    totals = sweep(home_cols, blocks, near_list, far_list, pair_total)
+    totals = sweep(home_cols, blocks, pair_tiles, pair_cands, pair_count)
     aux_field = totals[0].reshape(atom_count)
     resid_field = totals[1].reshape(atom_count)
     field = negativity + aux_field + resid_field

time: 82.6 us -> 79.7 us (0.965)
  starting transfers between devices: 42.6 us -> 40.3 us
  other arithmetic: 7.68 us -> 6.27 us
  Pallas kernels: 16.1 us -> 17 us
    all_to_all x1, starting transfers between devices: 30 us -> 27.6 us  [on_device(): lax.all_to_all(sums_out, ('brick', 'plane'), split_axis=0, concat_axis=0,...]
    unnamed x3 -> x1, other arithmetic: 2.71 us -> 1.28 us
    pallas_call x1, Pallas kernels: 16.1 us -> 17 us  [sweep(): pl.pallas_call(sweep_kernel, out_shape=jax.ShapeDtypeStruct((2, atom_coun...]
  transfers between devices with their start and end apart: 8 -> 8, of which waited for: 2 -> 2; matrix products, arithmetic and copies ran while one was open for 10% -> 8% of each run, Pallas kernels for 0% -> 0%
where the time goes in v8:
time: 79.7 us; the launch traced here: 79.1 us
  starting transfers between devices  40.3 us (51%)
  Pallas kernels  17 us (21%)
  local copies, waits for them, and re-layouts  6.56 us (8%)
  other arithmetic  6.27 us (8%)
  waiting for transfers between devices  4.43 us (6%)
  between operations  3.54 us (4%)
  matrix products  1 us (1%)
    all_to_all x1, starting transfers between devices, on_device(): lax.all_to_all(sums_out, ('brick', 'plane'), split_axis=0, concat_axis=0,...  27.6 us
    pallas_call x1, Pallas kernels, sweep(): pl.pallas_call(sweep_kernel, out_shape=jax.ShapeDtypeStruct((2, atom_coun...  17 us
    ppermute x4, starting transfers between devices, shifted_from(): return lax.ppermute(block, axis, pairs)  7.78 us
    ppermute x3, starting transfers between devices, to_owners(): lax.ppermute(part, 'plane', [(i, (i + step) % planes) for i in range(plan...  4.86 us
    concatenate x4, local copies, waits for them, and re-layouts, on_device(): jnp.concatenate([positions.reshape(3, atom_count), jnp.square(radius)[Non...  3.15 us
    ppermute x3, waiting for transfers between devices, to_owners(): lax.ppermute(part, 'plane', [(i, (i + step) % planes) for i in range(plan...  3.07 us
    another operation x1, other arithmetic, on_device(): jnp.stack([jnp.sum(charge_row), jnp.sum(field / hardness_row), jnp.sum(1....  2.01 us
  transfers between devices with their start and end apart: 8, of which 2 were waited for; matrix products, arithmetic and copies ran while one was open for 8% of the time, Pallas kernels for 0%

profile of v8, /device:TPU:0, one launch (start us, length us, event | category | flops | bytes accessed | tf_op | source)
XLA Modules:
  0.0 79.1 jit_solution(9135798318838848434)
XLA Ops:
  0.7 0.9 %select_reduce_fusion.2 = (f32[4096]{0:T(1024)S(1)}, f32[4096]{0:T(1024)S(1)}, f32[4096]{0:T(1024)S(1)}) fusion(f32[8]{0:T(128)} %param.21, s32[4096]{0:T(1024)} %bitcast.86, f32[8]{0:T(128)} %param.22, f32[8]{0:T(128)} %param.23), kind=kLoop, calls=%fused_computation.9 | loop fusion | flops 217088 | bytes 65632 | tf_op jit(solution)/shard_map/reduce_sum | solution.py:41
  1.6 0.8 %copy.42 = f32[3,32,128]{2,0,1:T(4,128)S(1)} copy(f32[3,32,128]{2,1,0:T(8,128)} %bitcast.77) | data formatting | bytes 98304 | tf_op jit(solution)/shard_map/concatenate | solution.py:200
  2.5 0.9 %concatenate.17 = f32[8,32,128]{2,0,1:T(8,128)S(1)} concatenate(f32[3,32,128]{2,0,1:T(4,128)S(1)} %copy.42, f32[1,32,128]{2,0,1:T(1,128)S(1)} %bitcast.78, f32[1,32,128]{2,0,1:T(1,128)} %bitcast.80, f32[1,32,128]{2,0,1:T(1,128)} %bitcast.82, f32[2,32,128]{2,0,1:T(2,128)S(1)} %broadcast_in_dim.7), dimensions={0} | concatenate | bytes 262144 | tf_op jit(solution)/shard_map/concatenate | solution.py:200
  3.3 0.5 collective-permute-start
  3.9 2.9 %collective-permute-start.1 = (f32[32,8,128]{2,1,0:T(8,128)S(1)}, f32[32,8,128]{2,1,0:T(8,128)S(1)}, u32[]{:S(2)}, u32[]{:S(2)}) collective-permute-start(f32[32,8,128]{2,1,0:T(8,128)S(1)} %bitcast.69), channel_id=1, source_target_pairs={{0,28},{4,0},{8,4},{12,8},{16,12},{20,16},{24,20},{28,24},{1,29},{... | collective-permute-start | bytes 393224 | tf_op jit(solution)/shard_map/ppermute | solution.py:24
  6.8 2.3 %collective-permute-start.2 = (f32[32,8,128]{2,1,0:T(8,128)S(1)}, f32[32,8,128]{2,1,0:T(8,128)S(1)}, u32[]{:S(2)}, u32[]{:S(2)}) collective-permute-start(f32[32,8,128]{2,1,0:T(8,128)S(1)} %bitcast.70), channel_id=1, source_target_pairs={{0,1},{1,2},{2,3},{3,0},{4,5},{5,6},{6,7},{7,4},{8,9},{9,10},{10,1... | collective-permute-start | bytes 393224 | tf_op jit(solution)/shard_map/ppermute | solution.py:24
  9.1 2.0 %collective-permute-start.3 = (f32[32,8,128]{2,1,0:T(8,128)S(1)}, f32[32,8,128]{2,1,0:T(8,128)S(1)}, u32[]{:S(2)}, u32[]{:S(2)}) collective-permute-start(f32[32,8,128]{2,1,0:T(8,128)S(1)} %bitcast.71), channel_id=1, source_target_pairs={{0,3},{1,0},{2,1},{3,2},{4,7},{5,4},{6,5},{7,6},{8,11},{9,8},{10,9... | collective-permute-start | bytes 393224 | tf_op jit(solution)/shard_map/ppermute | solution.py:24
  11.1 0.8 %copy.55 = f32[1,1,3,4096]{3,2,1,0:T(4,128)S(1)} copy(f32[1,1,3,4096]{3,1,2,0:T(1,128)} %param.12) | data formatting | bytes 98304
  12.6 0.9 %concatenate.13 = f32[8,4096]{1,0:T(8,128)S(1)} concatenate(f32[3,4096]{1,0:T(4,128)S(1)} %bitcast.73, f32[1,4096]{1,0:T(1,128)S(1)} %bitcast.79, f32[1,4096]{1,0:T(1,128)} %bitcast.81, f32[1,4096]{1,0:T(1,128)} %bitcast.83, f32[2,4096]{1,0:T(2,128)S(1)} %broadcast_in_dim.6), dimensions={0} | concatenate | bytes 262144 | tf_op jit(solution)/shard_map/concatenate | solution.py:200
  13.5 0.6 copy.41
  14.1 0.5 broadcast.94
  14.6 1.3 %fusion.25 = (f32[4096]{0:T(1024)S(1)}, f32[]{:T(128)}) fusion(f32[1,1,4096]{2,1,0:T(1,128)S(1)} %copy-done.2, f32[]{:T(128)} %broadcast.94), kind=kLoop, calls=%fused_computation.51 | loop fusion | flops 4095 | bytes 32776 | tf_op args[1]
  16.1 0.1 copy.44
  16.3 17.0 %shard_map.139 = f32[2,4096]{1,0:T(2,128)S(1)} custom-call(s32[1,1,1496]{2,1,0:T(1,128)S(1)} %copy-done, s32[1,1,1496]{2,1,0:T(1,128)S(1)} %copy-done.1, s32[1,1]{1,0:T(1,128)S(6)} %copy.56.count_ref, f32[4096,8]{1,0:T(8,128)S(1)} %bitcast.67, f32[32,8,128]{2,1,0:T(8,128)S(1)} %bitcast.72, f32[32,8,128]{2,1,0:T(8,128)S(1)} %collective-permute-done.refs_1_, ...), custom_call_target="tpu_custom_call" | custom-call | tf_op jit(solution)/shard_map/pallas_call | solution.py:164
  33.3 0.1 add_reduce_fusion
  33.4 0.6 fusion.20
  34.0 2.0 %select_maximum_fusion = f32[8]{0:T(128)S(1)} fusion(f32[1]{0:T(128)} %bitcast.14, f32[1]{0:T(128)} %bitcast.13, f32[1]{0:T(128)} %bitcast), kind=kLoop, calls=%fused_computation.39 | loop fusion | flops 48 | bytes 44 | tf_op jit(solution)/shard_map/stack | solution.py:239
  36.1 0.6 broadcast_in_dim.8
  36.7 27.6 %all-to-all-start = ((f32[32,1,8]{2,1,0:T(1,128)}), f32[32,1,8]{2,1,0:T(1,128)S(1)}, u32[]{:S(2)}, u32[]{:S(2)}) async-start(f32[32,1,8]{2,1,0:T(1,128)} %broadcast_in_dim.8), calls=%async_computation | async-start | bytes 32768 | tf_op jit(solution)/shard_map/all_to_all | solution.py:243
  64.5 0.3 convolution_bitcast_fusion
  64.7 3.7 %collective-permute-start.6 = (f32[3,64,64]{1,2,0:T(8,128)S(1)}, f32[3,64,64]{1,2,0:T(8,128)S(1)}, u32[]{:S(2)}, u32[]{:S(2)}) collective-permute-start(f32[3,64,64]{1,2,0:T(8,128)S(1)} %convolution_bitcast_fusion), channel_id=1, source_target_pairs={{0,3},{1,0},{2,1},{3,2},{4,7},{5,4},{6,5},{7,6},{8,11},{9,8},{10,9... | collective-permute-start | bytes 147464 | tf_op jit(solution)/shard_map/ppermute | solution.py:233
  68.4 0.2 convolution_bitcast_fusion.1
  68.7 0.2 convolution_bitcast_fusion.2
  69.0 1.1 %collective-permute-start.4 = (f32[3,64,64]{1,2,0:T(8,128)S(1)}, f32[3,64,64]{1,2,0:T(8,128)S(1)}, u32[]{:S(2)}, u32[]{:S(2)}) collective-permute-start(f32[3,64,64]{1,2,0:T(8,128)S(1)} %convolution_bitcast_fusion.2), channel_id=1, source_target_pairs={{0,1},{1,2},{2,3},{3,0},{4,5},{5,6},{6,7},{7,4},{8,9},{9,10},{10,1... | collective-permute-start | bytes 147464 | tf_op jit(solution)/shard_map/ppermute | solution.py:233
  70.1 1.4 %all-to-all-done = f32[32,1,8]{2,1,0:T(1,128)S(1)} async-done(((f32[32,1,8]{2,1,0:T(1,128)}), f32[32,1,8]{2,1,0:T(1,128)S(1)}, u32[]{:S(2)}, u32[]{:S(2)}) %all-to-all-start) | async-done | bytes 1056 | tf_op jit(solution)/shard_map/all_to_all | solution.py:243
  71.5 0.6 fusion.26
  74.1 0.6 fusion.15
  74.7 3.1 %collective-permute-done.5 = f32[3,64,64]{1,2,0:T(8,128)S(1)} collective-permute-done((f32[3,64,64]{1,2,0:T(8,128)S(1)}, f32[3,64,64]{1,2,0:T(8,128)S(1)}, u32[]{:S(2)}, u32[]{:S(2)}) %collective-permute-start.5) | collective-permute-done | bytes 49184 | tf_op jit(solution)/shard_map/ppermute | solution.py:233
  77.8 0.3 fusion.2
  78.1 0.1 mul.83
  78.3 0.1 mul.80
  78.4 0.6 subtract_add_fusion
  (30 shorter events, 0.7 us)
Async XLA Ops:
  0.6 14.0 %copy-start.2 = (f32[1,1,4096]{2,1,0:T(1,128)S(1)}, f32[1,1,4096]{2,1,0:T(1,128)}, u32[]{:S(2)}) copy-start(f32[1,1,4096]{2,1,0:T(1,128)} %param.13) | copy-start | bytes 49156
  0.6 15.6 %copy-start.4 = (s32[1,1,64]{2,1,0:T(1,128)S(1)}, s32[1,1,64]{2,1,0:T(1,128)}, u32[]{:S(2)}) copy-start(s32[1,1,64]{2,1,0:T(1,128)} %param.20) | copy-start | bytes 772
  0.7 15.6 %copy-start = (s32[1,1,1496]{2,1,0:T(1,128)S(1)}, s32[1,1,1496]{2,1,0:T(1,128)}, u32[]{:S(2)}) copy-start(s32[1,1,1496]{2,1,0:T(1,128)} %near_ref.1) | copy-start | bytes 17956
  0.7 15.6 %copy-start.1 = (s32[1,1,1496]{2,1,0:T(1,128)S(1)}, s32[1,1,1496]{2,1,0:T(1,128)}, u32[]{:S(2)}) copy-start(s32[1,1,1496]{2,1,0:T(1,128)} %far_ref.1) | copy-start | bytes 17956
  3.3 12.9 %collective-permute-start = (f32[32,8,128]{2,1,0:T(8,128)S(1)}, f32[32,8,128]{2,1,0:T(8,128)S(1)}, u32[]{:S(2)}, u32[]{:S(2)}) collective-permute-start(f32[32,8,128]{2,1,0:T(8,128)S(1)} %bitcast.68), channel_id=1, source_target_pairs={{0,4},{4,8},{8,12},{12,16},{16,20},{20,24},{24,28},{28,0},{1,5},{5... | collective-permute-start | bytes 393224 | tf_op jit(solution)/shard_map/ppermute | solution.py:24
  3.9 12.4 %collective-permute-start.1 = (f32[32,8,128]{2,1,0:T(8,128)S(1)}, f32[32,8,128]{2,1,0:T(8,128)S(1)}, u32[]{:S(2)}, u32[]{:S(2)}) collective-permute-start(f32[32,8,128]{2,1,0:T(8,128)S(1)} %bitcast.69), channel_id=1, source_target_pairs={{0,28},{4,0},{8,4},{12,8},{16,12},{20,16},{24,20},{28,24},{1,29},{... | collective-permute-start | bytes 393224 | tf_op jit(solution)/shard_map/ppermute | solution.py:24
  6.8 9.5 %collective-permute-start.2 = (f32[32,8,128]{2,1,0:T(8,128)S(1)}, f32[32,8,128]{2,1,0:T(8,128)S(1)}, u32[]{:S(2)}, u32[]{:S(2)}) collective-permute-start(f32[32,8,128]{2,1,0:T(8,128)S(1)} %bitcast.70), channel_id=1, source_target_pairs={{0,1},{1,2},{2,3},{3,0},{4,5},{5,6},{6,7},{7,4},{8,9},{9,10},{10,1... | collective-permute-start | bytes 393224 | tf_op jit(solution)/shard_map/ppermute | solution.py:24
  9.1 7.2 %collective-permute-start.3 = (f32[32,8,128]{2,1,0:T(8,128)S(1)}, f32[32,8,128]{2,1,0:T(8,128)S(1)}, u32[]{:S(2)}, u32[]{:S(2)}) collective-permute-start(f32[32,8,128]{2,1,0:T(8,128)S(1)} %bitcast.71), channel_id=1, source_target_pairs={{0,3},{1,0},{2,1},{3,2},{4,7},{5,4},{6,5},{7,6},{8,11},{9,8},{10,9... | collective-permute-start | bytes 393224 | tf_op jit(solution)/shard_map/ppermute | solution.py:24
  16.3 62.1 %copy-start.3 = (f32[1,1,4096]{2,1,0:T(1,128)S(1)}, f32[1,1,4096]{2,1,0:T(1,128)}, u32[]{:S(2)}) copy-start(f32[1,1,4096]{2,1,0:T(1,128)} %param.14) | copy-start | bytes 49156
  36.7 34.8 %all-to-all-start = ((f32[32,1,8]{2,1,0:T(1,128)}), f32[32,1,8]{2,1,0:T(1,128)S(1)}, u32[]{:S(2)}, u32[]{:S(2)}) async-start(f32[32,1,8]{2,1,0:T(1,128)} %broadcast_in_dim.8), calls=%async_computation | async-start | bytes 32768 | tf_op jit(solution)/shard_map/all_to_all | solution.py:243
  64.7 10.0 %collective-permute-start.6 = (f32[3,64,64]{1,2,0:T(8,128)S(1)}, f32[3,64,64]{1,2,0:T(8,128)S(1)}, u32[]{:S(2)}, u32[]{:S(2)}) collective-permute-start(f32[3,64,64]{1,2,0:T(8,128)S(1)} %convolution_bitcast_fusion), channel_id=1, source_target_pairs={{0,3},{1,0},{2,1},{3,2},{4,7},{5,4},{6,5},{7,6},{8,11},{9,8},{10,9... | collective-permute-start | bytes 147464 | tf_op jit(solution)/shard_map/ppermute | solution.py:233
  68.6 9.1 %collective-permute-start.5 = (f32[3,64,64]{1,2,0:T(8,128)S(1)}, f32[3,64,64]{1,2,0:T(8,128)S(1)}, u32[]{:S(2)}, u32[]{:S(2)}) collective-permute-start(f32[3,64,64]{1,2,0:T(8,128)S(1)} %convolution_bitcast_fusion.1), channel_id=1, source_target_pairs={{0,2},{1,3},{2,0},{3,1},{4,6},{5,7},{6,4},{7,5},{8,10},{9,11},{10,... | collective-permute-start | bytes 147464 | tf_op jit(solution)/shard_map/ppermute | solution.py:233
  69.0 8.8 %collective-permute-start.4 = (f32[3,64,64]{1,2,0:T(8,128)S(1)}, f32[3,64,64]{1,2,0:T(8,128)S(1)}, u32[]{:S(2)}, u32[]{:S(2)}) collective-permute-start(f32[3,64,64]{1,2,0:T(8,128)S(1)} %convolution_bitcast_fusion.2), channel_id=1, source_target_pairs={{0,1},{1,2},{2,3},{3,0},{4,5},{5,6},{6,7},{7,4},{8,9},{9,10},{10,1... | collective-permute-start | bytes 147464 | tf_op jit(solution)/shard_map/ppermute | solution.py:233

commit v9 on v8

--- a/solution.py
+++ b/solution.py
@@ -55,9 +55,9 @@
 LANES = 128
 
 
-def sweep_kernel(near_ref, far_ref, count_ref, home_ref, *refs):
+def sweep_kernel(near_ref, far_ref, count_ref, home_ref, chi_ref, eta_ref, *refs):
     block_refs = refs[:5]
-    out_ref, cand_ref, spread_ref, acc_ref = refs[5:]
+    out_ref, sum_ref, cand_ref, spread_ref, acc_ref = refs[5:]
     rows_per_block = block_refs[0].shape[0]
     atom_count = rows_per_block * LANES
     tile_count = atom_count // TILE
@@ -145,6 +145,7 @@
 
     lax.fori_loop(0, (total + 15) // 16, body, 0)
     ones = jnp.ones((8, LANES), jnp.float32)
+    fields = []
     for c in range(2):
         summed = lax.dot_general(
             ones,
@@ -153,26 +154,33 @@
             precision=lax.Precision.HIGHEST,
             preferred_element_type=jnp.float32,
         )
-        out_ref[c:c + 1, :] = summed[0:1]
-
-
-def sweep(home_cols, blocks, near_list, far_list, pair_total):
+        fields.append(summed[0:1])
+    field = chi_ref[...] + fields[0] + fields[1]
+    out_ref[0:1, :] = field
+    out_ref[1:2, :] = fields[1]
+    sum_ref[...] = jnp.broadcast_to(jnp.sum(field / eta_ref[...]), sum_ref.shape)
+
+
+def sweep(home_cols, chi, eta, blocks, near_list, far_list, pair_total):
     rows_per_block = blocks[0].shape[0]
     atom_count = rows_per_block * LANES
     smem = pl.BlockSpec(memory_space=pltpu.SMEM)
     vmem = pl.BlockSpec(memory_space=pltpu.VMEM)
     return pl.pallas_call(
         sweep_kernel,
-        out_shape=jax.ShapeDtypeStruct((2, atom_count), jnp.float32),
-        in_specs=[smem, smem, smem] + [vmem] * 6,
-        out_specs=vmem,
+        out_shape=(
+            jax.ShapeDtypeStruct((2, atom_count), jnp.float32),
+            jax.ShapeDtypeStruct((1, LANES), jnp.float32),
+        ),
+        in_specs=[smem, smem, smem] + [vmem] * 8,
+        out_specs=(vmem, vmem),
         scratch_shapes=[
             pltpu.VMEM((10 * rows_per_block, 8, LANES), jnp.float32),
             pltpu.VMEM((4, atom_count, LANES), jnp.float32),
             pltpu.VMEM((2, atom_count, LANES), jnp.float32),
         ],
         compiler_params=pltpu.CompilerParams(vmem_limit_bytes=48 * 1024 * 1024),
-    )(near_list, far_list, pair_total, home_cols, *blocks)
+    )(near_list, far_list, pair_total, home_cols, chi, eta, *blocks)
 
 
 def on_device(
@@ -207,13 +215,20 @@
         ],
         axis=0,
     )
-    home_cols = packed.T
     packed = packed.reshape(8, atom_count // LANES, LANES).transpose(1, 0, 2)
+    home_cols = packed.transpose(0, 2, 1).reshape(atom_count, 8)
     blocks = neighbours(packed)
-    totals = sweep(home_cols, blocks, pair_tiles, pair_cands, pair_count)
-    aux_field = totals[0].reshape(atom_count)
-    resid_field = totals[1].reshape(atom_count)
-    field = negativity + aux_field + resid_field
+    totals, field_sum = sweep(
+        home_cols,
+        negativity[None],
+        hardness_row[None],
+        blocks,
+        pair_tiles,
+        pair_cands,
+        pair_count,
+    )
+    field = totals[0]
+    resid_field = totals[1]
     planes = lax.axis_size("plane")
     devices = lax.axis_size("brick") * planes
     target = owner_tile.reshape(tile_count)
@@ -237,7 +252,7 @@
         return total
 
     local_sums = jnp.stack(
-        [jnp.sum(charge_row), jnp.sum(field / hardness_row), jnp.sum(1.0 / hardness_row)]
+        [jnp.sum(charge_row), field_sum[0, 0], jnp.sum(1.0 / hardness_row)]
     )
     sums_out = jnp.broadcast_to(jnp.pad(local_sums, (0, 5))[None, :], (devices, 8))
     sums_in = lax.all_to_all(sums_out, ("brick", "plane"), split_axis=0, concat_axis=0, tiled=True)

time: 79.7 us -> 79.1 us (level)
  Pallas kernels: 17 us -> 14.4 us
  starting transfers between devices: 40.3 us -> 42.8 us
  local copies, waits for them, and re-layouts: 6.56 us -> 5.55 us
    pallas_call x1, Pallas kernels: 17 us -> 14.4 us  [sweep(): pl.pallas_call(sweep_kernel, out_shape=(jax.ShapeDtypeStruct((2, atom_cou...]
    all_to_all x1, starting transfers between devices: 27.6 us -> 30.1 us  [on_device(): lax.all_to_all(sums_out, ('brick', 'plane'), split_axis=0, concat_axis=0,...]
    concatenate x4 -> x2, local copies, waits for them, and re-layouts: 3.15 us -> 1.71 us  [on_device(): jnp.concatenate([positions.reshape(3, atom_count), jnp.square(radius)[Non...]
    unnamed x12 -> x7, local copies, waits for them, and re-layouts: 1.39 us -> 0.53 us
  transfers between devices with their start and end apart: 8 -> 8, of which waited for: 2 -> 2; matrix products, arithmetic and copies ran while one was open for 8% -> 10% of each run, Pallas kernels for 0% -> 0%
where the time goes in v9:
time: 79.1 us; the launch traced here: 78.4 us
  starting transfers between devices  42.8 us (54%)
  Pallas kernels  14.4 us (18%)
  other arithmetic  6.9 us (9%)
  local copies, waits for them, and re-layouts  5.55 us (7%)
  waiting for transfers between devices  4.31 us (5%)
  between operations  3.49 us (4%)
  matrix products  0.99 us (1%)
    all_to_all x1, starting transfers between devices, on_device(): lax.all_to_all(sums_out, ('brick', 'plane'), split_axis=0, concat_axis=0,...  30.1 us
    pallas_call x1, Pallas kernels, sweep(): pl.pallas_call(sweep_kernel, out_shape=(jax.ShapeDtypeStruct((2, atom_cou...  14.4 us
    ppermute x4, starting transfers between devices, shifted_from(): return lax.ppermute(block, axis, pairs)  7.78 us
    ppermute x3, starting transfers between devices, to_owners(): lax.ppermute(part, 'plane', [(i, (i + step) % planes) for i in range(plan...  4.86 us
    ppermute x3, waiting for transfers between devices, to_owners(): lax.ppermute(part, 'plane', [(i, (i + step) % planes) for i in range(plan...  3.5 us
    unnamed x1, other arithmetic  2.01 us
    concatenate x2, local copies, waits for them, and re-layouts, on_device(): jnp.concatenate([positions.reshape(3, atom_count), jnp.square(radius)[Non...  1.71 us
  transfers between devices with their start and end apart: 8, of which 2 were waited for; matrix products, arithmetic and copies ran while one was open for 10% of the time, Pallas kernels for 0%

profile of v9, /device:TPU:0, one launch (start us, length us, event | category | flops | bytes accessed | tf_op | source)
XLA Modules:
  0.0 78.4 jit_solution(191592899918372836)
XLA Ops:
  0.7 0.8 %copy.30 = f32[3,32,128]{2,0,1:T(4,128)S(1)} copy(f32[3,32,128]{2,1,0:T(8,128)} %bitcast.67) | data formatting | bytes 98304 | tf_op jit(solution)/shard_map/concatenate | solution.py:208
  1.5 0.9 %select_reduce_fusion.1 = (f32[4096]{0:T(1024)S(1)}, f32[4096]{0:T(1024)S(1)}, f32[4096]{0:T(1024)S(1)}) fusion(f32[8]{0:T(128)} %param.21, s32[4096]{0:T(1024)} %bitcast.69, f32[8]{0:T(128)} %param.22, f32[8]{0:T(128)} %param.23), kind=kLoop, calls=%fused_computation.8 | loop fusion | flops 217088 | bytes 65632 | tf_op jit(solution)/shard_map/reduce_sum | solution.py:41
  2.4 0.9 %concatenate.14 = f32[8,32,128]{2,0,1:T(8,128)S(1)} concatenate(f32[3,32,128]{2,0,1:T(4,128)S(1)} %copy.30, f32[1,32,128]{2,0,1:T(1,128)S(1)} %bitcast.65, f32[1,32,128]{2,0,1:T(1,128)} %bitcast.66, f32[1,32,128]{2,0,1:T(1,128)} %bitcast.68, f32[2,32,128]{2,0,1:T(2,128)S(1)} %broadcast_in_dim.8), dimensions={0} | concatenate | bytes 262144 | tf_op jit(solution)/shard_map/concatenate | solution.py:208
  3.3 0.5 collective-permute-start
  3.8 2.9 %collective-permute-start.1 = (f32[32,8,128]{2,1,0:T(8,128)S(1)}, f32[32,8,128]{2,1,0:T(8,128)S(1)}, u32[]{:S(2)}, u32[]{:S(2)}) collective-permute-start(f32[32,8,128]{2,1,0:T(8,128)S(1)} %bitcast.56), channel_id=1, source_target_pairs={{0,28},{4,0},{8,4},{12,8},{16,12},{20,16},{24,20},{28,24},{1,29},{... | collective-permute-start | bytes 393224 | tf_op jit(solution)/shard_map/ppermute | solution.py:24
  6.8 2.3 %collective-permute-start.2 = (f32[32,8,128]{2,1,0:T(8,128)S(1)}, f32[32,8,128]{2,1,0:T(8,128)S(1)}, u32[]{:S(2)}, u32[]{:S(2)}) collective-permute-start(f32[32,8,128]{2,1,0:T(8,128)S(1)} %bitcast.57), channel_id=1, source_target_pairs={{0,1},{1,2},{2,3},{3,0},{4,5},{5,6},{6,7},{7,4},{8,9},{9,10},{10,1... | collective-permute-start | bytes 393224 | tf_op jit(solution)/shard_map/ppermute | solution.py:24
  9.0 2.0 %collective-permute-start.3 = (f32[32,8,128]{2,1,0:T(8,128)S(1)}, f32[32,8,128]{2,1,0:T(8,128)S(1)}, u32[]{:S(2)}, u32[]{:S(2)}) collective-permute-start(f32[32,8,128]{2,1,0:T(8,128)S(1)} %bitcast.58), channel_id=1, source_target_pairs={{0,3},{1,0},{2,1},{3,2},{4,7},{5,4},{6,5},{7,6},{8,11},{9,8},{10,9... | collective-permute-start | bytes 393224 | tf_op jit(solution)/shard_map/ppermute | solution.py:24
  11.1 0.7 subtract_bitcast_fusion.3
  11.7 0.5 broadcast.95
  12.2 2.0 %fusion.21 = (f32[4096]{0:T(1024)S(1)}, f32[]{:T(128)}) fusion(f32[1,1,4096]{2,1,0:T(1,128)} %param.13, f32[]{:T(128)} %broadcast.95), kind=kLoop, calls=%fused_computation.45 | loop fusion | flops 4095 | bytes 32776 | tf_op args[1]
  14.9 0.6 copy.31.home_ref
  15.6 0.1 copy.34
  15.7 0.1 stack.22
  15.8 0.6 divide_reduce_fusion
  16.5 14.4 %shard_map.139 = (f32[2,4096]{1,0:T(2,128)S(1)}, f32[1,128]{1,0:T(1,128)S(1)}) custom-call(s32[1,1,1496]{2,1,0:T(1,128)S(1)} %copy-done, s32[1,1,1496]{2,1,0:T(1,128)S(1)} %copy-done.1, s32[1,1]{1,0:T(1,128)S(6)} %copy.42.count_ref, f32[4096,8]{1,0:T(8,128)S(1)} %copy.31.home_ref, f32[1,4096]{1,0:T(1,128)S(1)} %bitcast.63, f32[1,4096]{1,0:T(1,128)S(1)} %bitcast.61, ...), custom_call_target="tpu_custom_call" | custom-call | tf_op jit(solution)/shard_map/pallas_call | solution.py:169
  30.9 1.4 %select_maximum_fusion = f32[8]{0:T(128)S(1)} fusion(f32[1]{0:T(128)} %bitcast.12, f32[1]{0:T(128)S(1)} %bitcast.64, f32[1]{0:T(128)} %bitcast), kind=kLoop, calls=%fused_computation.34 | loop fusion | flops 48 | bytes 44 | tf_op jit(solution)/shard_map/stack | solution.py:254
  32.3 0.6 broadcast_in_dim.11
  32.9 30.1 %all-to-all-start = ((f32[32,1,8]{2,1,0:T(1,128)}), f32[32,1,8]{2,1,0:T(1,128)S(1)}, u32[]{:S(2)}, u32[]{:S(2)}) async-start(f32[32,1,8]{2,1,0:T(1,128)} %broadcast_in_dim.11), calls=%async_computation | async-start | bytes 32768 | tf_op jit(solution)/shard_map/all_to_all | solution.py:258
  63.1 0.6 slice_bitcast_fusion
  63.9 0.3 convolution_bitcast_fusion
  64.1 3.7 %collective-permute-start.6 = (f32[3,64,64]{1,2,0:T(8,128)S(1)}, f32[3,64,64]{1,2,0:T(8,128)S(1)}, u32[]{:S(2)}, u32[]{:S(2)}) collective-permute-start(f32[3,64,64]{1,2,0:T(8,128)S(1)} %convolution_bitcast_fusion), channel_id=1, source_target_pairs={{0,3},{1,0},{2,1},{3,2},{4,7},{5,4},{6,5},{7,6},{8,11},{9,8},{10,9... | collective-permute-start | bytes 147464 | tf_op jit(solution)/shard_map/ppermute | solution.py:248
  67.8 0.2 convolution_bitcast_fusion.1
  68.1 0.2 convolution_bitcast_fusion.2
  68.4 1.1 %collective-permute-start.4 = (f32[3,64,64]{1,2,0:T(8,128)S(1)}, f32[3,64,64]{1,2,0:T(8,128)S(1)}, u32[]{:S(2)}, u32[]{:S(2)}) collective-permute-start(f32[3,64,64]{1,2,0:T(8,128)S(1)} %convolution_bitcast_fusion.2), channel_id=1, source_target_pairs={{0,1},{1,2},{2,3},{3,0},{4,5},{5,6},{6,7},{7,4},{8,9},{9,10},{10,1... | collective-permute-start | bytes 147464 | tf_op jit(solution)/shard_map/ppermute | solution.py:248
  69.5 0.8 %all-to-all-done = f32[32,1,8]{2,1,0:T(1,128)S(1)} async-done(((f32[32,1,8]{2,1,0:T(1,128)}), f32[32,1,8]{2,1,0:T(1,128)S(1)}, u32[]{:S(2)}, u32[]{:S(2)}) %all-to-all-start) | async-done | bytes 1056 | tf_op jit(solution)/shard_map/all_to_all | solution.py:258
  70.3 0.7 fusion.22
  73.0 0.6 bitcast_divide_fusion
  73.7 3.5 %collective-permute-done.5 = f32[3,64,64]{1,2,0:T(8,128)S(1)} collective-permute-done((f32[3,64,64]{1,2,0:T(8,128)S(1)}, f32[3,64,64]{1,2,0:T(8,128)S(1)}, u32[]{:S(2)}, u32[]{:S(2)}) %collective-permute-start.5) | collective-permute-done | bytes 49184 | tf_op jit(solution)/shard_map/ppermute | solution.py:248
  77.2 0.3 fusion.2
  77.5 0.1 mul.83
  77.7 0.1 mul.80
  77.8 0.6 subtract_add_fusion
  (23 shorter events, 0.6 us)
Async XLA Ops:
  0.6 15.8 %copy-start = (s32[1,1,1496]{2,1,0:T(1,128)S(1)}, s32[1,1,1496]{2,1,0:T(1,128)}, u32[]{:S(2)}) copy-start(s32[1,1,1496]{2,1,0:T(1,128)} %near_ref.1) | copy-start | bytes 17956
  0.6 15.8 %copy-start.1 = (s32[1,1,1496]{2,1,0:T(1,128)S(1)}, s32[1,1,1496]{2,1,0:T(1,128)}, u32[]{:S(2)}) copy-start(s32[1,1,1496]{2,1,0:T(1,128)} %far_ref.1) | copy-start | bytes 17956
  3.3 13.2 %collective-permute-start = (f32[32,8,128]{2,1,0:T(8,128)S(1)}, f32[32,8,128]{2,1,0:T(8,128)S(1)}, u32[]{:S(2)}, u32[]{:S(2)}) collective-permute-start(f32[32,8,128]{2,1,0:T(8,128)S(1)} %bitcast.55), channel_id=1, source_target_pairs={{0,4},{4,8},{8,12},{12,16},{16,20},{20,24},{24,28},{28,0},{1,5},{5... | collective-permute-start | bytes 393224 | tf_op jit(solution)/shard_map/ppermute | solution.py:24
  3.8 12.6 %collective-permute-start.1 = (f32[32,8,128]{2,1,0:T(8,128)S(1)}, f32[32,8,128]{2,1,0:T(8,128)S(1)}, u32[]{:S(2)}, u32[]{:S(2)}) collective-permute-start(f32[32,8,128]{2,1,0:T(8,128)S(1)} %bitcast.56), channel_id=1, source_target_pairs={{0,28},{4,0},{8,4},{12,8},{16,12},{20,16},{24,20},{28,24},{1,29},{... | collective-permute-start | bytes 393224 | tf_op jit(solution)/shard_map/ppermute | solution.py:24
  6.8 9.7 %collective-permute-start.2 = (f32[32,8,128]{2,1,0:T(8,128)S(1)}, f32[32,8,128]{2,1,0:T(8,128)S(1)}, u32[]{:S(2)}, u32[]{:S(2)}) collective-permute-start(f32[32,8,128]{2,1,0:T(8,128)S(1)} %bitcast.57), channel_id=1, source_target_pairs={{0,1},{1,2},{2,3},{3,0},{4,5},{5,6},{6,7},{7,4},{8,9},{9,10},{10,1... | collective-permute-start | bytes 393224 | tf_op jit(solution)/shard_map/ppermute | solution.py:24
  9.0 7.4 %collective-permute-start.3 = (f32[32,8,128]{2,1,0:T(8,128)S(1)}, f32[32,8,128]{2,1,0:T(8,128)S(1)}, u32[]{:S(2)}, u32[]{:S(2)}) collective-permute-start(f32[32,8,128]{2,1,0:T(8,128)S(1)} %bitcast.58), channel_id=1, source_target_pairs={{0,3},{1,0},{2,1},{3,2},{4,7},{5,4},{6,5},{7,6},{8,11},{9,8},{10,9... | collective-permute-start | bytes 393224 | tf_op jit(solution)/shard_map/ppermute | solution.py:24
  16.5 61.3 %copy-start.2 = (f32[1,1,4096]{2,1,0:T(1,128)S(1)}, f32[1,1,4096]{2,1,0:T(1,128)}, u32[]{:S(2)}) copy-start(f32[1,1,4096]{2,1,0:T(1,128)} %param.14) | copy-start | bytes 49156
  32.9 37.3 %all-to-all-start = ((f32[32,1,8]{2,1,0:T(1,128)}), f32[32,1,8]{2,1,0:T(1,128)S(1)}, u32[]{:S(2)}, u32[]{:S(2)}) async-start(f32[32,1,8]{2,1,0:T(1,128)} %broadcast_in_dim.11), calls=%async_computation | async-start | bytes 32768 | tf_op jit(solution)/shard_map/all_to_all | solution.py:258
  64.1 9.5 %collective-permute-start.6 = (f32[3,64,64]{1,2,0:T(8,128)S(1)}, f32[3,64,64]{1,2,0:T(8,128)S(1)}, u32[]{:S(2)}, u32[]{:S(2)}) collective-permute-start(f32[3,64,64]{1,2,0:T(8,128)S(1)} %convolution_bitcast_fusion), channel_id=1, source_target_pairs={{0,3},{1,0},{2,1},{3,2},{4,7},{5,4},{6,5},{7,6},{8,11},{9,8},{10,9... | collective-permute-start | bytes 147464 | tf_op jit(solution)/shard_map/ppermute | solution.py:248
  68.0 9.1 %collective-permute-start.5 = (f32[3,64,64]{1,2,0:T(8,128)S(1)}, f32[3,64,64]{1,2,0:T(8,128)S(1)}, u32[]{:S(2)}, u32[]{:S(2)}) collective-permute-start(f32[3,64,64]{1,2,0:T(8,128)S(1)} %convolution_bitcast_fusion.1), channel_id=1, source_target_pairs={{0,2},{1,3},{2,0},{3,1},{4,6},{5,7},{6,4},{7,5},{8,10},{9,11},{10,... | collective-permute-start | bytes 147464 | tf_op jit(solution)/shard_map/ppermute | solution.py:248
  68.4 8.8 %collective-permute-start.4 = (f32[3,64,64]{1,2,0:T(8,128)S(1)}, f32[3,64,64]{1,2,0:T(8,128)S(1)}, u32[]{:S(2)}, u32[]{:S(2)}) collective-permute-start(f32[3,64,64]{1,2,0:T(8,128)S(1)} %convolution_bitcast_fusion.2), channel_id=1, source_target_pairs={{0,1},{1,2},{2,3},{3,0},{4,5},{5,6},{6,7},{7,4},{8,9},{9,10},{10,1... | collective-permute-start | bytes 147464 | tf_op jit(solution)/shard_map/ppermute | solution.py:248

commit v10 on v9

--- a/solution.py
+++ b/solution.py
@@ -151,7 +151,7 @@
             ones,
             acc_ref[c],
             (((1,), (1,)), ((), ())),
-            precision=lax.Precision.HIGHEST,
+            precision=lax.Precision.HIGH,
             preferred_element_type=jnp.float32,
         )
         fields.append(summed[0:1])

time: 79.1 us -> 77.4 us (0.979)
  starting transfers between devices: 42.8 us -> 40 us
  Pallas kernels: 14.4 us -> 15.6 us
    all_to_all x1, starting transfers between devices: 30.1 us -> 27.4 us  [on_device(): lax.all_to_all(sums_out, ('brick', 'plane'), split_axis=0, concat_axis=0,...]
    pallas_call x1, Pallas kernels: 14.4 us -> 15.6 us  [sweep(): pl.pallas_call(sweep_kernel, out_shape=(jax.ShapeDtypeStruct((2, atom_cou...]
where the time goes in v10:
time: 77.4 us; the launch traced here: 76.8 us
  starting transfers between devices  40 us (52%)
  Pallas kernels  15.6 us (20%)
  other arithmetic  6.9 us (9%)
  local copies, waits for them, and re-layouts  5.55 us (7%)
  waiting for transfers between devices  4.31 us (6%)
  between operations  3.49 us (5%)
  matrix products  0.99 us (1%)
    all_to_all x1, starting transfers between devices, on_device(): lax.all_to_all(sums_out, ('brick', 'plane'), split_axis=0, concat_axis=0,...  27.4 us
    pallas_call x1, Pallas kernels, sweep(): pl.pallas_call(sweep_kernel, out_shape=(jax.ShapeDtypeStruct((2, atom_cou...  15.6 us
    ppermute x4, starting transfers between devices, shifted_from(): return lax.ppermute(block, axis, pairs)  7.78 us
    ppermute x3, starting transfers between devices, to_owners(): lax.ppermute(part, 'plane', [(i, (i + step) % planes) for i in range(plan...  4.86 us
    ppermute x3, waiting for transfers between devices, to_owners(): lax.ppermute(part, 'plane', [(i, (i + step) % planes) for i in range(plan...  3.5 us
    unnamed x1, other arithmetic  2.01 us
    concatenate x2, local copies, waits for them, and re-layouts, on_device(): jnp.concatenate([positions.reshape(3, atom_count), jnp.square(radius)[Non...  1.71 us
  transfers between devices with their start and end apart: 8, of which 2 were waited for; matrix products, arithmetic and copies ran while one was open for 10% of the time, Pallas kernels for 0%

profile of v10, /device:TPU:0, one launch (start us, length us, event | category | flops | bytes accessed | tf_op | source)
XLA Modules:
  0.0 76.8 jit_solution(12586891944743562391)
XLA Ops:
  0.7 0.8 %copy.30 = f32[3,32,128]{2,0,1:T(4,128)S(1)} copy(f32[3,32,128]{2,1,0:T(8,128)} %bitcast.67) | data formatting | bytes 98304 | tf_op jit(solution)/shard_map/concatenate | solution.py:208
  1.5 0.9 %select_reduce_fusion.1 = (f32[4096]{0:T(1024)S(1)}, f32[4096]{0:T(1024)S(1)}, f32[4096]{0:T(1024)S(1)}) fusion(f32[8]{0:T(128)} %param.21, s32[4096]{0:T(1024)} %bitcast.69, f32[8]{0:T(128)} %param.22, f32[8]{0:T(128)} %param.23), kind=kLoop, calls=%fused_computation.8 | loop fusion | flops 217088 | bytes 65632 | tf_op jit(solution)/shard_map/reduce_sum | solution.py:41
  2.4 0.9 %concatenate.14 = f32[8,32,128]{2,0,1:T(8,128)S(1)} concatenate(f32[3,32,128]{2,0,1:T(4,128)S(1)} %copy.30, f32[1,32,128]{2,0,1:T(1,128)S(1)} %bitcast.65, f32[1,32,128]{2,0,1:T(1,128)} %bitcast.66, f32[1,32,128]{2,0,1:T(1,128)} %bitcast.68, f32[2,32,128]{2,0,1:T(2,128)S(1)} %broadcast_in_dim.8), dimensions={0} | concatenate | bytes 262144 | tf_op jit(solution)/shard_map/concatenate | solution.py:208
  3.3 0.5 collective-permute-start
  3.8 2.9 %collective-permute-start.1 = (f32[32,8,128]{2,1,0:T(8,128)S(1)}, f32[32,8,128]{2,1,0:T(8,128)S(1)}, u32[]{:S(2)}, u32[]{:S(2)}) collective-permute-start(f32[32,8,128]{2,1,0:T(8,128)S(1)} %bitcast.56), channel_id=1, source_target_pairs={{0,28},{4,0},{8,4},{12,8},{16,12},{20,16},{24,20},{28,24},{1,29},{... | collective-permute-start | bytes 393224 | tf_op jit(solution)/shard_map/ppermute | solution.py:24
  6.8 2.3 %collective-permute-start.2 = (f32[32,8,128]{2,1,0:T(8,128)S(1)}, f32[32,8,128]{2,1,0:T(8,128)S(1)}, u32[]{:S(2)}, u32[]{:S(2)}) collective-permute-start(f32[32,8,128]{2,1,0:T(8,128)S(1)} %bitcast.57), channel_id=1, source_target_pairs={{0,1},{1,2},{2,3},{3,0},{4,5},{5,6},{6,7},{7,4},{8,9},{9,10},{10,1... | collective-permute-start | bytes 393224 | tf_op jit(solution)/shard_map/ppermute | solution.py:24
  9.0 2.0 %collective-permute-start.3 = (f32[32,8,128]{2,1,0:T(8,128)S(1)}, f32[32,8,128]{2,1,0:T(8,128)S(1)}, u32[]{:S(2)}, u32[]{:S(2)}) collective-permute-start(f32[32,8,128]{2,1,0:T(8,128)S(1)} %bitcast.58), channel_id=1, source_target_pairs={{0,3},{1,0},{2,1},{3,2},{4,7},{5,4},{6,5},{7,6},{8,11},{9,8},{10,9... | collective-permute-start | bytes 393224 | tf_op jit(solution)/shard_map/ppermute | solution.py:24
  11.1 0.7 subtract_bitcast_fusion.3
  11.7 0.5 broadcast.95
  12.2 2.0 %fusion.21 = (f32[4096]{0:T(1024)S(1)}, f32[]{:T(128)}) fusion(f32[1,1,4096]{2,1,0:T(1,128)} %param.13, f32[]{:T(128)} %broadcast.95), kind=kLoop, calls=%fused_computation.45 | loop fusion | flops 4095 | bytes 32776 | tf_op args[1]
  14.9 0.6 copy.31.home_ref
  15.6 0.1 copy.34
  15.7 0.1 stack.22
  15.8 0.6 divide_reduce_fusion
  16.5 15.6 %shard_map.139 = (f32[2,4096]{1,0:T(2,128)S(1)}, f32[1,128]{1,0:T(1,128)S(1)}) custom-call(s32[1,1,1496]{2,1,0:T(1,128)S(1)} %copy-done, s32[1,1,1496]{2,1,0:T(1,128)S(1)} %copy-done.1, s32[1,1]{1,0:T(1,128)S(6)} %copy.42.count_ref, f32[4096,8]{1,0:T(8,128)S(1)} %copy.31.home_ref, f32[1,4096]{1,0:T(1,128)S(1)} %bitcast.63, f32[1,4096]{1,0:T(1,128)S(1)} %bitcast.61, ...), custom_call_target="tpu_custom_call" | custom-call | tf_op jit(solution)/shard_map/pallas_call | solution.py:169
  32.1 1.4 %select_maximum_fusion = f32[8]{0:T(128)S(1)} fusion(f32[1]{0:T(128)} %bitcast.12, f32[1]{0:T(128)S(1)} %bitcast.64, f32[1]{0:T(128)} %bitcast), kind=kLoop, calls=%fused_computation.34 | loop fusion | flops 48 | bytes 44 | tf_op jit(solution)/shard_map/stack | solution.py:254
  33.4 0.6 broadcast_in_dim.11
  34.1 27.4 %all-to-all-start = ((f32[32,1,8]{2,1,0:T(1,128)}), f32[32,1,8]{2,1,0:T(1,128)S(1)}, u32[]{:S(2)}, u32[]{:S(2)}) async-start(f32[32,1,8]{2,1,0:T(1,128)} %broadcast_in_dim.11), calls=%async_computation | async-start | bytes 32768 | tf_op jit(solution)/shard_map/all_to_all | solution.py:258
  61.5 0.6 slice_bitcast_fusion
  62.2 0.3 convolution_bitcast_fusion
  62.5 3.7 %collective-permute-start.6 = (f32[3,64,64]{1,2,0:T(8,128)S(1)}, f32[3,64,64]{1,2,0:T(8,128)S(1)}, u32[]{:S(2)}, u32[]{:S(2)}) collective-permute-start(f32[3,64,64]{1,2,0:T(8,128)S(1)} %convolution_bitcast_fusion), channel_id=1, source_target_pairs={{0,3},{1,0},{2,1},{3,2},{4,7},{5,4},{6,5},{7,6},{8,11},{9,8},{10,9... | collective-permute-start | bytes 147464 | tf_op jit(solution)/shard_map/ppermute | solution.py:248
  66.2 0.2 convolution_bitcast_fusion.1
  66.5 0.2 convolution_bitcast_fusion.2
  66.8 1.1 %collective-permute-start.4 = (f32[3,64,64]{1,2,0:T(8,128)S(1)}, f32[3,64,64]{1,2,0:T(8,128)S(1)}, u32[]{:S(2)}, u32[]{:S(2)}) collective-permute-start(f32[3,64,64]{1,2,0:T(8,128)S(1)} %convolution_bitcast_fusion.2), channel_id=1, source_target_pairs={{0,1},{1,2},{2,3},{3,0},{4,5},{5,6},{6,7},{7,4},{8,9},{9,10},{10,1... | collective-permute-start | bytes 147464 | tf_op jit(solution)/shard_map/ppermute | solution.py:248
  67.9 0.8 %all-to-all-done = f32[32,1,8]{2,1,0:T(1,128)S(1)} async-done(((f32[32,1,8]{2,1,0:T(1,128)}), f32[32,1,8]{2,1,0:T(1,128)S(1)}, u32[]{:S(2)}, u32[]{:S(2)}) %all-to-all-start) | async-done | bytes 1056 | tf_op jit(solution)/shard_map/all_to_all | solution.py:258
  68.7 0.7 fusion.22
  71.4 0.6 bitcast_divide_fusion
  72.1 3.5 %collective-permute-done.5 = f32[3,64,64]{1,2,0:T(8,128)S(1)} collective-permute-done((f32[3,64,64]{1,2,0:T(8,128)S(1)}, f32[3,64,64]{1,2,0:T(8,128)S(1)}, u32[]{:S(2)}, u32[]{:S(2)}) %collective-permute-start.5) | collective-permute-done | bytes 49184 | tf_op jit(solution)/shard_map/ppermute | solution.py:248
  75.6 0.2 fusion.2
  75.9 0.1 mul.83
  76.1 0.1 mul.80
  76.2 0.6 subtract_add_fusion
  (23 shorter events, 0.6 us)
Async XLA Ops:
  0.6 15.8 %copy-start = (s32[1,1,1496]{2,1,0:T(1,128)S(1)}, s32[1,1,1496]{2,1,0:T(1,128)}, u32[]{:S(2)}) copy-start(s32[1,1,1496]{2,1,0:T(1,128)} %near_ref.1) | copy-start | bytes 17956
  0.6 15.8 %copy-start.1 = (s32[1,1,1496]{2,1,0:T(1,128)S(1)}, s32[1,1,1496]{2,1,0:T(1,128)}, u32[]{:S(2)}) copy-start(s32[1,1,1496]{2,1,0:T(1,128)} %far_ref.1) | copy-start | bytes 17956
  3.3 13.2 %collective-permute-start = (f32[32,8,128]{2,1,0:T(8,128)S(1)}, f32[32,8,128]{2,1,0:T(8,128)S(1)}, u32[]{:S(2)}, u32[]{:S(2)}) collective-permute-start(f32[32,8,128]{2,1,0:T(8,128)S(1)} %bitcast.55), channel_id=1, source_target_pairs={{0,4},{4,8},{8,12},{12,16},{16,20},{20,24},{24,28},{28,0},{1,5},{5... | collective-permute-start | bytes 393224 | tf_op jit(solution)/shard_map/ppermute | solution.py:24
  3.8 12.6 %collective-permute-start.1 = (f32[32,8,128]{2,1,0:T(8,128)S(1)}, f32[32,8,128]{2,1,0:T(8,128)S(1)}, u32[]{:S(2)}, u32[]{:S(2)}) collective-permute-start(f32[32,8,128]{2,1,0:T(8,128)S(1)} %bitcast.56), channel_id=1, source_target_pairs={{0,28},{4,0},{8,4},{12,8},{16,12},{20,16},{24,20},{28,24},{1,29},{... | collective-permute-start | bytes 393224 | tf_op jit(solution)/shard_map/ppermute | solution.py:24
  6.8 9.7 %collective-permute-start.2 = (f32[32,8,128]{2,1,0:T(8,128)S(1)}, f32[32,8,128]{2,1,0:T(8,128)S(1)}, u32[]{:S(2)}, u32[]{:S(2)}) collective-permute-start(f32[32,8,128]{2,1,0:T(8,128)S(1)} %bitcast.57), channel_id=1, source_target_pairs={{0,1},{1,2},{2,3},{3,0},{4,5},{5,6},{6,7},{7,4},{8,9},{9,10},{10,1... | collective-permute-start | bytes 393224 | tf_op jit(solution)/shard_map/ppermute | solution.py:24
  9.0 7.4 %collective-permute-start.3 = (f32[32,8,128]{2,1,0:T(8,128)S(1)}, f32[32,8,128]{2,1,0:T(8,128)S(1)}, u32[]{:S(2)}, u32[]{:S(2)}) collective-permute-start(f32[32,8,128]{2,1,0:T(8,128)S(1)} %bitcast.58), channel_id=1, source_target_pairs={{0,3},{1,0},{2,1},{3,2},{4,7},{5,4},{6,5},{7,6},{8,11},{9,8},{10,9... | collective-permute-start | bytes 393224 | tf_op jit(solution)/shard_map/ppermute | solution.py:24
  16.5 59.7 %copy-start.2 = (f32[1,1,4096]{2,1,0:T(1,128)S(1)}, f32[1,1,4096]{2,1,0:T(1,128)}, u32[]{:S(2)}) copy-start(f32[1,1,4096]{2,1,0:T(1,128)} %param.14) | copy-start | bytes 49156
  34.1 34.6 %all-to-all-start = ((f32[32,1,8]{2,1,0:T(1,128)}), f32[32,1,8]{2,1,0:T(1,128)S(1)}, u32[]{:S(2)}, u32[]{:S(2)}) async-start(f32[32,1,8]{2,1,0:T(1,128)} %broadcast_in_dim.11), calls=%async_computation | async-start | bytes 32768 | tf_op jit(solution)/shard_map/all_to_all | solution.py:258
  62.5 9.5 %collective-permute-start.6 = (f32[3,64,64]{1,2,0:T(8,128)S(1)}, f32[3,64,64]{1,2,0:T(8,128)S(1)}, u32[]{:S(2)}, u32[]{:S(2)}) collective-permute-start(f32[3,64,64]{1,2,0:T(8,128)S(1)} %convolution_bitcast_fusion), channel_id=1, source_target_pairs={{0,3},{1,0},{2,1},{3,2},{4,7},{5,4},{6,5},{7,6},{8,11},{9,8},{10,9... | collective-permute-start | bytes 147464 | tf_op jit(solution)/shard_map/ppermute | solution.py:248
  66.4 9.1 %collective-permute-start.5 = (f32[3,64,64]{1,2,0:T(8,128)S(1)}, f32[3,64,64]{1,2,0:T(8,128)S(1)}, u32[]{:S(2)}, u32[]{:S(2)}) collective-permute-start(f32[3,64,64]{1,2,0:T(8,128)S(1)} %convolution_bitcast_fusion.1), channel_id=1, source_target_pairs={{0,2},{1,3},{2,0},{3,1},{4,6},{5,7},{6,4},{7,5},{8,10},{9,11},{10,... | collective-permute-start | bytes 147464 | tf_op jit(solution)/shard_map/ppermute | solution.py:248
  66.8 8.8 %collective-permute-start.4 = (f32[3,64,64]{1,2,0:T(8,128)S(1)}, f32[3,64,64]{1,2,0:T(8,128)S(1)}, u32[]{:S(2)}, u32[]{:S(2)}) collective-permute-start(f32[3,64,64]{1,2,0:T(8,128)S(1)} %convolution_bitcast_fusion.2), channel_id=1, source_target_pairs={{0,1},{1,2},{2,3},{3,0},{4,5},{5,6},{6,7},{7,4},{8,9},{9,10},{10,1... | collective-permute-start | bytes 147464 | tf_op jit(solution)/shard_map/ppermute | solution.py:248

commit v11 on v10

--- a/solution.py
+++ b/solution.py
@@ -158,10 +158,19 @@
     field = chi_ref[...] + fields[0] + fields[1]
     out_ref[0:1, :] = field
     out_ref[1:2, :] = fields[1]
-    sum_ref[...] = jnp.broadcast_to(jnp.sum(field / eta_ref[...]), sum_ref.shape)
-
-
-def sweep(home_cols, chi, eta, blocks, near_list, far_list, pair_total):
+    eta = eta_ref[...]
+    sums = (
+        jnp.sum(block_refs[0][:, 4:5, :]),
+        jnp.sum(field / eta),
+        jnp.sum(1.0 / eta),
+    )
+    column = lax.broadcasted_iota(jnp.int32, sum_ref.shape, 1)
+    sum_ref[...] = jnp.where(
+        column == 0, sums[0], jnp.where(column == 1, sums[1], jnp.where(column == 2, sums[2], 0.0))
+    )
+
+
+def sweep(home_cols, chi, eta, blocks, near_list, far_list, pair_total, devices):
     rows_per_block = blocks[0].shape[0]
     atom_count = rows_per_block * LANES
     smem = pl.BlockSpec(memory_space=pltpu.SMEM)
@@ -170,7 +179,7 @@
         sweep_kernel,
         out_shape=(
             jax.ShapeDtypeStruct((2, atom_count), jnp.float32),
-            jax.ShapeDtypeStruct((1, LANES), jnp.float32),
+            jax.ShapeDtypeStruct((devices, 8), jnp.float32),
         ),
         in_specs=[smem, smem, smem] + [vmem] * 8,
         out_specs=(vmem, vmem),
@@ -218,7 +227,8 @@
     packed = packed.reshape(8, atom_count // LANES, LANES).transpose(1, 0, 2)
     home_cols = packed.transpose(0, 2, 1).reshape(atom_count, 8)
     blocks = neighbours(packed)
-    totals, field_sum = sweep(
+    devices = lax.axis_size("brick") * lax.axis_size("plane")
+    totals, sums_out = sweep(
         home_cols,
         negativity[None],
         hardness_row[None],
@@ -226,6 +236,7 @@
         pair_tiles,
         pair_cands,
         pair_count,
+        devices,
     )
     field = totals[0]
     resid_field = totals[1]
@@ -251,10 +262,6 @@
             total = part if total is None else total + part
         return total
 
-    local_sums = jnp.stack(
-        [jnp.sum(charge_row), field_sum[0, 0], jnp.sum(1.0 / hardness_row)]
-    )
-    sums_out = jnp.broadcast_to(jnp.pad(local_sums, (0, 5))[None, :], (devices, 8))
     sums_in = lax.all_to_all(sums_out, ("brick", "plane"), split_axis=0, concat_axis=0, tiled=True)
     placed = to_owners(jnp.stack([charge_row, hardness_row, field]))
     global_sums = jnp.sum(sums_in, axis=0)

time: 77.4 us -> 75.9 us (0.981)
  other arithmetic: 6.9 us -> 2.93 us
  waiting for transfers between devices: 4.31 us -> 6.38 us
  starting transfers between devices: 40 us -> 41.9 us
  Pallas kernels: 15.6 us -> 14.8 us
    ppermute x4, waiting for transfers between devices: 0.01 us -> 2.01 us  [shifted_from(): return lax.ppermute(block, axis, pairs)]
    all_to_all x1, starting transfers between devices: 27.4 us -> 29.3 us  [on_device(): lax.all_to_all(sums_out, ('brick', 'plane'), split_axis=0, concat_axis=0,...]
    another operation x1 -> x0, other arithmetic: 1.37 us -> none  [on_device(): jnp.stack([jnp.sum(charge_row), field_sum[0, 0], jnp.sum(1.0 / hardness_r...]
    unnamed x1, other arithmetic: 2.01 us -> 0.68 us
  transfers between devices with their start and end apart: 8 -> 8, of which waited for: 2 -> 4; matrix products, arithmetic and copies ran while one was open for 10% -> 7% of each run, Pallas kernels for 0% -> 0%
where the time goes in v11:
time: 75.9 us; the launch traced here: 75.4 us
  starting transfers between devices  41.9 us (55%)
  Pallas kernels  14.8 us (19%)
  waiting for transfers between devices  6.38 us (8%)
  local copies, waits for them, and re-layouts  4.94 us (7%)
  between operations  3.48 us (5%)
  other arithmetic  2.93 us (4%)
  matrix products  0.99 us (1%)
    all_to_all x1, starting transfers between devices, on_device(): lax.all_to_all(sums_out, ('brick', 'plane'), split_axis=0, concat_axis=0,...  29.3 us
    pallas_call x1, Pallas kernels, sweep(): pl.pallas_call(sweep_kernel, out_shape=(jax.ShapeDtypeStruct((2, atom_cou...  14.8 us
    ppermute x4, starting transfers between devices, shifted_from(): return lax.ppermute(block, axis, pairs)  7.78 us
    ppermute x3, starting transfers between devices, to_owners(): lax.ppermute(part, 'plane', [(i, (i + step) % planes) for i in range(plan...  4.86 us
    ppermute x3, waiting for transfers between devices, to_owners(): lax.ppermute(part, 'plane', [(i, (i + step) % planes) for i in range(plan...  3.58 us
    ppermute x4, waiting for transfers between devices, shifted_from(): return lax.ppermute(block, axis, pairs)  2.01 us
    concatenate x2, local copies, waits for them, and re-layouts, on_device(): jnp.concatenate([positions.reshape(3, atom_count), jnp.square(radius)[Non...  1.72 us
  transfers between devices with their start and end apart: 8, of which 4 were waited for; matrix products, arithmetic and copies ran while one was open for 7% of the time, Pallas kernels for 0%

profile of v11, /device:TPU:0, one launch (start us, length us, event | category | flops | bytes accessed | tf_op | source)
XLA Modules:
  0.0 75.4 jit_solution(7748001293691453208)
XLA Ops:
  0.7 0.9 %copy.31 = f32[3,32,128]{2,0,1:T(4,128)S(1)} copy(f32[3,32,128]{2,1,0:T(8,128)} %bitcast.65) | data formatting | bytes 98304 | tf_op jit(solution)/shard_map/concatenate | solution.py:217
  1.5 0.9 %select_reduce_fusion.1 = (f32[4096]{0:T(1024)S(1)}, f32[4096]{0:T(1024)S(1)}, f32[4096]{0:T(1024)S(1)}) fusion(f32[8]{0:T(128)} %param.21, s32[4096]{0:T(1024)} %bitcast.67, f32[8]{0:T(128)} %param.22, f32[8]{0:T(128)} %param.23), kind=kLoop, calls=%fused_computation.8 | loop fusion | flops 217088 | bytes 65632 | tf_op jit(solution)/shard_map/reduce_sum | solution.py:41
  2.5 0.9 %concatenate.14 = f32[8,32,128]{2,0,1:T(8,128)S(1)} concatenate(f32[3,32,128]{2,0,1:T(4,128)S(1)} %copy.31, f32[1,32,128]{2,0,1:T(1,128)S(1)} %bitcast.63, f32[1,32,128]{2,0,1:T(1,128)} %bitcast.64, f32[1,32,128]{2,0,1:T(1,128)} %bitcast.66, f32[2,32,128]{2,0,1:T(2,128)S(1)} %broadcast_in_dim.6), dimensions={0} | concatenate | bytes 262144 | tf_op jit(solution)/shard_map/concatenate | solution.py:217
  3.3 0.5 collective-permute-start
  3.9 2.9 %collective-permute-start.1 = (f32[32,8,128]{2,1,0:T(8,128)S(1)}, f32[32,8,128]{2,1,0:T(8,128)S(1)}, u32[]{:S(2)}, u32[]{:S(2)}) collective-permute-start(f32[32,8,128]{2,1,0:T(8,128)S(1)} %bitcast.55), channel_id=1, source_target_pairs={{0,28},{4,0},{8,4},{12,8},{16,12},{20,16},{24,20},{28,24},{1,29},{... | collective-permute-start | bytes 393224 | tf_op jit(solution)/shard_map/ppermute | solution.py:24
  6.8 2.3 %collective-permute-start.2 = (f32[32,8,128]{2,1,0:T(8,128)S(1)}, f32[32,8,128]{2,1,0:T(8,128)S(1)}, u32[]{:S(2)}, u32[]{:S(2)}) collective-permute-start(f32[32,8,128]{2,1,0:T(8,128)S(1)} %bitcast.56), channel_id=1, source_target_pairs={{0,1},{1,2},{2,3},{3,0},{4,5},{5,6},{6,7},{7,4},{8,9},{9,10},{10,1... | collective-permute-start | bytes 393224 | tf_op jit(solution)/shard_map/ppermute | solution.py:24
  9.1 2.0 %collective-permute-start.3 = (f32[32,8,128]{2,1,0:T(8,128)S(1)}, f32[32,8,128]{2,1,0:T(8,128)S(1)}, u32[]{:S(2)}, u32[]{:S(2)}) collective-permute-start(f32[32,8,128]{2,1,0:T(8,128)S(1)} %bitcast.57), channel_id=1, source_target_pairs={{0,3},{1,0},{2,1},{3,2},{4,7},{5,4},{6,5},{7,6},{8,11},{9,8},{10,9... | collective-permute-start | bytes 393224 | tf_op jit(solution)/shard_map/ppermute | solution.py:24
  11.8 0.6 copy.32.home_ref
  12.5 0.1 copy.35
  12.6 0.5 broadcast.82
  13.1 0.7 reduce.8
  13.8 0.1 copy.34
  14.0 1.2 %collective-permute-done.2.refs_3_ = f32[32,8,128]{2,1,0:T(8,128)S(1)} collective-permute-done((f32[32,8,128]{2,1,0:T(8,128)S(1)}, f32[32,8,128]{2,1,0:T(8,128)S(1)}, u32[]{:S(2)}, u32[]{:S(2)}) %collective-permute-start.2) | collective-permute-done | bytes 131104 | tf_op jit(solution)/shard_map/ppermute | solution.py:24
  15.2 0.8 %collective-permute-done.3.refs_4_ = f32[32,8,128]{2,1,0:T(8,128)S(1)} collective-permute-done((f32[32,8,128]{2,1,0:T(8,128)S(1)}, f32[32,8,128]{2,1,0:T(8,128)S(1)}, u32[]{:S(2)}, u32[]{:S(2)}) %collective-permute-start.3) | collective-permute-done | bytes 131104 | tf_op jit(solution)/shard_map/ppermute | solution.py:24
  16.0 14.8 %shard_map.139 = (f32[2,4096]{1,0:T(2,128)S(1)}, f32[32,8]{1,0:T(8,128)}) custom-call(s32[1,1,1496]{2,1,0:T(1,128)S(1)} %copy-done, s32[1,1,1496]{2,1,0:T(1,128)S(1)} %copy-done.1, s32[1,1]{1,0:T(1,128)S(6)} %copy.39.count_ref, f32[4096,8]{1,0:T(8,128)S(1)} %copy.32.home_ref, f32[1,4096]{1,0:T(1,128)S(1)} %bitcast.62, f32[1,4096]{1,0:T(1,128)S(1)} %bitcast.60, ...), custom_call_target="tpu_custom_call" | custom-call | tf_op jit(solution)/shard_map/pallas_call | solution.py:178
  30.8 29.3 %all-to-all-start = ((f32[32,1,8]{2,1,0:T(1,128)}), f32[32,1,8]{2,1,0:T(1,128)S(1)}, u32[]{:S(2)}, u32[]{:S(2)}) async-start(f32[32,1,8]{2,1,0:T(1,128)} %bitcast.11), calls=%async_computation | async-start | bytes 32768 | tf_op jit(solution)/shard_map/all_to_all | solution.py:265
  60.1 0.6 slice_bitcast_fusion
  60.8 0.1 copy.36
  60.8 0.3 convolution_bitcast_fusion
  61.1 3.7 %collective-permute-start.6 = (f32[3,64,64]{1,2,0:T(8,128)S(1)}, f32[3,64,64]{1,2,0:T(8,128)S(1)}, u32[]{:S(2)}, u32[]{:S(2)}) collective-permute-start(f32[3,64,64]{1,2,0:T(8,128)S(1)} %convolution_bitcast_fusion), channel_id=1, source_target_pairs={{0,3},{1,0},{2,1},{3,2},{4,7},{5,4},{6,5},{7,6},{8,11},{9,8},{10,9... | collective-permute-start | bytes 147464 | tf_op jit(solution)/shard_map/ppermute | solution.py:259
  64.8 0.2 convolution_bitcast_fusion.1
  65.1 0.2 convolution_bitcast_fusion.2
  65.4 1.1 %collective-permute-start.4 = (f32[3,64,64]{1,2,0:T(8,128)S(1)}, f32[3,64,64]{1,2,0:T(8,128)S(1)}, u32[]{:S(2)}, u32[]{:S(2)}) collective-permute-start(f32[3,64,64]{1,2,0:T(8,128)S(1)} %convolution_bitcast_fusion.2), channel_id=1, source_target_pairs={{0,1},{1,2},{2,3},{3,0},{4,5},{5,6},{6,7},{7,4},{8,9},{9,10},{10,1... | collective-permute-start | bytes 147464 | tf_op jit(solution)/shard_map/ppermute | solution.py:259
  66.5 0.8 %all-to-all-done = f32[32,1,8]{2,1,0:T(1,128)S(1)} async-done(((f32[32,1,8]{2,1,0:T(1,128)}), f32[32,1,8]{2,1,0:T(1,128)S(1)}, u32[]{:S(2)}, u32[]{:S(2)}) %all-to-all-start) | async-done | bytes 1056 | tf_op jit(solution)/shard_map/all_to_all | solution.py:265
  67.3 0.7 fusion.21
  69.9 0.6 bitcast_divide_fusion
  70.6 3.6 %collective-permute-done.5 = f32[3,64,64]{1,2,0:T(8,128)S(1)} collective-permute-done((f32[3,64,64]{1,2,0:T(8,128)S(1)}, f32[3,64,64]{1,2,0:T(8,128)S(1)}, u32[]{:S(2)}, u32[]{:S(2)}) %collective-permute-start.5) | collective-permute-done | bytes 49184 | tf_op jit(solution)/shard_map/ppermute | solution.py:259
  74.2 0.3 fusion.2
  74.4 0.1 copy.38
  74.5 0.1 mul.83
  74.7 0.1 mul.80
  74.8 0.6 subtract_add_fusion
  (24 shorter events, 0.5 us)
Async XLA Ops:
  0.6 12.5 %copy-start.2 = (f32[1,1,4096]{2,1,0:T(1,128)S(1)}, f32[1,1,4096]{2,1,0:T(1,128)}, u32[]{:S(2)}) copy-start(f32[1,1,4096]{2,1,0:T(1,128)} %param.13) | copy-start | bytes 49156
  0.6 13.3 %copy-start.4 = (s32[1,1,64]{2,1,0:T(1,128)S(1)}, s32[1,1,64]{2,1,0:T(1,128)}, u32[]{:S(2)}) copy-start(s32[1,1,64]{2,1,0:T(1,128)} %param.20) | copy-start | bytes 772
  0.7 15.3 %copy-start = (s32[1,1,1496]{2,1,0:T(1,128)S(1)}, s32[1,1,1496]{2,1,0:T(1,128)}, u32[]{:S(2)}) copy-start(s32[1,1,1496]{2,1,0:T(1,128)} %near_ref.1) | copy-start | bytes 17956
  0.7 15.3 %copy-start.1 = (s32[1,1,1496]{2,1,0:T(1,128)S(1)}, s32[1,1,1496]{2,1,0:T(1,128)}, u32[]{:S(2)}) copy-start(s32[1,1,1496]{2,1,0:T(1,128)} %far_ref.1) | copy-start | bytes 17956
  3.3 10.6 %collective-permute-start = (f32[32,8,128]{2,1,0:T(8,128)S(1)}, f32[32,8,128]{2,1,0:T(8,128)S(1)}, u32[]{:S(2)}, u32[]{:S(2)}) collective-permute-start(f32[32,8,128]{2,1,0:T(8,128)S(1)} %bitcast.54), channel_id=1, source_target_pairs={{0,4},{4,8},{8,12},{12,16},{16,20},{20,24},{24,28},{28,0},{1,5},{5... | collective-permute-start | bytes 393224 | tf_op jit(solution)/shard_map/ppermute | solution.py:24
  3.9 10.1 %collective-permute-start.1 = (f32[32,8,128]{2,1,0:T(8,128)S(1)}, f32[32,8,128]{2,1,0:T(8,128)S(1)}, u32[]{:S(2)}, u32[]{:S(2)}) collective-permute-start(f32[32,8,128]{2,1,0:T(8,128)S(1)} %bitcast.55), channel_id=1, source_target_pairs={{0,28},{4,0},{8,4},{12,8},{16,12},{20,16},{24,20},{28,24},{1,29},{... | collective-permute-start | bytes 393224 | tf_op jit(solution)/shard_map/ppermute | solution.py:24
  6.8 8.4 %collective-permute-start.2 = (f32[32,8,128]{2,1,0:T(8,128)S(1)}, f32[32,8,128]{2,1,0:T(8,128)S(1)}, u32[]{:S(2)}, u32[]{:S(2)}) collective-permute-start(f32[32,8,128]{2,1,0:T(8,128)S(1)} %bitcast.56), channel_id=1, source_target_pairs={{0,1},{1,2},{2,3},{3,0},{4,5},{5,6},{6,7},{7,4},{8,9},{9,10},{10,1... | collective-permute-start | bytes 393224 | tf_op jit(solution)/shard_map/ppermute | solution.py:24
  9.1 6.9 %collective-permute-start.3 = (f32[32,8,128]{2,1,0:T(8,128)S(1)}, f32[32,8,128]{2,1,0:T(8,128)S(1)}, u32[]{:S(2)}, u32[]{:S(2)}) collective-permute-start(f32[32,8,128]{2,1,0:T(8,128)S(1)} %bitcast.57), channel_id=1, source_target_pairs={{0,3},{1,0},{2,1},{3,2},{4,7},{5,4},{6,5},{7,6},{8,11},{9,8},{10,9... | collective-permute-start | bytes 393224 | tf_op jit(solution)/shard_map/ppermute | solution.py:24
  16.0 58.8 %copy-start.3 = (f32[1,1,4096]{2,1,0:T(1,128)S(1)}, f32[1,1,4096]{2,1,0:T(1,128)}, u32[]{:S(2)}) copy-start(f32[1,1,4096]{2,1,0:T(1,128)} %param.14) | copy-start | bytes 49156
  30.8 36.5 %all-to-all-start = ((f32[32,1,8]{2,1,0:T(1,128)}), f32[32,1,8]{2,1,0:T(1,128)S(1)}, u32[]{:S(2)}, u32[]{:S(2)}) async-start(f32[32,1,8]{2,1,0:T(1,128)} %bitcast.11), calls=%async_computation | async-start | bytes 32768 | tf_op jit(solution)/shard_map/all_to_all | solution.py:265
  61.1 9.5 %collective-permute-start.6 = (f32[3,64,64]{1,2,0:T(8,128)S(1)}, f32[3,64,64]{1,2,0:T(8,128)S(1)}, u32[]{:S(2)}, u32[]{:S(2)}) collective-permute-start(f32[3,64,64]{1,2,0:T(8,128)S(1)} %convolution_bitcast_fusion), channel_id=1, source_target_pairs={{0,3},{1,0},{2,1},{3,2},{4,7},{5,4},{6,5},{7,6},{8,11},{9,8},{10,9... | collective-permute-start | bytes 147464 | tf_op jit(solution)/shard_map/ppermute | solution.py:259
  65.0 9.1 %collective-permute-start.5 = (f32[3,64,64]{1,2,0:T(8,128)S(1)}, f32[3,64,64]{1,2,0:T(8,128)S(1)}, u32[]{:S(2)}, u32[]{:S(2)}) collective-permute-start(f32[3,64,64]{1,2,0:T(8,128)S(1)} %convolution_bitcast_fusion.1), channel_id=1, source_target_pairs={{0,2},{1,3},{2,0},{3,1},{4,6},{5,7},{6,4},{7,5},{8,10},{9,11},{10,... | collective-permute-start | bytes 147464 | tf_op jit(solution)/shard_map/ppermute | solution.py:259
  65.4 8.8 %collective-permute-start.4 = (f32[3,64,64]{1,2,0:T(8,128)S(1)}, f32[3,64,64]{1,2,0:T(8,128)S(1)}, u32[]{:S(2)}, u32[]{:S(2)}) collective-permute-start(f32[3,64,64]{1,2,0:T(8,128)S(1)} %convolution_bitcast_fusion.2), channel_id=1, source_target_pairs={{0,1},{1,2},{2,3},{3,0},{4,5},{5,6},{6,7},{7,4},{8,9},{9,10},{10,1... | collective-permute-start | bytes 147464 | tf_op jit(solution)/shard_map/ppermute | solution.py:259

commit v12 on v8

--- a/solution.py
+++ b/solution.py
@@ -1,3 +1,5 @@
+import functools
+
 import numpy as np
 import jax
 import jax.numpy as jnp
@@ -53,16 +55,16 @@
 
 
 LANES = 128
-
-
-def sweep_kernel(near_ref, far_ref, count_ref, home_ref, *refs):
+HELPER_SLACK = 320
+
+
+def sweep_kernel(near_ref, far_ref, range_ref, home_ref, *refs, pair_cap, far_offset):
     block_refs = refs[:5]
     out_ref, cand_ref, spread_ref, acc_ref = refs[5:]
     rows_per_block = block_refs[0].shape[0]
     atom_count = rows_per_block * LANES
     tile_count = atom_count // TILE
     cand_tiles = 5 * tile_count
-    pair_cap = near_ref.shape[-1]
     sublane = lax.broadcasted_iota(jnp.int32, (8, LANES), 0)
     left_rows = lax.broadcasted_iota(jnp.int32, (8, LANES), 1) < TILE
     shifts = ((0.0, 0.0), (-TX * cell_edge, 0.0), (TX * cell_edge, 0.0),
@@ -87,7 +89,8 @@
             column = home_ref[r * chunk:(r + 1) * chunk, q:q + 1]
             spread_ref[q, r * chunk:(r + 1) * chunk, :] = jnp.broadcast_to(column, (chunk, LANES))
     acc_ref[...] = jnp.zeros(acc_ref.shape, jnp.float32)
-    total = count_ref[0, 0]
+    begin = range_ref[0, 0]
+    end = range_ref[0, 1]
     lane = lax.broadcasted_iota(jnp.int32, (1, LANES), 1)
     left = lane < TILE
     lane_full = lax.broadcasted_iota(jnp.int32, (TILE, LANES), 1)
@@ -96,14 +99,15 @@
     diagonal = (lane_full % TILE) == lax.broadcasted_iota(jnp.int32, (TILE, LANES), 0)
 
     def pair_kernel(first):
-        second = jnp.minimum(first + 1, pair_cap - 1)
-        has_first = (first < total).astype(jnp.float32)
-        has_second = (first + 1 < total).astype(jnp.float32)
-        first = jnp.minimum(first, pair_cap - 1)
+        first = begin + first
+        has_first = (first < end).astype(jnp.float32)
+        has_second = (first + 1 < end).astype(jnp.float32)
+        second = jnp.clip(first + 1, 0, pair_cap - 1)
+        first = jnp.clip(first, 0, pair_cap - 1)
         home_a = jnp.clip(near_ref[0, 0, first], 0, tile_count - 1)
-        cand_a = jnp.clip(far_ref[0, 0, first], 0, cand_tiles - 1)
+        cand_a = jnp.clip(far_ref[0, 0, far_offset + first], 0, cand_tiles - 1)
         home_b = jnp.clip(near_ref[0, 0, second], 0, tile_count - 1)
-        cand_b = jnp.clip(far_ref[0, 0, second], 0, cand_tiles - 1)
+        cand_b = jnp.clip(far_ref[0, 0, far_offset + second], 0, cand_tiles - 1)
         rows = jnp.where(left, cand_ref[cand_a] * has_first, cand_ref[cand_b] * has_second)
         base_a = pl.multiple_of(home_a * TILE, TILE)
         base_b = pl.multiple_of(home_b * TILE, TILE)
@@ -143,26 +147,29 @@
             accumulate(*part)
         return carry
 
-    lax.fori_loop(0, (total + 15) // 16, body, 0)
+    lax.fori_loop(0, jnp.maximum(end - begin + 15, 0) // 16, body, 0)
     ones = jnp.ones((8, LANES), jnp.float32)
     for c in range(2):
         summed = lax.dot_general(
             ones,
             acc_ref[c],
             (((1,), (1,)), ((), ())),
-            precision=lax.Precision.HIGHEST,
+            precision=lax.Precision.HIGH,
             preferred_element_type=jnp.float32,
         )
         out_ref[c:c + 1, :] = summed[0:1]
 
 
-def sweep(home_cols, blocks, near_list, far_list, pair_total):
+def sweep(home_cols, blocks, near_list, far_list, pair_range, far_offset):
     rows_per_block = blocks[0].shape[0]
     atom_count = rows_per_block * LANES
     smem = pl.BlockSpec(memory_space=pltpu.SMEM)
     vmem = pl.BlockSpec(memory_space=pltpu.VMEM)
+    kernel = functools.partial(
+        sweep_kernel, pair_cap=near_list.shape[-1], far_offset=far_offset
+    )
     return pl.pallas_call(
-        sweep_kernel,
+        kernel,
         out_shape=jax.ShapeDtypeStruct((2, atom_count), jnp.float32),
         in_specs=[smem, smem, smem] + [vmem] * 6,
         out_specs=vmem,
@@ -172,7 +179,7 @@
             pltpu.VMEM((2, atom_count, LANES), jnp.float32),
         ],
         compiler_params=pltpu.CompilerParams(vmem_limit_bytes=48 * 1024 * 1024),
-    )(near_list, far_list, pair_total, home_cols, *blocks)
+    )(near_list, far_list, pair_range, home_cols, *blocks)
 
 
 def on_device(
@@ -207,13 +214,56 @@
         ],
         axis=0,
     )
-    home_cols = packed.T
     packed = packed.reshape(8, atom_count // LANES, LANES).transpose(1, 0, 2)
+    home_cols = packed.transpose(0, 2, 1).reshape(atom_count, 8)
     blocks = neighbours(packed)
-    totals = sweep(home_cols, blocks, pair_tiles, pair_cands, pair_count)
-    aux_field = totals[0].reshape(atom_count)
-    resid_field = totals[1].reshape(atom_count)
-    field = negativity + aux_field + resid_field
+    pair_cap = pair_tiles.shape[-1]
+    bricks = lax.axis_size("brick")
+    partner = [(i, (i + bricks // 2) % bricks) for i in range(bricks)]
+    lists = jnp.concatenate(
+        [pair_tiles.reshape(-1), pair_cands.reshape(-1), pair_count.reshape(-1)]
+    )
+    partner_lists = lax.ppermute(lists, "brick", partner)
+    partner_blocks = lax.ppermute(jnp.stack(blocks), "brick", partner)
+    own_count = pair_count[0, 0]
+    partner_count = partner_lists[2 * pair_cap]
+    both = own_count + partner_count
+    share = (both + HELPER_SLACK + 1) // 2
+    own_keep = jnp.where(own_count > partner_count, jnp.minimum(own_count, share), own_count)
+    partner_keep = jnp.where(
+        partner_count > own_count, jnp.minimum(partner_count, share), partner_count
+    )
+    own_fields = sweep(
+        home_cols,
+        blocks,
+        pair_tiles,
+        pair_cands,
+        jnp.stack([0, own_keep]).reshape(1, 2).astype(jnp.int32),
+        0,
+    )
+
+    after_own = (0.0 * own_fields[0, 0]).astype(jnp.int32)
+
+    def help_partner():
+        partner_cols = partner_blocks[0].transpose(0, 2, 1).reshape(atom_count, 8)
+        partner_list = partner_lists.reshape(1, 1, -1)
+        return sweep(
+            partner_cols,
+            [partner_blocks[k] for k in range(5)],
+            partner_list,
+            partner_list,
+            jnp.stack([partner_keep, partner_count]).reshape(1, 2).astype(jnp.int32) + after_own,
+            pair_cap,
+        )
+
+    helped = lax.cond(
+        partner_keep < partner_count,
+        help_partner,
+        lambda: jnp.zeros((2, atom_count), jnp.float32),
+    )
+    totals = own_fields + lax.ppermute(helped, "brick", partner)
+    field = negativity + totals[0] + totals[1]
+    resid_field = totals[1]
     planes = lax.axis_size("plane")
     devices = lax.axis_size("brick") * planes
     target = owner_tile.reshape(tile_count)

time: 79.7 us -> 101 us (1.27)
  waiting for transfers between devices: 4.43 us -> 14.8 us
  Pallas kernels: 17 us -> 11.3 us
  starting transfers between devices: 40.3 us -> 45.3 us
  between operations: 3.54 us -> 8.06 us
  local copies, waits for them, and re-layouts: 6.56 us -> 9.35 us
  other arithmetic: 6.27 us -> 8.97 us
  matrix products: 1 us -> 2.27 us
    ppermute x0 -> x3, waiting for transfers between devices: none -> 9.96 us  [the longest x1 9.95 us: on_device(): partner_lists = lax.ppermute(lists, 'brick', partner)]
    ppermute x0 -> x3, starting transfers between devices: none -> 7.5 us  [the longest x1 5.47 us: on_device(): totals = own_fields + lax.ppermute(helped, 'brick', partner)]
    all_to_all x1, starting transfers between devices: 27.6 us -> 21.5 us  [on_device(): lax.all_to_all(sums_out, ('brick', 'plane'), split_axis=0, concat_axis=0,...]
    pallas_call x1, Pallas kernels: 17 us -> 11.3 us  [sweep(): pl.pallas_call(kernel, out_shape=jax.ShapeDtypeStruct((2, atom_count), jn...]
    ppermute x3, starting transfers between devices: 4.86 us -> 8.48 us  [to_owners(): lax.ppermute(part, 'plane', [(i, (i + step) % planes) for i in range(plan...]
    ppermute x3, waiting for transfers between devices: 3.07 us -> 0.01 us  [to_owners(): lax.ppermute(part, 'plane', [(i, (i + step) % planes) for i in range(plan...]
    ppermute x4, waiting for transfers between devices: 0.01 us -> 2.23 us  [shifted_from(): return lax.ppermute(block, axis, pairs)]
    unnamed x12 -> x15, local copies, waits for them, and re-layouts: 1.39 us -> 3.18 us
  transfers between devices with their start and end apart: 8 -> 11, of which waited for: 2 -> 4; matrix products, arithmetic and copies ran while one was open for 8% -> 16% of each run, Pallas kernels for 0% -> 11%
where the time goes in v12:
time: 101 us; the launch traced here: 100 us
  starting transfers between devices  45.3 us (45%)
  waiting for transfers between devices  14.8 us (15%)
  Pallas kernels  11.3 us (11%)
  local copies, waits for them, and re-layouts  9.35 us (9%)
  other arithmetic  8.97 us (9%)
  between operations  8.06 us (8%)
  matrix products  2.27 us (2%)
    all_to_all x1, starting transfers between devices, on_device(): lax.all_to_all(sums_out, ('brick', 'plane'), split_axis=0, concat_axis=0,...  21.5 us
    pallas_call x1, Pallas kernels, sweep(): pl.pallas_call(kernel, out_shape=jax.ShapeDtypeStruct((2, atom_count), jn...  11.3 us
    ppermute x1, waiting for transfers between devices, on_device(): partner_lists = lax.ppermute(lists, 'brick', partner)  9.95 us
    ppermute x3, starting transfers between devices, to_owners(): lax.ppermute(part, 'plane', [(i, (i + step) % planes) for i in range(plan...  8.48 us
    ppermute x4, starting transfers between devices, shifted_from(): return lax.ppermute(block, axis, pairs)  7.78 us
    ppermute x1, starting transfers between devices, on_device(): totals = own_fields + lax.ppermute(helped, 'brick', partner)  5.47 us
    unnamed x15, local copies, waits for them, and re-layouts  3.18 us
    unnamed x3, other arithmetic  2.71 us
  transfers between devices with their start and end apart: 11, of which 4 were waited for; matrix products, arithmetic and copies ran while one was open for 16% of the time, Pallas kernels for 11%

profile of v12, /device:TPU:0, one launch (start us, length us, event | category | flops | bytes accessed | tf_op | source)
XLA Modules:
  0.0 100.1 jit_solution(17633791576904356614)
XLA Ops:
  0.6 0.9 select_reduce_fusion.2
  1.6 0.8 copy.33
  2.4 0.9 concatenate.28
  3.8 2.9 %collective-permute-start.2 = (f32[32,8,128]{2,1,0:T(8,128)S(1)}, f32[32,8,128]{2,1,0:T(8,128)S(1)}, u32[]{:S(2)}, u32[]{:S(2)}) collective-permute-start(f32[32,8,128]{2,1,0:T(8,128)S(1)} %bitcast.106), channel_id=1, source_target_pairs={{0,28},{4,0},{8,4},{12,8},{16,12},{20,16},{24,20},{28,24},{1,29},{... | collective-permute-start | bytes 393224 | tf_op jit(solution)/shard_map/ppermute | solution.py:26
  6.8 2.3 %collective-permute-start.3 = (f32[32,8,128]{2,1,0:T(8,128)S(1)}, f32[32,8,128]{2,1,0:T(8,128)S(1)}, u32[]{:S(2)}, u32[]{:S(2)}) collective-permute-start(f32[32,8,128]{2,1,0:T(8,128)S(1)} %bitcast.107), channel_id=1, source_target_pairs={{0,1},{1,2},{2,3},{3,0},{4,5},{5,6},{6,7},{7,4},{8,9},{9,10},{10,1... | collective-permute-start | bytes 393224 | tf_op jit(solution)/shard_map/ppermute | solution.py:26
  9.1 2.0 %collective-permute-start.4 = (f32[32,8,128]{2,1,0:T(8,128)S(1)}, f32[32,8,128]{2,1,0:T(8,128)S(1)}, u32[]{:S(2)}, u32[]{:S(2)}) collective-permute-start(f32[32,8,128]{2,1,0:T(8,128)S(1)} %bitcast.108), channel_id=1, source_target_pairs={{0,3},{1,0},{2,1},{3,2},{4,7},{5,4},{6,5},{7,6},{8,11},{9,8},{10,9... | collective-permute-start | bytes 393224 | tf_op jit(solution)/shard_map/ppermute | solution.py:26
  11.1 0.6 bitcast_dynamic-update-slice_fusion
  11.7 0.7 bitcast_dynamic-update-slice_fusion.4
  12.4 0.7 bitcast_dynamic-update-slice_fusion.3
  13.1 2.1 %collective-permute-done.3.refs_3_ = f32[32,8,128]{2,1,0:T(8,128)S(1)} collective-permute-done((f32[32,8,128]{2,1,0:T(8,128)S(1)}, f32[32,8,128]{2,1,0:T(8,128)S(1)}, u32[]{:S(2)}, u32[]{:S(2)}) %collective-permute-start.3) | collective-permute-done | bytes 131104 | tf_op jit(solution)/shard_map/ppermute | solution.py:26
  15.2 0.7 bitcast_dynamic-update-slice_fusion.2
  15.9 0.7 bitcast_dynamic-update-slice_fusion.1
  16.6 1.5 %collective-permute-start.5 = (f32[5,32,8,128]{3,2,1,0:T(8,128)}, f32[5,32,8,128]{3,2,1,0:T(8,128)S(1)}, u32[]{:S(2)}, u32[]{:S(2)}) collective-permute-start(f32[5,32,8,128]{3,2,1,0:T(8,128)} %bitcast_dynamic-update-slice_fusion.1), channel_id=1, source_target_pairs={{0,16},{4,20},{8,24},{12,28},{16,0},{20,4},{24,8},{28,12},{1,17},{... | collective-permute-start | bytes 1966088 | tf_op jit(solution)/shard_map/ppermute | solution.py:227
  18.8 0.7 reduce.2
  19.5 0.7 reduce.3
  20.8 1.2 %subtract_bitcast_fusion.3 = (s32[64]{0:T(128)S(1)}, s32[64]{0:T(128)}, s32[64]{0:T(128)}, s32[64]{0:T(128)}) fusion(s32[1,1,64]{2,1,0:T(1,128)} %param.22, s32[]{:T(128)S(6)} %mul.79, s32[]{:T(128)S(6)} %mul.80, s32[]{:T(128)S(6)} %mul.82, s32[]{:T(128)S(6)} %mul.81), kind=kLoop, calls=%fused_computation.57 | loop fusion | flops 256 | bytes 1296 | tf_op jit(solution)/shard_map/sub | solution.py:277
  22.0 0.6 copy.34.home_ref
  22.6 9.9 %collective-permute-done = s32[2993]{0:T(1024)S(1)} collective-permute-done((s32[2993]{0:T(1024)S(1)}, s32[2993]{0:T(1024)S(1)}, u32[]{:S(2)}, u32[]{:S(2)}) %collective-permute-start) | collective-permute-done | bytes 12004 | tf_op jit(solution)/shard_map/ppermute | solution.py:226
  37.2 11.3 %shard_map.139 = f32[2,4096]{1,0:T(2,128)S(1)} custom-call(s32[1,1,1496]{2,1,0:T(1,128)S(1)} %copy-done, s32[1,1,1496]{2,1,0:T(1,128)S(1)} %copy-done.1, s32[1,2]{1,0:T(1,128)S(1)} %add_bitcast_fusion.range_ref, f32[4096,8]{1,0:T(8,128)S(1)} %copy.34.home_ref, f32[32,8,128]{2,1,0:T(8,128)S(1)} %bitcast.110, ...), custom_call_target="tpu_custom_call" | custom-call | tf_op jit(solution)/shard_map/pallas_call | solution.py:171
  49.8 5.5 %collective-permute-start.6 = (f32[2,4096]{1,0:T(2,128)S(1)}, f32[2,4096]{1,0:T(2,128)S(1)}, u32[]{:S(2)}, u32[]{:S(2)}) collective-permute-start(f32[2,4096]{1,0:T(2,128)S(1)} %get-tuple-element.49), channel_id=1, source_target_pairs={{0,16},{4,20},{8,24},{12,28},{16,0},{20,4},{24,8},{28,12},{1,17},{... | collective-permute-start | bytes 98312 | tf_op jit(solution)/shard_map/ppermute | solution.py:264
  55.7 1.3 %fusion.25 = (f32[4096]{0:T(1024)S(1)}, f32[]{:T(128)}) fusion(f32[1,1,4096]{2,1,0:T(1,128)S(1)} %copy-done.2, f32[]{:T(128)} %broadcast.109), kind=kLoop, calls=%fused_computation.63 | loop fusion | flops 4095 | bytes 32776 | tf_op args[1]
  57.9 0.9 convolution_bitcast_fusion.1
  58.8 4.7 %collective-permute-start.8 = (f32[3,64,64]{1,2,0:T(8,128)S(1)}, f32[3,64,64]{1,2,0:T(8,128)S(1)}, u32[]{:S(2)}, u32[]{:S(2)}) collective-permute-start(f32[3,64,64]{1,2,0:T(8,128)S(1)} %convolution_bitcast_fusion.1), channel_id=1, source_target_pairs={{0,2},{1,3},{2,0},{3,1},{4,6},{5,7},{6,4},{7,5},{8,10},{9,11},{10,... | collective-permute-start | bytes 147464 | tf_op jit(solution)/shard_map/ppermute | solution.py:283
  63.5 0.6 fusion.20
  64.2 2.0 %select_maximum_fusion = f32[8]{0:T(128)S(1)} fusion(f32[1]{0:T(128)} %bitcast.33, f32[1]{0:T(128)} %bitcast.32, f32[1]{0:T(128)} %bitcast.11), kind=kLoop, calls=%fused_computation.50 | loop fusion | flops 48 | bytes 44 | tf_op jit(solution)/shard_map/stack | solution.py:289
  66.2 0.6 broadcast_in_dim.2
  66.8 21.5 %all-to-all-start = ((f32[32,1,8]{2,1,0:T(1,128)}), f32[32,1,8]{2,1,0:T(1,128)S(1)}, u32[]{:S(2)}, u32[]{:S(2)}) async-start(f32[32,1,8]{2,1,0:T(1,128)} %broadcast_in_dim.2), calls=%async_computation | async-start | bytes 32768 | tf_op jit(solution)/shard_map/all_to_all | solution.py:293
  88.3 0.9 convolution_bitcast_fusion
  89.2 3.7 %collective-permute-start.9 = (f32[3,64,64]{1,2,0:T(8,128)S(1)}, f32[3,64,64]{1,2,0:T(8,128)S(1)}, u32[]{:S(2)}, u32[]{:S(2)}) collective-permute-start(f32[3,64,64]{1,2,0:T(8,128)S(1)} %convolution_bitcast_fusion), channel_id=1, source_target_pairs={{0,3},{1,0},{2,1},{3,2},{4,7},{5,4},{6,5},{7,6},{8,11},{9,8},{10,9... | collective-permute-start | bytes 147464 | tf_op jit(solution)/shard_map/ppermute | solution.py:283
  92.9 2.6 %all-to-all-done = f32[32,1,8]{2,1,0:T(1,128)S(1)} async-done(((f32[32,1,8]{2,1,0:T(1,128)}), f32[32,1,8]{2,1,0:T(1,128)S(1)}, u32[]{:S(2)}, u32[]{:S(2)}) %all-to-all-start) | async-done | bytes 1056 | tf_op jit(solution)/shard_map/all_to_all | solution.py:293
  98.2 0.6 fusion.15
  99.5 0.6 subtract_add_fusion
  (47 shorter events, 5.2 us)
Async XLA Ops:
  1.5 35.6 %copy-start = (s32[1,1,1496]{2,1,0:T(1,128)S(1)}, s32[1,1,1496]{2,1,0:T(1,128)}, u32[]{:S(2)}) copy-start(s32[1,1,1496]{2,1,0:T(1,128)} %near_ref.1) | copy-start | bytes 17956
  1.6 35.6 %copy-start.1 = (s32[1,1,1496]{2,1,0:T(1,128)S(1)}, s32[1,1,1496]{2,1,0:T(1,128)}, u32[]{:S(2)}) copy-start(s32[1,1,1496]{2,1,0:T(1,128)} %far_ref.1) | copy-start | bytes 17956
  3.3 8.4 %collective-permute-start.1 = (f32[32,8,128]{2,1,0:T(8,128)S(1)}, f32[32,8,128]{2,1,0:T(8,128)S(1)}, u32[]{:S(2)}, u32[]{:S(2)}) collective-permute-start(f32[32,8,128]{2,1,0:T(8,128)S(1)} %bitcast.105), channel_id=1, source_target_pairs={{0,4},{4,8},{8,12},{12,16},{16,20},{20,24},{24,28},{28,0},{1,5},{5... | collective-permute-start | bytes 393224 | tf_op jit(solution)/shard_map/ppermute | solution.py:26
  3.8 8.5 %collective-permute-start.2 = (f32[32,8,128]{2,1,0:T(8,128)S(1)}, f32[32,8,128]{2,1,0:T(8,128)S(1)}, u32[]{:S(2)}, u32[]{:S(2)}) collective-permute-start(f32[32,8,128]{2,1,0:T(8,128)S(1)} %bitcast.106), channel_id=1, source_target_pairs={{0,28},{4,0},{8,4},{12,8},{16,12},{20,16},{24,20},{28,24},{1,29},{... | collective-permute-start | bytes 393224 | tf_op jit(solution)/shard_map/ppermute | solution.py:26
  6.8 8.4 %collective-permute-start.3 = (f32[32,8,128]{2,1,0:T(8,128)S(1)}, f32[32,8,128]{2,1,0:T(8,128)S(1)}, u32[]{:S(2)}, u32[]{:S(2)}) collective-permute-start(f32[32,8,128]{2,1,0:T(8,128)S(1)} %bitcast.107), channel_id=1, source_target_pairs={{0,1},{1,2},{2,3},{3,0},{4,5},{5,6},{6,7},{7,4},{8,9},{9,10},{10,1... | collective-permute-start | bytes 393224 | tf_op jit(solution)/shard_map/ppermute | solution.py:26
  9.1 6.9 %collective-permute-start.4 = (f32[32,8,128]{2,1,0:T(8,128)S(1)}, f32[32,8,128]{2,1,0:T(8,128)S(1)}, u32[]{:S(2)}, u32[]{:S(2)}) collective-permute-start(f32[32,8,128]{2,1,0:T(8,128)S(1)} %bitcast.108), channel_id=1, source_target_pairs={{0,3},{1,0},{2,1},{3,2},{4,7},{5,4},{6,5},{7,6},{8,11},{9,8},{10,9... | collective-permute-start | bytes 393224 | tf_op jit(solution)/shard_map/ppermute | solution.py:26
  16.6 33.1 %collective-permute-start.5 = (f32[5,32,8,128]{3,2,1,0:T(8,128)}, f32[5,32,8,128]{3,2,1,0:T(8,128)S(1)}, u32[]{:S(2)}, u32[]{:S(2)}) collective-permute-start(f32[5,32,8,128]{3,2,1,0:T(8,128)} %bitcast_dynamic-update-slice_fusion.1), channel_id=1, source_target_pairs={{0,16},{4,20},{8,24},{12,28},{16,0},{20,4},{24,8},{28,12},{1,17},{... | collective-permute-start | bytes 1966088 | tf_op jit(solution)/shard_map/ppermute | solution.py:227
  20.3 12.3 %collective-permute-start = (s32[2993]{0:T(1024)S(1)}, s32[2993]{0:T(1024)S(1)}, u32[]{:S(2)}, u32[]{:S(2)}) collective-permute-start(s32[2993]{0:T(1024)S(1)} %concatenate.23), channel_id=1, source_target_pairs={{0,16},{4,20},{8,24},{12,28},{16,0},{20,4},{24,8},{28,12},{1,17},{... | collective-permute-start | bytes 35924 | tf_op jit(solution)/shard_map/ppermute | solution.py:226
  49.7 6.1 %copy-start.2 = (f32[1,1,4096]{2,1,0:T(1,128)S(1)}, f32[1,1,4096]{2,1,0:T(1,128)}, u32[]{:S(2)}) copy-start(f32[1,1,4096]{2,1,0:T(1,128)} %param.15) | copy-start | bytes 49156
  49.7 7.9 %copy-start.4 = (s32[64]{0:T(128)S(1)}, s32[64]{0:T(128)}, u32[]{:S(2)}) copy-start(s32[64]{0:T(128)} %get-tuple-element.43) | copy-start | bytes 772
  49.7 49.7 %copy-start.3 = (f32[1,1,4096]{2,1,0:T(1,128)S(1)}, f32[1,1,4096]{2,1,0:T(1,128)}, u32[]{:S(2)}) copy-start(f32[1,1,4096]{2,1,0:T(1,128)} %param.16) | copy-start | bytes 49156
  49.8 7.6 %collective-permute-start.6 = (f32[2,4096]{1,0:T(2,128)S(1)}, f32[2,4096]{1,0:T(2,128)S(1)}, u32[]{:S(2)}, u32[]{:S(2)}) collective-permute-start(f32[2,4096]{1,0:T(2,128)S(1)} %get-tuple-element.49), channel_id=1, source_target_pairs={{0,16},{4,20},{8,24},{12,28},{16,0},{20,4},{24,8},{28,12},{1,17},{... | collective-permute-start | bytes 98312 | tf_op jit(solution)/shard_map/ppermute | solution.py:264
  57.9 41.0 %collective-permute-start.7 = (f32[3,64,64]{1,2,0:T(8,128)S(1)}, f32[3,64,64]{1,2,0:T(8,128)S(1)}, u32[]{:S(2)}, u32[]{:S(2)}) collective-permute-start(f32[3,64,64]{1,2,0:T(8,128)S(1)} %convolution_bitcast_fusion.2), channel_id=1, source_target_pairs={{0,1},{1,2},{2,3},{3,0},{4,5},{5,6},{6,7},{7,4},{8,9},{9,10},{10,1... | collective-permute-start | bytes 147464 | tf_op jit(solution)/shard_map/ppermute | solution.py:283
  58.8 40.0 %collective-permute-start.8 = (f32[3,64,64]{1,2,0:T(8,128)S(1)}, f32[3,64,64]{1,2,0:T(8,128)S(1)}, u32[]{:S(2)}, u32[]{:S(2)}) collective-permute-start(f32[3,64,64]{1,2,0:T(8,128)S(1)} %convolution_bitcast_fusion.1), channel_id=1, source_target_pairs={{0,2},{1,3},{2,0},{3,1},{4,6},{5,7},{6,4},{7,5},{8,10},{9,11},{10,... | collective-permute-start | bytes 147464 | tf_op jit(solution)/shard_map/ppermute | solution.py:283
  66.8 28.7 %all-to-all-start = ((f32[32,1,8]{2,1,0:T(1,128)}), f32[32,1,8]{2,1,0:T(1,128)S(1)}, u32[]{:S(2)}, u32[]{:S(2)}) async-start(f32[32,1,8]{2,1,0:T(1,128)} %broadcast_in_dim.2), calls=%async_computation | async-start | bytes 32768 | tf_op jit(solution)/shard_map/all_to_all | solution.py:293
  89.2 9.6 %collective-permute-start.9 = (f32[3,64,64]{1,2,0:T(8,128)S(1)}, f32[3,64,64]{1,2,0:T(8,128)S(1)}, u32[]{:S(2)}, u32[]{:S(2)}) collective-permute-start(f32[3,64,64]{1,2,0:T(8,128)S(1)} %convolution_bitcast_fusion), channel_id=1, source_target_pairs={{0,3},{1,0},{2,1},{3,2},{4,7},{5,4},{6,5},{7,6},{8,11},{9,8},{10,9... | collective-permute-start | bytes 147464 | tf_op jit(solution)/shard_map/ppermute | solution.py:283

commit v13 on v12

--- a/solution.py
+++ b/solution.py
@@ -55,7 +55,7 @@
 
 
 LANES = 128
-HELPER_SLACK = 320
+OWN_SHARE = 1040
 
 
 def sweep_kernel(near_ref, far_ref, range_ref, home_ref, *refs, pair_cap, far_offset):
@@ -226,13 +226,7 @@
     partner_lists = lax.ppermute(lists, "brick", partner)
     partner_blocks = lax.ppermute(jnp.stack(blocks), "brick", partner)
     own_count = pair_count[0, 0]
-    partner_count = partner_lists[2 * pair_cap]
-    both = own_count + partner_count
-    share = (both + HELPER_SLACK + 1) // 2
-    own_keep = jnp.where(own_count > partner_count, jnp.minimum(own_count, share), own_count)
-    partner_keep = jnp.where(
-        partner_count > own_count, jnp.minimum(partner_count, share), partner_count
-    )
+    own_keep = jnp.minimum(own_count, OWN_SHARE)
     own_fields = sweep(
         home_cols,
         blocks,
@@ -243,6 +237,9 @@
     )
 
     after_own = (0.0 * own_fields[0, 0]).astype(jnp.int32)
+    partner_lists = partner_lists + after_own
+    partner_count = partner_lists[2 * pair_cap]
+    partner_keep = jnp.minimum(partner_count, OWN_SHARE)
 
     def help_partner():
         partner_cols = partner_blocks[0].transpose(0, 2, 1).reshape(atom_count, 8)

time: 101 us -> 88.3 us (0.87)
  waiting for transfers between devices: 14.8 us -> 5.55 us
  between operations: 8.06 us -> 5.47 us
  matrix products: 2.27 us -> 0.99 us
    ppermute x1, waiting for transfers between devices: 9.95 us -> 0.01 us  [on_device(): partner_lists = lax.ppermute(lists, 'brick', partner)]
    ppermute x3, starting transfers between devices: 8.48 us -> 4.92 us  [to_owners(): lax.ppermute(part, 'plane', [(i, (i + step) % planes) for i in range(plan...]
    all_to_all x1, starting transfers between devices: 21.5 us -> 23.7 us  [on_device(): lax.all_to_all(sums_out, ('brick', 'plane'), split_axis=0, concat_axis=0,...]
    ppermute x1, starting transfers between devices: 5.47 us -> 7.06 us  [on_device(): totals = own_fields + lax.ppermute(helped, 'brick', partner)]
    dot_general x4, matrix products: 2.27 us -> 0.99 us  [to_owners(): jnp.einsum('ts,ctj->csj', placer, tiles, precision=lax.Precision.HIGHEST)]
  transfers between devices with their start and end apart: 11 -> 11, of which waited for: 4 -> 3; matrix products, arithmetic and copies ran while one was open for 16% -> 16% of each run, Pallas kernels for 11% -> 13%
where the time goes in v13:
time: 88.3 us; the launch traced here: 87.1 us
  starting transfers between devices  45.5 us (52%)
  Pallas kernels  11.3 us (13%)
  local copies, waits for them, and re-layouts  9.34 us (11%)
  other arithmetic  8.94 us (10%)
  waiting for transfers between devices  5.55 us (6%)
  between operations  5.47 us (6%)
  matrix products  0.99 us (1%)
    all_to_all x1, starting transfers between devices, on_device(): lax.all_to_all(sums_out, ('brick', 'plane'), split_axis=0, concat_axis=0,...  23.7 us
    pallas_call x1, Pallas kernels, sweep(): pl.pallas_call(kernel, out_shape=jax.ShapeDtypeStruct((2, atom_count), jn...  11.3 us
    ppermute x4, starting transfers between devices, shifted_from(): return lax.ppermute(block, axis, pairs)  7.78 us
    ppermute x1, starting transfers between devices, on_device(): totals = own_fields + lax.ppermute(helped, 'brick', partner)  7.06 us
    ppermute x3, starting transfers between devices, to_owners(): lax.ppermute(part, 'plane', [(i, (i + step) % planes) for i in range(plan...  4.92 us
    all_to_all x1, waiting for transfers between devices, on_device(): lax.all_to_all(sums_out, ('brick', 'plane'), split_axis=0, concat_axis=0,...  3.3 us
    unnamed x15, local copies, waits for them, and re-layouts  3.18 us
    unnamed x3, other arithmetic  2.71 us
  transfers between devices with their start and end apart: 11, of which 3 were waited for; matrix products, arithmetic and copies ran while one was open for 16% of the time, Pallas kernels for 13%

profile of v13, /device:TPU:0, one launch (start us, length us, event | category | flops | bytes accessed | tf_op | source)
XLA Modules:
  0.0 87.1 jit_solution(12292461544295621161)
XLA Ops:
  0.6 0.9 %select_reduce_fusion.2 = (f32[4096]{0:T(1024)S(1)}, f32[4096]{0:T(1024)S(1)}, f32[4096]{0:T(1024)S(1)}) fusion(f32[8]{0:T(128)} %param.23, s32[4096]{0:T(1024)} %bitcast.116, f32[8]{0:T(128)} %param.24, f32[8]{0:T(128)} %param.25), kind=kLoop, calls=%fused_computation.21 | loop fusion | flops 217088 | bytes 65632 | tf_op jit(solution)/shard_map/reduce_sum | solution.py:43
  1.6 0.8 copy.33
  2.4 0.9 concatenate.27
  3.3 0.5 collective-permute-start
  3.8 2.9 %collective-permute-start.1 = (f32[32,8,128]{2,1,0:T(8,128)S(1)}, f32[32,8,128]{2,1,0:T(8,128)S(1)}, u32[]{:S(2)}, u32[]{:S(2)}) collective-permute-start(f32[32,8,128]{2,1,0:T(8,128)S(1)} %bitcast.100), channel_id=1, source_target_pairs={{0,28},{4,0},{8,4},{12,8},{16,12},{20,16},{24,20},{28,24},{1,29},{... | collective-permute-start | bytes 393224 | tf_op jit(solution)/shard_map/ppermute | solution.py:26
  6.8 2.3 %collective-permute-start.2 = (f32[32,8,128]{2,1,0:T(8,128)S(1)}, f32[32,8,128]{2,1,0:T(8,128)S(1)}, u32[]{:S(2)}, u32[]{:S(2)}) collective-permute-start(f32[32,8,128]{2,1,0:T(8,128)S(1)} %bitcast.101), channel_id=1, source_target_pairs={{0,1},{1,2},{2,3},{3,0},{4,5},{5,6},{6,7},{7,4},{8,9},{9,10},{10,1... | collective-permute-start | bytes 393224 | tf_op jit(solution)/shard_map/ppermute | solution.py:26
  9.0 2.0 %collective-permute-start.3 = (f32[32,8,128]{2,1,0:T(8,128)S(1)}, f32[32,8,128]{2,1,0:T(8,128)S(1)}, u32[]{:S(2)}, u32[]{:S(2)}) collective-permute-start(f32[32,8,128]{2,1,0:T(8,128)S(1)} %bitcast.102), channel_id=1, source_target_pairs={{0,3},{1,0},{2,1},{3,2},{4,7},{5,4},{6,5},{7,6},{8,11},{9,8},{10,9... | collective-permute-start | bytes 393224 | tf_op jit(solution)/shard_map/ppermute | solution.py:26
  11.1 0.6 bitcast_dynamic-update-slice_fusion
  11.7 0.7 bitcast_dynamic-update-slice_fusion.4
  12.4 0.7 bitcast_dynamic-update-slice_fusion.3
  13.1 2.1 %collective-permute-done.2.refs_3_ = f32[32,8,128]{2,1,0:T(8,128)S(1)} collective-permute-done((f32[32,8,128]{2,1,0:T(8,128)S(1)}, f32[32,8,128]{2,1,0:T(8,128)S(1)}, u32[]{:S(2)}, u32[]{:S(2)}) %collective-permute-start.2) | collective-permute-done | bytes 131104 | tf_op jit(solution)/shard_map/ppermute | solution.py:26
  15.2 0.7 bitcast_dynamic-update-slice_fusion.2
  15.9 0.7 bitcast_dynamic-update-slice_fusion.1
  16.6 1.5 %collective-permute-start.5 = (f32[5,32,8,128]{3,2,1,0:T(8,128)}, f32[5,32,8,128]{3,2,1,0:T(8,128)S(1)}, u32[]{:S(2)}, u32[]{:S(2)}) collective-permute-start(f32[5,32,8,128]{3,2,1,0:T(8,128)} %bitcast_dynamic-update-slice_fusion.1), channel_id=1, source_target_pairs={{0,16},{4,20},{8,24},{12,28},{16,0},{20,4},{24,8},{28,12},{1,17},{... | collective-permute-start | bytes 1966088 | tf_op jit(solution)/shard_map/ppermute | solution.py:227
  18.8 0.7 reduce.2
  19.5 0.7 reduce.3
  20.8 1.2 %subtract_bitcast_fusion.3 = (s32[64]{0:T(128)S(1)}, s32[64]{0:T(128)}, s32[64]{0:T(128)S(1)}, s32[64]{0:T(128)S(1)}) fusion(s32[1,1,64]{2,1,0:T(1,128)} %param.22, s32[]{:T(128)S(6)} %mul.79, s32[]{:T(128)S(6)} %mul.80, s32[]{:T(128)S(6)} %mul.82, s32[]{:T(128)S(6)} %mul.81), kind=kLoop, calls=%fused_computation.58 | loop fusion | flops 256 | bytes 1296 | tf_op jit(solution)/shard_map/sub | solution.py:274
  22.1 0.6 copy.34.home_ref
  22.7 11.3 %shard_map.139 = f32[2,4096]{1,0:T(2,128)S(1)} custom-call(s32[1,1,1496]{2,1,0:T(1,128)S(1)} %copy-done, s32[1,1,1496]{2,1,0:T(1,128)S(1)} %copy-done.1, s32[1,2]{1,0:T(1,128)S(1)} %add_bitcast_fusion.range_ref, f32[4096,8]{1,0:T(8,128)S(1)} %copy.34.home_ref, f32[32,8,128]{2,1,0:T(8,128)S(1)} %bitcast.104, f32[32,8,128]{2,1,0:T(8,128)S(1)} %collective-permute-done.refs_1_, ...), custom_call_target="tpu_custom_call" | custom-call | tf_op jit(solution)/shard_map/pallas_call | solution.py:171
  35.2 0.6 slice.58
  37.2 7.1 %collective-permute-start.6 = (f32[2,4096]{1,0:T(2,128)S(1)}, f32[2,4096]{1,0:T(2,128)S(1)}, u32[]{:S(2)}, u32[]{:S(2)}) collective-permute-start(f32[2,4096]{1,0:T(2,128)S(1)} %get-tuple-element.48), channel_id=1, source_target_pairs={{0,16},{4,20},{8,24},{12,28},{16,0},{20,4},{24,8},{28,12},{1,17},{... | collective-permute-start | bytes 98312 | tf_op jit(solution)/shard_map/ppermute | solution.py:261
  44.8 1.3 %fusion.25 = (f32[4096]{0:T(1024)S(1)}, f32[]{:T(128)}) fusion(f32[1,1,4096]{2,1,0:T(1,128)S(1)} %copy-done.2, f32[]{:T(128)} %broadcast.108), kind=kLoop, calls=%fused_computation.64 | loop fusion | flops 4095 | bytes 32776 | tf_op args[1]
  46.9 1.2 %collective-permute-start.7 = (f32[3,64,64]{1,2,0:T(8,128)S(1)}, f32[3,64,64]{1,2,0:T(8,128)S(1)}, u32[]{:S(2)}, u32[]{:S(2)}) collective-permute-start(f32[3,64,64]{1,2,0:T(8,128)S(1)} %convolution_bitcast_fusion.2), channel_id=1, source_target_pairs={{0,1},{1,2},{2,3},{3,0},{4,5},{5,6},{6,7},{7,4},{8,9},{9,10},{10,1... | collective-permute-start | bytes 147464 | tf_op jit(solution)/shard_map/ppermute | solution.py:280
  48.4 0.6 fusion.20
  49.0 2.0 %select_maximum_fusion = f32[8]{0:T(128)S(1)} fusion(f32[1]{0:T(128)} %bitcast.32, f32[1]{0:T(128)} %bitcast.31, f32[1]{0:T(128)} %bitcast.10), kind=kLoop, calls=%fused_computation.51 | loop fusion | flops 48 | bytes 44 | tf_op jit(solution)/shard_map/stack | solution.py:286
  51.0 0.6 broadcast_in_dim.2
  51.6 23.7 %all-to-all-start = ((f32[32,1,8]{2,1,0:T(1,128)}), f32[32,1,8]{2,1,0:T(1,128)S(1)}, u32[]{:S(2)}, u32[]{:S(2)}) async-start(f32[32,1,8]{2,1,0:T(1,128)} %broadcast_in_dim.2), calls=%async_computation | async-start | bytes 32768 | tf_op jit(solution)/shard_map/all_to_all | solution.py:290
  75.6 3.7 %collective-permute-start.9 = (f32[3,64,64]{1,2,0:T(8,128)S(1)}, f32[3,64,64]{1,2,0:T(8,128)S(1)}, u32[]{:S(2)}, u32[]{:S(2)}) collective-permute-start(f32[3,64,64]{1,2,0:T(8,128)S(1)} %convolution_bitcast_fusion), channel_id=1, source_target_pairs={{0,3},{1,0},{2,1},{3,2},{4,7},{5,4},{6,5},{7,6},{8,11},{9,8},{10,9... | collective-permute-start | bytes 147464 | tf_op jit(solution)/shard_map/ppermute | solution.py:280
  79.3 3.3 %all-to-all-done = f32[32,1,8]{2,1,0:T(1,128)S(1)} async-done(((f32[32,1,8]{2,1,0:T(1,128)}), f32[32,1,8]{2,1,0:T(1,128)S(1)}, u32[]{:S(2)}, u32[]{:S(2)}) %all-to-all-start) | async-done | bytes 1056 | tf_op jit(solution)/shard_map/all_to_all | solution.py:290
  82.6 0.6 fusion.26
  85.2 0.6 fusion.15
  86.5 0.6 subtract_add_fusion
  (48 shorter events, 3.9 us)
Async XLA Ops:
  1.5 21.1 %copy-start = (s32[1,1,1496]{2,1,0:T(1,128)S(1)}, s32[1,1,1496]{2,1,0:T(1,128)}, u32[]{:S(2)}) copy-start(s32[1,1,1496]{2,1,0:T(1,128)} %near_ref.1) | copy-start | bytes 17956
  1.5 21.1 %copy-start.1 = (s32[1,1,1496]{2,1,0:T(1,128)S(1)}, s32[1,1,1496]{2,1,0:T(1,128)}, u32[]{:S(2)}) copy-start(s32[1,1,1496]{2,1,0:T(1,128)} %far_ref.1) | copy-start | bytes 17956
  3.3 8.4 %collective-permute-start = (f32[32,8,128]{2,1,0:T(8,128)S(1)}, f32[32,8,128]{2,1,0:T(8,128)S(1)}, u32[]{:S(2)}, u32[]{:S(2)}) collective-permute-start(f32[32,8,128]{2,1,0:T(8,128)S(1)} %bitcast.99), channel_id=1, source_target_pairs={{0,4},{4,8},{8,12},{12,16},{16,20},{20,24},{24,28},{28,0},{1,5},{5... | collective-permute-start | bytes 393224 | tf_op jit(solution)/shard_map/ppermute | solution.py:26
  3.8 8.5 %collective-permute-start.1 = (f32[32,8,128]{2,1,0:T(8,128)S(1)}, f32[32,8,128]{2,1,0:T(8,128)S(1)}, u32[]{:S(2)}, u32[]{:S(2)}) collective-permute-start(f32[32,8,128]{2,1,0:T(8,128)S(1)} %bitcast.100), channel_id=1, source_target_pairs={{0,28},{4,0},{8,4},{12,8},{16,12},{20,16},{24,20},{28,24},{1,29},{... | collective-permute-start | bytes 393224 | tf_op jit(solution)/shard_map/ppermute | solution.py:26
  6.8 8.4 %collective-permute-start.2 = (f32[32,8,128]{2,1,0:T(8,128)S(1)}, f32[32,8,128]{2,1,0:T(8,128)S(1)}, u32[]{:S(2)}, u32[]{:S(2)}) collective-permute-start(f32[32,8,128]{2,1,0:T(8,128)S(1)} %bitcast.101), channel_id=1, source_target_pairs={{0,1},{1,2},{2,3},{3,0},{4,5},{5,6},{6,7},{7,4},{8,9},{9,10},{10,1... | collective-permute-start | bytes 393224 | tf_op jit(solution)/shard_map/ppermute | solution.py:26
  9.0 6.9 %collective-permute-start.3 = (f32[32,8,128]{2,1,0:T(8,128)S(1)}, f32[32,8,128]{2,1,0:T(8,128)S(1)}, u32[]{:S(2)}, u32[]{:S(2)}) collective-permute-start(f32[32,8,128]{2,1,0:T(8,128)S(1)} %bitcast.102), channel_id=1, source_target_pairs={{0,3},{1,0},{2,1},{3,2},{4,7},{5,4},{6,5},{7,6},{8,11},{9,8},{10,9... | collective-permute-start | bytes 393224 | tf_op jit(solution)/shard_map/ppermute | solution.py:26
  16.6 20.5 %collective-permute-start.5 = (f32[5,32,8,128]{3,2,1,0:T(8,128)}, f32[5,32,8,128]{3,2,1,0:T(8,128)S(1)}, u32[]{:S(2)}, u32[]{:S(2)}) collective-permute-start(f32[5,32,8,128]{3,2,1,0:T(8,128)} %bitcast_dynamic-update-slice_fusion.1), channel_id=1, source_target_pairs={{0,16},{4,20},{8,24},{12,28},{16,0},{20,4},{24,8},{28,12},{1,17},{... | collective-permute-start | bytes 1966088 | tf_op jit(solution)/shard_map/ppermute | solution.py:227
  20.3 14.9 %collective-permute-start.4 = (s32[2993]{0:T(1024)S(1)}, s32[2993]{0:T(1024)S(1)}, u32[]{:S(2)}, u32[]{:S(2)}) collective-permute-start(s32[2993]{0:T(1024)S(1)} %concatenate.28), channel_id=1, source_target_pairs={{0,16},{4,20},{8,24},{12,28},{16,0},{20,4},{24,8},{28,12},{1,17},{... | collective-permute-start | bytes 35924 | tf_op jit(solution)/shard_map/ppermute | solution.py:226
  37.1 7.6 %copy-start.2 = (f32[1,1,4096]{2,1,0:T(1,128)S(1)}, f32[1,1,4096]{2,1,0:T(1,128)}, u32[]{:S(2)}) copy-start(f32[1,1,4096]{2,1,0:T(1,128)} %param.15) | copy-start | bytes 49156
  37.1 9.5 %copy-start.4 = (s32[64]{0:T(128)S(1)}, s32[64]{0:T(128)}, u32[]{:S(2)}) copy-start(s32[64]{0:T(128)} %get-tuple-element.42) | copy-start | bytes 772
  37.2 49.3 %copy-start.3 = (f32[1,1,4096]{2,1,0:T(1,128)S(1)}, f32[1,1,4096]{2,1,0:T(1,128)}, u32[]{:S(2)}) copy-start(f32[1,1,4096]{2,1,0:T(1,128)} %param.16) | copy-start | bytes 49156
  37.2 9.2 %collective-permute-start.6 = (f32[2,4096]{1,0:T(2,128)S(1)}, f32[2,4096]{1,0:T(2,128)S(1)}, u32[]{:S(2)}, u32[]{:S(2)}) collective-permute-start(f32[2,4096]{1,0:T(2,128)S(1)} %get-tuple-element.48), channel_id=1, source_target_pairs={{0,16},{4,20},{8,24},{12,28},{16,0},{20,4},{24,8},{28,12},{1,17},{... | collective-permute-start | bytes 98312 | tf_op jit(solution)/shard_map/ppermute | solution.py:261
  46.9 39.0 %collective-permute-start.7 = (f32[3,64,64]{1,2,0:T(8,128)S(1)}, f32[3,64,64]{1,2,0:T(8,128)S(1)}, u32[]{:S(2)}, u32[]{:S(2)}) collective-permute-start(f32[3,64,64]{1,2,0:T(8,128)S(1)} %convolution_bitcast_fusion.2), channel_id=1, source_target_pairs={{0,1},{1,2},{2,3},{3,0},{4,5},{5,6},{6,7},{7,4},{8,9},{9,10},{10,1... | collective-permute-start | bytes 147464 | tf_op jit(solution)/shard_map/ppermute | solution.py:280
  48.3 37.6 %collective-permute-start.8 = (f32[3,64,64]{1,2,0:T(8,128)S(1)}, f32[3,64,64]{1,2,0:T(8,128)S(1)}, u32[]{:S(2)}, u32[]{:S(2)}) collective-permute-start(f32[3,64,64]{1,2,0:T(8,128)S(1)} %convolution_bitcast_fusion.1), channel_id=1, source_target_pairs={{0,2},{1,3},{2,0},{3,1},{4,6},{5,7},{6,4},{7,5},{8,10},{9,11},{10,... | collective-permute-start | bytes 147464 | tf_op jit(solution)/shard_map/ppermute | solution.py:280
  51.6 30.9 %all-to-all-start = ((f32[32,1,8]{2,1,0:T(1,128)}), f32[32,1,8]{2,1,0:T(1,128)S(1)}, u32[]{:S(2)}, u32[]{:S(2)}) async-start(f32[32,1,8]{2,1,0:T(1,128)} %broadcast_in_dim.2), calls=%async_computation | async-start | bytes 32768 | tf_op jit(solution)/shard_map/all_to_all | solution.py:290
  75.6 10.3 %collective-permute-start.9 = (f32[3,64,64]{1,2,0:T(8,128)S(1)}, f32[3,64,64]{1,2,0:T(8,128)S(1)}, u32[]{:S(2)}, u32[]{:S(2)}) collective-permute-start(f32[3,64,64]{1,2,0:T(8,128)S(1)} %convolution_bitcast_fusion), channel_id=1, source_target_pairs={{0,3},{1,0},{2,1},{3,2},{4,7},{5,4},{6,5},{7,6},{8,11},{9,8},{10,9... | collective-permute-start | bytes 147464 | tf_op jit(solution)/shard_map/ppermute | solution.py:280

commit v14 on v11

--- a/solution.py
+++ b/solution.py
@@ -121,7 +121,7 @@
         inv_spacing = lax.rsqrt(shifted)
         spacing = shifted * inv_spacing
         inv_width = lax.rsqrt(near_q(3) + rows[3:4])
-        taper = jnp.maximum(1.0 - dist_sq * (1.0 / (cutoff * cutoff)), 0.0)
+        taper = jnp.maximum(cutoff * cutoff - dist_sq, 0.0)
         kernel = lax.erf(inv_width * spacing) * inv_spacing * (taper * taper)
         self_half = jnp.where(
             left, (cand_a == home_a).astype(jnp.int32), (cand_b == home_b).astype(jnp.int32)
@@ -130,20 +130,21 @@
         return kernel, rows, base_a, base_b
 
     def accumulate(kernel, rows, base_a, base_b):
+        charges = rows[4:6] * (1.0 / (cutoff * cutoff)) ** 2
         for c in range(2):
-            contribution = kernel * rows[4 + c:5 + c]
+            contribution = kernel * charges[c:c + 1]
             slot_a = acc_ref.at[c, pl.ds(base_a, TILE), :]
             pltpu.store(slot_a, slot_a[...] + contribution, mask=left_full)
             slot_b = acc_ref.at[c, pl.ds(base_b, TILE), :]
             pltpu.store(slot_b, slot_b[...] + contribution, mask=right_full)
 
     def body(k, carry):
-        parts = [pair_kernel(16 * k + 2 * u) for u in range(8)]
+        parts = [pair_kernel(24 * k + 2 * u) for u in range(12)]
         for part in parts:
             accumulate(*part)
         return carry
 
-    lax.fori_loop(0, (total + 15) // 16, body, 0)
+    lax.fori_loop(0, (total + 23) // 24, body, 0)
     ones = jnp.ones((8, LANES), jnp.float32)
     fields = []
     for c in range(2):

time: 75.9 us -> 75 us (0.988)
  Pallas kernels: 14.8 us -> 11.9 us
  starting transfers between devices: 41.9 us -> 43.9 us
    pallas_call x1, Pallas kernels: 14.8 us -> 11.9 us  [sweep(): pl.pallas_call(sweep_kernel, out_shape=(jax.ShapeDtypeStruct((2, atom_cou...]
    all_to_all x1, starting transfers between devices: 29.3 us -> 31.2 us  [on_device(): lax.all_to_all(sums_out, ('brick', 'plane'), split_axis=0, concat_axis=0,...]
where the time goes in v14:
time: 75 us; the launch traced here: 74.5 us
  starting transfers between devices  43.9 us (59%)
  Pallas kernels  11.9 us (16%)
  waiting for transfers between devices  6.38 us (9%)
  local copies, waits for them, and re-layouts  4.94 us (7%)
  between operations  3.48 us (5%)
  other arithmetic  2.93 us (4%)
  matrix products  1 us (1%)
    all_to_all x1, starting transfers between devices, on_device(): lax.all_to_all(sums_out, ('brick', 'plane'), split_axis=0, concat_axis=0,...  31.2 us
    pallas_call x1, Pallas kernels, sweep(): pl.pallas_call(sweep_kernel, out_shape=(jax.ShapeDtypeStruct((2, atom_cou...  11.9 us
    ppermute x4, starting transfers between devices, shifted_from(): return lax.ppermute(block, axis, pairs)  7.78 us
    ppermute x3, starting transfers between devices, to_owners(): lax.ppermute(part, 'plane', [(i, (i + step) % planes) for i in range(plan...  4.86 us
    ppermute x3, waiting for transfers between devices, to_owners(): lax.ppermute(part, 'plane', [(i, (i + step) % planes) for i in range(plan...  3.58 us
    ppermute x4, waiting for transfers between devices, shifted_from(): return lax.ppermute(block, axis, pairs)  2.01 us
    concatenate x2, local copies, waits for them, and re-layouts, on_device(): jnp.concatenate([positions.reshape(3, atom_count), jnp.square(radius)[Non...  1.72 us
  transfers between devices with their start and end apart: 8, of which 4 were waited for; matrix products, arithmetic and copies ran while one was open for 7% of the time, Pallas kernels for 0%

profile of v14, /device:TPU:0, one launch (start us, length us, event | category | flops | bytes accessed | tf_op | source)
XLA Modules:
  0.0 74.5 jit_solution(8623646690928564320)
XLA Ops:
  0.7 0.9 %copy.31 = f32[3,32,128]{2,0,1:T(4,128)S(1)} copy(f32[3,32,128]{2,1,0:T(8,128)} %bitcast.65) | data formatting | bytes 98304 | tf_op jit(solution)/shard_map/concatenate | solution.py:218
  1.5 0.9 %select_reduce_fusion.1 = (f32[4096]{0:T(1024)S(1)}, f32[4096]{0:T(1024)S(1)}, f32[4096]{0:T(1024)S(1)}) fusion(f32[8]{0:T(128)} %param.21, s32[4096]{0:T(1024)} %bitcast.67, f32[8]{0:T(128)} %param.22, f32[8]{0:T(128)} %param.23), kind=kLoop, calls=%fused_computation.8 | loop fusion | flops 217088 | bytes 65632 | tf_op jit(solution)/shard_map/reduce_sum | solution.py:41
  2.5 0.9 %concatenate.14 = f32[8,32,128]{2,0,1:T(8,128)S(1)} concatenate(f32[3,32,128]{2,0,1:T(4,128)S(1)} %copy.31, f32[1,32,128]{2,0,1:T(1,128)S(1)} %bitcast.63, f32[1,32,128]{2,0,1:T(1,128)} %bitcast.64, f32[1,32,128]{2,0,1:T(1,128)} %bitcast.66, f32[2,32,128]{2,0,1:T(2,128)S(1)} %broadcast_in_dim.6), dimensions={0} | concatenate | bytes 262144 | tf_op jit(solution)/shard_map/concatenate | solution.py:218
  3.3 0.5 collective-permute-start
  3.9 2.9 %collective-permute-start.1 = (f32[32,8,128]{2,1,0:T(8,128)S(1)}, f32[32,8,128]{2,1,0:T(8,128)S(1)}, u32[]{:S(2)}, u32[]{:S(2)}) collective-permute-start(f32[32,8,128]{2,1,0:T(8,128)S(1)} %bitcast.55), channel_id=1, source_target_pairs={{0,28},{4,0},{8,4},{12,8},{16,12},{20,16},{24,20},{28,24},{1,29},{... | collective-permute-start | bytes 393224 | tf_op jit(solution)/shard_map/ppermute | solution.py:24
  6.8 2.3 %collective-permute-start.2 = (f32[32,8,128]{2,1,0:T(8,128)S(1)}, f32[32,8,128]{2,1,0:T(8,128)S(1)}, u32[]{:S(2)}, u32[]{:S(2)}) collective-permute-start(f32[32,8,128]{2,1,0:T(8,128)S(1)} %bitcast.56), channel_id=1, source_target_pairs={{0,1},{1,2},{2,3},{3,0},{4,5},{5,6},{6,7},{7,4},{8,9},{9,10},{10,1... | collective-permute-start | bytes 393224 | tf_op jit(solution)/shard_map/ppermute | solution.py:24
  9.1 2.0 %collective-permute-start.3 = (f32[32,8,128]{2,1,0:T(8,128)S(1)}, f32[32,8,128]{2,1,0:T(8,128)S(1)}, u32[]{:S(2)}, u32[]{:S(2)}) collective-permute-start(f32[32,8,128]{2,1,0:T(8,128)S(1)} %bitcast.57), channel_id=1, source_target_pairs={{0,3},{1,0},{2,1},{3,2},{4,7},{5,4},{6,5},{7,6},{8,11},{9,8},{10,9... | collective-permute-start | bytes 393224 | tf_op jit(solution)/shard_map/ppermute | solution.py:24
  11.8 0.6 copy.32.home_ref
  12.5 0.1 copy.35
  12.6 0.5 broadcast.82
  13.1 0.7 reduce.8
  13.8 0.1 copy.34
  14.0 1.2 %collective-permute-done.2.refs_3_ = f32[32,8,128]{2,1,0:T(8,128)S(1)} collective-permute-done((f32[32,8,128]{2,1,0:T(8,128)S(1)}, f32[32,8,128]{2,1,0:T(8,128)S(1)}, u32[]{:S(2)}, u32[]{:S(2)}) %collective-permute-start.2) | collective-permute-done | bytes 131104 | tf_op jit(solution)/shard_map/ppermute | solution.py:24
  15.2 0.8 %collective-permute-done.3.refs_4_ = f32[32,8,128]{2,1,0:T(8,128)S(1)} collective-permute-done((f32[32,8,128]{2,1,0:T(8,128)S(1)}, f32[32,8,128]{2,1,0:T(8,128)S(1)}, u32[]{:S(2)}, u32[]{:S(2)}) %collective-permute-start.3) | collective-permute-done | bytes 131104 | tf_op jit(solution)/shard_map/ppermute | solution.py:24
  16.0 11.9 %shard_map.139 = (f32[2,4096]{1,0:T(2,128)S(1)}, f32[32,8]{1,0:T(8,128)}) custom-call(s32[1,1,1496]{2,1,0:T(1,128)S(1)} %copy-done, s32[1,1,1496]{2,1,0:T(1,128)S(1)} %copy-done.1, s32[1,1]{1,0:T(1,128)S(6)} %copy.39.count_ref, f32[4096,8]{1,0:T(8,128)S(1)} %copy.32.home_ref, f32[1,4096]{1,0:T(1,128)S(1)} %bitcast.62, f32[1,4096]{1,0:T(1,128)S(1)} %bitcast.60, ...), custom_call_target="tpu_custom_call" | custom-call | tf_op jit(solution)/shard_map/pallas_call | solution.py:179
  27.9 31.2 %all-to-all-start = ((f32[32,1,8]{2,1,0:T(1,128)}), f32[32,1,8]{2,1,0:T(1,128)S(1)}, u32[]{:S(2)}, u32[]{:S(2)}) async-start(f32[32,1,8]{2,1,0:T(1,128)} %bitcast.11), calls=%async_computation | async-start | bytes 32768 | tf_op jit(solution)/shard_map/all_to_all | solution.py:266
  59.1 0.6 slice_bitcast_fusion
  59.8 0.1 copy.36
  59.9 0.3 convolution_bitcast_fusion
  60.2 3.7 %collective-permute-start.6 = (f32[3,64,64]{1,2,0:T(8,128)S(1)}, f32[3,64,64]{1,2,0:T(8,128)S(1)}, u32[]{:S(2)}, u32[]{:S(2)}) collective-permute-start(f32[3,64,64]{1,2,0:T(8,128)S(1)} %convolution_bitcast_fusion), channel_id=1, source_target_pairs={{0,3},{1,0},{2,1},{3,2},{4,7},{5,4},{6,5},{7,6},{8,11},{9,8},{10,9... | collective-permute-start | bytes 147464 | tf_op jit(solution)/shard_map/ppermute | solution.py:260
  63.8 0.2 convolution_bitcast_fusion.1
  64.2 0.2 convolution_bitcast_fusion.2
  64.4 1.1 %collective-permute-start.4 = (f32[3,64,64]{1,2,0:T(8,128)S(1)}, f32[3,64,64]{1,2,0:T(8,128)S(1)}, u32[]{:S(2)}, u32[]{:S(2)}) collective-permute-start(f32[3,64,64]{1,2,0:T(8,128)S(1)} %convolution_bitcast_fusion.2), channel_id=1, source_target_pairs={{0,1},{1,2},{2,3},{3,0},{4,5},{5,6},{6,7},{7,4},{8,9},{9,10},{10,1... | collective-permute-start | bytes 147464 | tf_op jit(solution)/shard_map/ppermute | solution.py:260
  65.5 0.8 %all-to-all-done = f32[32,1,8]{2,1,0:T(1,128)S(1)} async-done(((f32[32,1,8]{2,1,0:T(1,128)}), f32[32,1,8]{2,1,0:T(1,128)S(1)}, u32[]{:S(2)}, u32[]{:S(2)}) %all-to-all-start) | async-done | bytes 1056 | tf_op jit(solution)/shard_map/all_to_all | solution.py:266
  66.4 0.7 fusion.21
  69.0 0.6 bitcast_divide_fusion
  69.6 3.6 %collective-permute-done.5 = f32[3,64,64]{1,2,0:T(8,128)S(1)} collective-permute-done((f32[3,64,64]{1,2,0:T(8,128)S(1)}, f32[3,64,64]{1,2,0:T(8,128)S(1)}, u32[]{:S(2)}, u32[]{:S(2)}) %collective-permute-start.5) | collective-permute-done | bytes 49184 | tf_op jit(solution)/shard_map/ppermute | solution.py:260
  73.2 0.2 fusion.2
  73.5 0.1 copy.38
  73.6 0.1 mul.83
  73.8 0.1 mul.80
  73.9 0.6 subtract_add_fusion
  (24 shorter events, 0.5 us)
Async XLA Ops:
  0.6 12.5 %copy-start.2 = (f32[1,1,4096]{2,1,0:T(1,128)S(1)}, f32[1,1,4096]{2,1,0:T(1,128)}, u32[]{:S(2)}) copy-start(f32[1,1,4096]{2,1,0:T(1,128)} %param.13) | copy-start | bytes 49156
  0.6 13.3 %copy-start.4 = (s32[1,1,64]{2,1,0:T(1,128)S(1)}, s32[1,1,64]{2,1,0:T(1,128)}, u32[]{:S(2)}) copy-start(s32[1,1,64]{2,1,0:T(1,128)} %param.20) | copy-start | bytes 772
  0.7 15.3 %copy-start = (s32[1,1,1496]{2,1,0:T(1,128)S(1)}, s32[1,1,1496]{2,1,0:T(1,128)}, u32[]{:S(2)}) copy-start(s32[1,1,1496]{2,1,0:T(1,128)} %near_ref.1) | copy-start | bytes 17956
  0.7 15.3 %copy-start.1 = (s32[1,1,1496]{2,1,0:T(1,128)S(1)}, s32[1,1,1496]{2,1,0:T(1,128)}, u32[]{:S(2)}) copy-start(s32[1,1,1496]{2,1,0:T(1,128)} %far_ref.1) | copy-start | bytes 17956
  3.3 10.6 %collective-permute-start = (f32[32,8,128]{2,1,0:T(8,128)S(1)}, f32[32,8,128]{2,1,0:T(8,128)S(1)}, u32[]{:S(2)}, u32[]{:S(2)}) collective-permute-start(f32[32,8,128]{2,1,0:T(8,128)S(1)} %bitcast.54), channel_id=1, source_target_pairs={{0,4},{4,8},{8,12},{12,16},{16,20},{20,24},{24,28},{28,0},{1,5},{5... | collective-permute-start | bytes 393224 | tf_op jit(solution)/shard_map/ppermute | solution.py:24
  3.9 10.1 %collective-permute-start.1 = (f32[32,8,128]{2,1,0:T(8,128)S(1)}, f32[32,8,128]{2,1,0:T(8,128)S(1)}, u32[]{:S(2)}, u32[]{:S(2)}) collective-permute-start(f32[32,8,128]{2,1,0:T(8,128)S(1)} %bitcast.55), channel_id=1, source_target_pairs={{0,28},{4,0},{8,4},{12,8},{16,12},{20,16},{24,20},{28,24},{1,29},{... | collective-permute-start | bytes 393224 | tf_op jit(solution)/shard_map/ppermute | solution.py:24
  6.8 8.4 %collective-permute-start.2 = (f32[32,8,128]{2,1,0:T(8,128)S(1)}, f32[32,8,128]{2,1,0:T(8,128)S(1)}, u32[]{:S(2)}, u32[]{:S(2)}) collective-permute-start(f32[32,8,128]{2,1,0:T(8,128)S(1)} %bitcast.56), channel_id=1, source_target_pairs={{0,1},{1,2},{2,3},{3,0},{4,5},{5,6},{6,7},{7,4},{8,9},{9,10},{10,1... | collective-permute-start | bytes 393224 | tf_op jit(solution)/shard_map/ppermute | solution.py:24
  9.1 6.9 %collective-permute-start.3 = (f32[32,8,128]{2,1,0:T(8,128)S(1)}, f32[32,8,128]{2,1,0:T(8,128)S(1)}, u32[]{:S(2)}, u32[]{:S(2)}) collective-permute-start(f32[32,8,128]{2,1,0:T(8,128)S(1)} %bitcast.57), channel_id=1, source_target_pairs={{0,3},{1,0},{2,1},{3,2},{4,7},{5,4},{6,5},{7,6},{8,11},{9,8},{10,9... | collective-permute-start | bytes 393224 | tf_op jit(solution)/shard_map/ppermute | solution.py:24
  16.0 57.9 %copy-start.3 = (f32[1,1,4096]{2,1,0:T(1,128)S(1)}, f32[1,1,4096]{2,1,0:T(1,128)}, u32[]{:S(2)}) copy-start(f32[1,1,4096]{2,1,0:T(1,128)} %param.14) | copy-start | bytes 49156
  27.9 38.4 %all-to-all-start = ((f32[32,1,8]{2,1,0:T(1,128)}), f32[32,1,8]{2,1,0:T(1,128)S(1)}, u32[]{:S(2)}, u32[]{:S(2)}) async-start(f32[32,1,8]{2,1,0:T(1,128)} %bitcast.11), calls=%async_computation | async-start | bytes 32768 | tf_op jit(solution)/shard_map/all_to_all | solution.py:266
  60.2 9.5 %collective-permute-start.6 = (f32[3,64,64]{1,2,0:T(8,128)S(1)}, f32[3,64,64]{1,2,0:T(8,128)S(1)}, u32[]{:S(2)}, u32[]{:S(2)}) collective-permute-start(f32[3,64,64]{1,2,0:T(8,128)S(1)} %convolution_bitcast_fusion), channel_id=1, source_target_pairs={{0,3},{1,0},{2,1},{3,2},{4,7},{5,4},{6,5},{7,6},{8,11},{9,8},{10,9... | collective-permute-start | bytes 147464 | tf_op jit(solution)/shard_map/ppermute | solution.py:260
  64.1 9.1 %collective-permute-start.5 = (f32[3,64,64]{1,2,0:T(8,128)S(1)}, f32[3,64,64]{1,2,0:T(8,128)S(1)}, u32[]{:S(2)}, u32[]{:S(2)}) collective-permute-start(f32[3,64,64]{1,2,0:T(8,128)S(1)} %convolution_bitcast_fusion.1), channel_id=1, source_target_pairs={{0,2},{1,3},{2,0},{3,1},{4,6},{5,7},{6,4},{7,5},{8,10},{9,11},{10,... | collective-permute-start | bytes 147464 | tf_op jit(solution)/shard_map/ppermute | solution.py:260
  64.4 8.8 %collective-permute-start.4 = (f32[3,64,64]{1,2,0:T(8,128)S(1)}, f32[3,64,64]{1,2,0:T(8,128)S(1)}, u32[]{:S(2)}, u32[]{:S(2)}) collective-permute-start(f32[3,64,64]{1,2,0:T(8,128)S(1)} %convolution_bitcast_fusion.2), channel_id=1, source_target_pairs={{0,1},{1,2},{2,3},{3,0},{4,5},{5,6},{6,7},{7,4},{8,9},{9,10},{10,1... | collective-permute-start | bytes 147464 | tf_op jit(solution)/shard_map/ppermute | solution.py:260

commit v15 on v14

--- a/solution.py
+++ b/solution.py
@@ -139,12 +139,12 @@
             pltpu.store(slot_b, slot_b[...] + contribution, mask=right_full)
 
     def body(k, carry):
-        parts = [pair_kernel(24 * k + 2 * u) for u in range(12)]
+        parts = [pair_kernel(32 * k + 2 * u) for u in range(16)]
         for part in parts:
             accumulate(*part)
         return carry
 
-    lax.fori_loop(0, (total + 23) // 24, body, 0)
+    lax.fori_loop(0, (total + 31) // 32, body, 0)
     ones = jnp.ones((8, LANES), jnp.float32)
     fields = []
     for c in range(2):

time: 75 us -> 74.4 us (level)
  starting transfers between devices: 43.9 us -> 42 us
  Pallas kernels: 11.9 us -> 13.2 us
    all_to_all x1, starting transfers between devices: 31.2 us -> 29.4 us  [on_device(): lax.all_to_all(sums_out, ('brick', 'plane'), split_axis=0, concat_axis=0,...]
    pallas_call x1, Pallas kernels: 11.9 us -> 13.2 us  [sweep(): pl.pallas_call(sweep_kernel, out_shape=(jax.ShapeDtypeStruct((2, atom_cou...]
where the time goes in v15:
time: 74.4 us; the launch traced here: 73.9 us
  starting transfers between devices  42 us (56%)
  Pallas kernels  13.2 us (18%)
  waiting for transfers between devices  6.38 us (9%)
  local copies, waits for them, and re-layouts  4.94 us (7%)
  between operations  3.49 us (5%)
  other arithmetic  2.93 us (4%)
  matrix products  0.98 us (1%)
    all_to_all x1, starting transfers between devices, on_device(): lax.all_to_all(sums_out, ('brick', 'plane'), split_axis=0, concat_axis=0,...  29.4 us
    pallas_call x1, Pallas kernels, sweep(): pl.pallas_call(sweep_kernel, out_shape=(jax.ShapeDtypeStruct((2, atom_cou...  13.2 us
    ppermute x4, starting transfers between devices, shifted_from(): return lax.ppermute(block, axis, pairs)  7.78 us
    ppermute x3, starting transfers between devices, to_owners(): lax.ppermute(part, 'plane', [(i, (i + step) % planes) for i in range(plan...  4.86 us
    ppermute x3, waiting for transfers between devices, to_owners(): lax.ppermute(part, 'plane', [(i, (i + step) % planes) for i in range(plan...  3.58 us
    ppermute x4, waiting for transfers between devices, shifted_from(): return lax.ppermute(block, axis, pairs)  2.01 us
    concatenate x2, local copies, waits for them, and re-layouts, on_device(): jnp.concatenate([positions.reshape(3, atom_count), jnp.square(radius)[Non...  1.72 us
  transfers between devices with their start and end apart: 8, of which 4 were waited for; matrix products, arithmetic and copies ran while one was open for 7% of the time, Pallas kernels for 0%

profile of v15, /device:TPU:0, one launch (start us, length us, event | category | flops | bytes accessed | tf_op | source)
XLA Modules:
  0.0 73.9 jit_solution(12192542286768983783)
XLA Ops:
  0.7 0.9 %copy.31 = f32[3,32,128]{2,0,1:T(4,128)S(1)} copy(f32[3,32,128]{2,1,0:T(8,128)} %bitcast.65) | data formatting | bytes 98304 | tf_op jit(solution)/shard_map/concatenate | solution.py:218
  1.5 0.9 %select_reduce_fusion.1 = (f32[4096]{0:T(1024)S(1)}, f32[4096]{0:T(1024)S(1)}, f32[4096]{0:T(1024)S(1)}) fusion(f32[8]{0:T(128)} %param.21, s32[4096]{0:T(1024)} %bitcast.67, f32[8]{0:T(128)} %param.22, f32[8]{0:T(128)} %param.23), kind=kLoop, calls=%fused_computation.8 | loop fusion | flops 217088 | bytes 65632 | tf_op jit(solution)/shard_map/reduce_sum | solution.py:41
  2.5 0.9 %concatenate.14 = f32[8,32,128]{2,0,1:T(8,128)S(1)} concatenate(f32[3,32,128]{2,0,1:T(4,128)S(1)} %copy.31, f32[1,32,128]{2,0,1:T(1,128)S(1)} %bitcast.63, f32[1,32,128]{2,0,1:T(1,128)} %bitcast.64, f32[1,32,128]{2,0,1:T(1,128)} %bitcast.66, f32[2,32,128]{2,0,1:T(2,128)S(1)} %broadcast_in_dim.6), dimensions={0} | concatenate | bytes 262144 | tf_op jit(solution)/shard_map/concatenate | solution.py:218
  3.3 0.5 collective-permute-start
  3.9 2.9 %collective-permute-start.1 = (f32[32,8,128]{2,1,0:T(8,128)S(1)}, f32[32,8,128]{2,1,0:T(8,128)S(1)}, u32[]{:S(2)}, u32[]{:S(2)}) collective-permute-start(f32[32,8,128]{2,1,0:T(8,128)S(1)} %bitcast.55), channel_id=1, source_target_pairs={{0,28},{4,0},{8,4},{12,8},{16,12},{20,16},{24,20},{28,24},{1,29},{... | collective-permute-start | bytes 393224 | tf_op jit(solution)/shard_map/ppermute | solution.py:24
  6.8 2.3 %collective-permute-start.2 = (f32[32,8,128]{2,1,0:T(8,128)S(1)}, f32[32,8,128]{2,1,0:T(8,128)S(1)}, u32[]{:S(2)}, u32[]{:S(2)}) collective-permute-start(f32[32,8,128]{2,1,0:T(8,128)S(1)} %bitcast.56), channel_id=1, source_target_pairs={{0,1},{1,2},{2,3},{3,0},{4,5},{5,6},{6,7},{7,4},{8,9},{9,10},{10,1... | collective-permute-start | bytes 393224 | tf_op jit(solution)/shard_map/ppermute | solution.py:24
  9.1 2.0 %collective-permute-start.3 = (f32[32,8,128]{2,1,0:T(8,128)S(1)}, f32[32,8,128]{2,1,0:T(8,128)S(1)}, u32[]{:S(2)}, u32[]{:S(2)}) collective-permute-start(f32[32,8,128]{2,1,0:T(8,128)S(1)} %bitcast.57), channel_id=1, source_target_pairs={{0,3},{1,0},{2,1},{3,2},{4,7},{5,4},{6,5},{7,6},{8,11},{9,8},{10,9... | collective-permute-start | bytes 393224 | tf_op jit(solution)/shard_map/ppermute | solution.py:24
  11.8 0.6 copy.32.home_ref
  12.5 0.1 copy.35
  12.6 0.5 broadcast.82
  13.1 0.7 reduce.8
  13.8 0.1 copy.34
  14.0 1.2 %collective-permute-done.2.refs_3_ = f32[32,8,128]{2,1,0:T(8,128)S(1)} collective-permute-done((f32[32,8,128]{2,1,0:T(8,128)S(1)}, f32[32,8,128]{2,1,0:T(8,128)S(1)}, u32[]{:S(2)}, u32[]{:S(2)}) %collective-permute-start.2) | collective-permute-done | bytes 131104 | tf_op jit(solution)/shard_map/ppermute | solution.py:24
  15.2 0.8 %collective-permute-done.3.refs_4_ = f32[32,8,128]{2,1,0:T(8,128)S(1)} collective-permute-done((f32[32,8,128]{2,1,0:T(8,128)S(1)}, f32[32,8,128]{2,1,0:T(8,128)S(1)}, u32[]{:S(2)}, u32[]{:S(2)}) %collective-permute-start.3) | collective-permute-done | bytes 131104 | tf_op jit(solution)/shard_map/ppermute | solution.py:24
  16.0 13.2 %shard_map.139 = (f32[2,4096]{1,0:T(2,128)S(1)}, f32[32,8]{1,0:T(8,128)}) custom-call(s32[1,1,1496]{2,1,0:T(1,128)S(1)} %copy-done, s32[1,1,1496]{2,1,0:T(1,128)S(1)} %copy-done.1, s32[1,1]{1,0:T(1,128)S(6)} %copy.39.count_ref, f32[4096,8]{1,0:T(8,128)S(1)} %copy.32.home_ref, f32[1,4096]{1,0:T(1,128)S(1)} %bitcast.62, f32[1,4096]{1,0:T(1,128)S(1)} %bitcast.60, ...), custom_call_target="tpu_custom_call" | custom-call | tf_op jit(solution)/shard_map/pallas_call | solution.py:179
  29.1 29.4 %all-to-all-start = ((f32[32,1,8]{2,1,0:T(1,128)}), f32[32,1,8]{2,1,0:T(1,128)S(1)}, u32[]{:S(2)}, u32[]{:S(2)}) async-start(f32[32,1,8]{2,1,0:T(1,128)} %bitcast.11), calls=%async_computation | async-start | bytes 32768 | tf_op jit(solution)/shard_map/all_to_all | solution.py:266
  58.5 0.6 slice_bitcast_fusion
  59.3 0.1 copy.36
  59.3 0.3 convolution_bitcast_fusion
  59.6 3.7 %collective-permute-start.6 = (f32[3,64,64]{1,2,0:T(8,128)S(1)}, f32[3,64,64]{1,2,0:T(8,128)S(1)}, u32[]{:S(2)}, u32[]{:S(2)}) collective-permute-start(f32[3,64,64]{1,2,0:T(8,128)S(1)} %convolution_bitcast_fusion), channel_id=1, source_target_pairs={{0,3},{1,0},{2,1},{3,2},{4,7},{5,4},{6,5},{7,6},{8,11},{9,8},{10,9... | collective-permute-start | bytes 147464 | tf_op jit(solution)/shard_map/ppermute | solution.py:260
  63.3 0.2 convolution_bitcast_fusion.1
  63.6 0.2 convolution_bitcast_fusion.2
  63.8 1.1 %collective-permute-start.4 = (f32[3,64,64]{1,2,0:T(8,128)S(1)}, f32[3,64,64]{1,2,0:T(8,128)S(1)}, u32[]{:S(2)}, u32[]{:S(2)}) collective-permute-start(f32[3,64,64]{1,2,0:T(8,128)S(1)} %convolution_bitcast_fusion.2), channel_id=1, source_target_pairs={{0,1},{1,2},{2,3},{3,0},{4,5},{5,6},{6,7},{7,4},{8,9},{9,10},{10,1... | collective-permute-start | bytes 147464 | tf_op jit(solution)/shard_map/ppermute | solution.py:260
  65.0 0.8 %all-to-all-done = f32[32,1,8]{2,1,0:T(1,128)S(1)} async-done(((f32[32,1,8]{2,1,0:T(1,128)}), f32[32,1,8]{2,1,0:T(1,128)S(1)}, u32[]{:S(2)}, u32[]{:S(2)}) %all-to-all-start) | async-done | bytes 1056 | tf_op jit(solution)/shard_map/all_to_all | solution.py:266
  65.8 0.7 fusion.21
  68.4 0.6 bitcast_divide_fusion
  69.1 3.6 %collective-permute-done.5 = f32[3,64,64]{1,2,0:T(8,128)S(1)} collective-permute-done((f32[3,64,64]{1,2,0:T(8,128)S(1)}, f32[3,64,64]{1,2,0:T(8,128)S(1)}, u32[]{:S(2)}, u32[]{:S(2)}) %collective-permute-start.5) | collective-permute-done | bytes 49184 | tf_op jit(solution)/shard_map/ppermute | solution.py:260
  72.6 0.2 fusion.2
  73.0 0.1 mul.83
  73.1 0.1 copy.37
  73.2 0.1 mul.80
  73.3 0.6 subtract_add_fusion
  (24 shorter events, 0.5 us)
Async XLA Ops:
  0.6 12.5 %copy-start.2 = (f32[1,1,4096]{2,1,0:T(1,128)S(1)}, f32[1,1,4096]{2,1,0:T(1,128)}, u32[]{:S(2)}) copy-start(f32[1,1,4096]{2,1,0:T(1,128)} %param.13) | copy-start | bytes 49156
  0.6 13.3 %copy-start.4 = (s32[1,1,64]{2,1,0:T(1,128)S(1)}, s32[1,1,64]{2,1,0:T(1,128)}, u32[]{:S(2)}) copy-start(s32[1,1,64]{2,1,0:T(1,128)} %param.20) | copy-start | bytes 772
  0.7 15.3 %copy-start = (s32[1,1,1496]{2,1,0:T(1,128)S(1)}, s32[1,1,1496]{2,1,0:T(1,128)}, u32[]{:S(2)}) copy-start(s32[1,1,1496]{2,1,0:T(1,128)} %near_ref.1) | copy-start | bytes 17956
  0.7 15.3 %copy-start.1 = (s32[1,1,1496]{2,1,0:T(1,128)S(1)}, s32[1,1,1496]{2,1,0:T(1,128)}, u32[]{:S(2)}) copy-start(s32[1,1,1496]{2,1,0:T(1,128)} %far_ref.1) | copy-start | bytes 17956
  3.3 10.6 %collective-permute-start = (f32[32,8,128]{2,1,0:T(8,128)S(1)}, f32[32,8,128]{2,1,0:T(8,128)S(1)}, u32[]{:S(2)}, u32[]{:S(2)}) collective-permute-start(f32[32,8,128]{2,1,0:T(8,128)S(1)} %bitcast.54), channel_id=1, source_target_pairs={{0,4},{4,8},{8,12},{12,16},{16,20},{20,24},{24,28},{28,0},{1,5},{5... | collective-permute-start | bytes 393224 | tf_op jit(solution)/shard_map/ppermute | solution.py:24
  3.9 10.1 %collective-permute-start.1 = (f32[32,8,128]{2,1,0:T(8,128)S(1)}, f32[32,8,128]{2,1,0:T(8,128)S(1)}, u32[]{:S(2)}, u32[]{:S(2)}) collective-permute-start(f32[32,8,128]{2,1,0:T(8,128)S(1)} %bitcast.55), channel_id=1, source_target_pairs={{0,28},{4,0},{8,4},{12,8},{16,12},{20,16},{24,20},{28,24},{1,29},{... | collective-permute-start | bytes 393224 | tf_op jit(solution)/shard_map/ppermute | solution.py:24
  6.8 8.4 %collective-permute-start.2 = (f32[32,8,128]{2,1,0:T(8,128)S(1)}, f32[32,8,128]{2,1,0:T(8,128)S(1)}, u32[]{:S(2)}, u32[]{:S(2)}) collective-permute-start(f32[32,8,128]{2,1,0:T(8,128)S(1)} %bitcast.56), channel_id=1, source_target_pairs={{0,1},{1,2},{2,3},{3,0},{4,5},{5,6},{6,7},{7,4},{8,9},{9,10},{10,1... | collective-permute-start | bytes 393224 | tf_op jit(solution)/shard_map/ppermute | solution.py:24
  9.1 6.9 %collective-permute-start.3 = (f32[32,8,128]{2,1,0:T(8,128)S(1)}, f32[32,8,128]{2,1,0:T(8,128)S(1)}, u32[]{:S(2)}, u32[]{:S(2)}) collective-permute-start(f32[32,8,128]{2,1,0:T(8,128)S(1)} %bitcast.57), channel_id=1, source_target_pairs={{0,3},{1,0},{2,1},{3,2},{4,7},{5,4},{6,5},{7,6},{8,11},{9,8},{10,9... | collective-permute-start | bytes 393224 | tf_op jit(solution)/shard_map/ppermute | solution.py:24
  16.0 57.3 %copy-start.3 = (f32[1,1,4096]{2,1,0:T(1,128)S(1)}, f32[1,1,4096]{2,1,0:T(1,128)}, u32[]{:S(2)}) copy-start(f32[1,1,4096]{2,1,0:T(1,128)} %param.14) | copy-start | bytes 49156
  29.1 36.6 %all-to-all-start = ((f32[32,1,8]{2,1,0:T(1,128)}), f32[32,1,8]{2,1,0:T(1,128)S(1)}, u32[]{:S(2)}, u32[]{:S(2)}) async-start(f32[32,1,8]{2,1,0:T(1,128)} %bitcast.11), calls=%async_computation | async-start | bytes 32768 | tf_op jit(solution)/shard_map/all_to_all | solution.py:266
  59.6 9.5 %collective-permute-start.6 = (f32[3,64,64]{1,2,0:T(8,128)S(1)}, f32[3,64,64]{1,2,0:T(8,128)S(1)}, u32[]{:S(2)}, u32[]{:S(2)}) collective-permute-start(f32[3,64,64]{1,2,0:T(8,128)S(1)} %convolution_bitcast_fusion), channel_id=1, source_target_pairs={{0,3},{1,0},{2,1},{3,2},{4,7},{5,4},{6,5},{7,6},{8,11},{9,8},{10,9... | collective-permute-start | bytes 147464 | tf_op jit(solution)/shard_map/ppermute | solution.py:260
  63.5 9.1 %collective-permute-start.5 = (f32[3,64,64]{1,2,0:T(8,128)S(1)}, f32[3,64,64]{1,2,0:T(8,128)S(1)}, u32[]{:S(2)}, u32[]{:S(2)}) collective-permute-start(f32[3,64,64]{1,2,0:T(8,128)S(1)} %convolution_bitcast_fusion.1), channel_id=1, source_target_pairs={{0,2},{1,3},{2,0},{3,1},{4,6},{5,7},{6,4},{7,5},{8,10},{9,11},{10,... | collective-permute-start | bytes 147464 | tf_op jit(solution)/shard_map/ppermute | solution.py:260
  63.8 8.8 %collective-permute-start.4 = (f32[3,64,64]{1,2,0:T(8,128)S(1)}, f32[3,64,64]{1,2,0:T(8,128)S(1)}, u32[]{:S(2)}, u32[]{:S(2)}) collective-permute-start(f32[3,64,64]{1,2,0:T(8,128)S(1)} %convolution_bitcast_fusion.2), channel_id=1, source_target_pairs={{0,1},{1,2},{2,3},{3,0},{4,5},{5,6},{6,7},{7,4},{8,9},{9,10},{10,1... | collective-permute-start | bytes 147464 | tf_op jit(solution)/shard_map/ppermute | solution.py:260
